TPU v7x, 32 devices: a whole 2x2x4 slice. The times are simulated.
32 devices in a mesh: groups: 2 (over y), context: 4 (over x, core), tensor: 4 (over z).
Axes of the slice: x: 2, y: 2, z: 4, core: 2. Of those that a mesh axis runs over, the one named last changes fastest.
Arguments:
- tokens: bfloat16 [8192, 1920], P(('groups', 'context'), 'tensor'), parts along dimension 0, may hold values from -6 to 6
- in_weight: bfloat16 [1920, 3, 1920], P(None, None, 'tensor'), may hold values from -0.125 to 0.125
- short_filter: bfloat16 [7, 3, 1920], P(None, None, 'tensor'), may hold values from -2 to 2
- mode_weight: float32 [1920, 16], P('tensor'), may hold values from -1.5 to 1.5
- decay_rate: float32 [1920, 16], P('tensor'), as said below
- out_weight: bfloat16 [1920, 1920], P('tensor'), may hold values from -0.1875 to 0.1875
Outputs:
- mixed: bfloat16 [8192, 1920], P(('groups', 'context'), 'tensor'), parts along dimension 0
There are 2 independent parts, one for each index of `groups`. A program takes and returns all parts, laid end to end along the dimension named above; an argument that names none is the same for every part. Nothing has to cross between parts.
Inputs may be any that keep to these rules, and one draw needn't show every extreme that they name: `decay_rate`: every rate lies between 0.2 / 4096 and 1 / 30.
All inputs are finite; a program needn't handle non-finite values.
Results may differ from a plain program's by a relative error of at most 0.025.
Values may be sent and summed in bfloat16 or wider, within the bound.
No kernel may reach another device: no remote copies, remote signals or barrier semaphores. Data moves between devices by JAX's collectives and lax.ppermute only.
A program may use at most 64 MiB of HBM per device.

v0:
```python
import jax
import jax.numpy as jnp
from jax import lax
from jax.sharding import PartitionSpec as P

TAPS = 7


HIGH = lax.Precision.HIGHEST


def shifted(array, axis, by):
    size = lax.axis_size(axis)
    pairs = [(i, i + by) for i in range(size) if 0 <= i + by < size]
    return lax.ppermute(array, axis, pairs)


def block_end(drive, decay):
    tok_rows, channels = drive.shape
    piece_len = min(128, tok_rows)
    count = tok_rows // piece_len
    blocks = drive.reshape(count, piece_len, channels)
    offsets = jnp.arange(piece_len).astype(jnp.float32)
    end_weights = jnp.exp(-decay[None] * (piece_len - offsets)[:, None, None])
    ends = jnp.einsum("bqc,qcn->bcn", blocks, end_weights, precision=HIGH)
    later = (count - 1 - jnp.arange(count)).astype(jnp.float32) * piece_len
    return jnp.sum(jnp.exp(-decay[None] * later[:, None, None]) * ends, 0)


def local_conv(drive, decay, amplitude, state_in):
    tok_rows, channels = drive.shape
    piece_len = min(128, tok_rows)
    count = tok_rows // piece_len
    blocks = drive.reshape(count, piece_len, channels)
    offsets = jnp.arange(piece_len).astype(jnp.float32)
    lag_table = offsets[:, None] - offsets[None, :]
    causal = lag_table >= 0.0
    toeplitz = jnp.zeros((piece_len, piece_len, channels), jnp.float32)
    for mode_number in range(decay.shape[1]):
        toeplitz = toeplitz + amplitude[:, mode_number][None, None, :] * jnp.exp(
            -decay[:, mode_number][None, None, :] * jnp.maximum(lag_table, 0.0)[:, :, None]
        )
    toeplitz = jnp.where(causal[:, :, None], toeplitz, 0.0)
    inside = jnp.einsum("tsc,bsc->btc", toeplitz, blocks, precision=HIGH)
    end_weights = jnp.exp(-decay[None] * (piece_len - offsets)[:, None, None])
    ends = jnp.einsum("bqc,qcn->bcn", blocks, end_weights, precision=HIGH)
    block_ids = jnp.arange(count).astype(jnp.float32)
    distance = block_ids[:, None] - block_ids[None, :] - 1.0
    before = distance >= 0.0
    spread = jnp.where(
        before[:, :, None, None],
        jnp.exp(-decay[None, None] * piece_len * jnp.maximum(distance, 0.0)[:, :, None, None]),
        0.0,
    )
    starts = jnp.einsum("bkcn,kcn->bcn", spread, ends, precision=HIGH)
    starts = starts + jnp.exp(-decay[None] * piece_len * block_ids[:, None, None]) * state_in[None]
    start_weights = amplitude[None] * jnp.exp(-decay[None] * offsets[:, None, None])
    carried = jnp.einsum("qcn,bcn->bqc", start_weights, starts, precision=HIGH)
    return (inside + carried).reshape(tok_rows, channels)


def per_device(tokens, in_weight, short_filter, mode_weight, decay_rate, out_weight):
    tok_rows = tokens.shape[0]
    channels = in_weight.shape[2]
    proj = jnp.einsum(
        "td,dkc->tkc",
        lax.all_gather(tokens, "tensor", axis=1, tiled=True),
        in_weight,
        preferred_element_type=jnp.float32,
    ).astype(jnp.bfloat16)
    rim = shifted(proj[tok_rows - (TAPS - 1) :], "context", 1)
    padded = jnp.concatenate([rim, proj], 0)
    filtered = jnp.zeros((tok_rows, 3, channels), jnp.float32)
    for tap_number in range(TAPS):
        begin = TAPS - 1 - tap_number
        filtered = filtered + short_filter[tap_number].astype(jnp.float32)[None] * padded[
            begin : begin + tok_rows
        ].astype(jnp.float32)
    query = filtered[:, 0]
    drive = filtered[:, 1] * filtered[:, 2]
    amplitude = mode_weight * jnp.sqrt(2.0 * decay_rate)
    zero_state = jnp.zeros(decay_rate.shape, jnp.float32)
    my_start = lax.axis_index("context") * tok_rows
    piece = lax.all_gather(drive.astype(jnp.bfloat16), "context", axis=0, tiled=True).astype(
        jnp.float32
    )
    shard_count = piece.shape[0] // tok_rows

    def one_shard(shard_number, running):
        shard = lax.dynamic_slice_in_dim(piece, shard_number * tok_rows, tok_rows, 0)
        shard_end = (shard_number + 1) * tok_rows
        spacing = (my_start - shard_end).astype(jnp.float32)
        factor = jnp.where(spacing >= 0.0, jnp.exp(-decay_rate * jnp.maximum(spacing, 0.0)), 0.0)
        return running + factor * block_end(shard, decay_rate)

    state_in = lax.fori_loop(0, shard_count, one_shard, zero_state)
    conv = local_conv(drive, decay_rate, amplitude, state_in)
    gated = (query * conv).astype(jnp.bfloat16)
    partial_sums = jnp.dot(gated, out_weight, preferred_element_type=jnp.float32)
    summed = lax.psum_scatter(
        partial_sums.astype(jnp.bfloat16), "tensor", scatter_dimension=1, tiled=True
    )
    return summed


def solution(mesh):
    placed = (
        P(("groups", "context"), "tensor"),
        P(None, None, "tensor"),
        P(None, None, "tensor"),
        P("tensor", None),
        P("tensor", None),
        P("tensor", None),
    )
    return jax.shard_map(
        per_device,
        mesh=mesh,
        in_specs=placed,
        out_specs=P(("groups", "context"), "tensor"),
        check_vma=False,
    )
```

profile of v0, /device:TPU:0, one launch (start us, length us, event | category | flops | bytes accessed | tf_op | source)
XLA Modules:
  0.0 414.9 jit_solution(163364691119471869)
XLA Ops:
  6.5 0.7 all-gather.4.cloned.1.call-update
  7.3 1.0 slice_convert_fusion.6
  8.4 79.7 %all-gather.4.cloned.1.call-done = bf16[1024,1920]{0,1:T(8,128)(2,1)} async-done(((bf16[1024,480]{0,1:T(8,128)(2,1)}), bf16[1024,1920]{0,1:T(8,128)(2,1)}) %all-gather.4.cloned.1.call-update) | async-done | bytes 3932176 | tf_op jit(solution)/shard_map/all_gather | solution.py:67
  88.1 9.4 %fusion.122 = bf16[1024,3,480]{0,2,1:T(8,128)(2,1)S(1)} fusion(bf16[1920,3,480]{0,2,1:T(8,128)(2,1)} %param.9, bf16[1024,1920]{0,1:T(8,128)(2,1)} %all-gather.4.cloned.1.call-done), kind=kOutput, calls=%fused_computation.137 | convolution fusion | flops 5663784960 | bytes 12410880 | tf_op jit(solution)/shard_map/td,dkc->tkc/dot_general | solution.py:65
  97.7 1.6 collective-permute-start
  99.3 1.2 collective-permute-done
  100.6 9.6 %multiply_add_fusion = f32[1024,3,480]{0,2,1:T(8,128)S(1)} fusion(bf16[1024,3,480]{0,2,1:T(8,128)(2,1)S(1)} %fusion.122, bf16[6,3,480]{0,2,1:T(8,128)(2,1)S(1)} %collective-permute-done, f32[3,480]{1,0:T(4,128)S(1)} %get-tuple-element.216, f32[3,480]{1,0:T(4,128)S(1)} %get-tuple-element.217, f32[3,480]{1,0:T(4,128)S(1)} %get-tuple-element.218, ...), kind=kLoop, calls=%fused_computation.116 | loop fusion | flops 56033280 | bytes 8904960 | tf_op jit(solution)/shard_map/add | solution.py:76
  110.1 2.6 copy-done.1
  112.7 2.1 fusion.141
  115.2 0.8 negate_bitcast_fusion
  116.1 0.8 copy.23
  117.2 0.6 slice_negate_fusion.15
  117.9 2.0 copy.42
  119.9 1.3 copy-done.2
  121.2 7.9 %fusion.114 = f32[480,16,8]{1,2,0:T(8,128)} fusion(f32[8,128,480]{1,0,2:T(8,128)S(1)} %bitcast.112, f32[128]{0:T(128)S(1)} %broadcast_subtract_fusion, f32[480,16]{1,0:T(8,128)S(1)} %get-tuple-element.262), kind=kOutput, calls=%fused_computation.124 | convolution fusion | flops 95354880 | bytes 2243072 | tf_op jit(solution)/shard_map/bqc,qcn->bcn/dot_general | solution.py:46
  129.1 2.1 copy.39
  131.8 1.9 copy.31
  133.7 18.7 %all-gather.6.cloned.1.call-done = bf16[4096,1,480]{0,2,1:T(8,128)(2,1)} async-done(((bf16[1024,1,480]{0,2,1:T(8,128)(2,1)}), bf16[4096,1,480]{0,2,1:T(8,128)(2,1)}) %all-gather.6.cloned.1.call-update) | async-done | bytes 3932176 | tf_op jit(solution)/shard_map/all_gather | solution.py:84
  152.4 6.2 %bitcast_convert_fusion = f32[4096,480]{0,1:T(8,128)} fusion(bf16[4096,1,480]{0,2,1:T(8,128)(2,1)} %all-gather.6.cloned.1.call-done), kind=kLoop, calls=%fused_computation.117 | loop fusion | flops 1966080 | bytes 11796480 | tf_op jit(solution)/shard_map/convert_element_type | solution.py:84
  158.6 36.5 %while.16 = (s32[]{:T(128)}, f32[480,16]{1,0:T(8,128)S(1)}, s32[]{:T(128)}, f32[480,16]{1,0:T(8,128)S(1)}, f32[1,480,16]{2,1,0:T(8,128)S(1)}, /*index=5*/f32[409...) while((s32[]{:T(128)}, f32[480,16]{1,0:T(8,128)S(1)}, ...), condition=%wide.region_2.3_spmd.clone, body=%wide.region_0.2_spmd.clone.sunk | while | flops 95570208 | bytes 10016043 | solution.py:96
  159.0 1.8 dynamic-slice_bitcast_fusion.2
  161.2 6.6 %fusion.160 = f32[480,16]{1,0:T(8,128)S(1)} fusion(f32[8,128,480]{1,0,2:T(8,128)S(1)} %bitcast.111, f32[128]{0:T(128)S(1)} %convert_subtract_fusion.2, f32[480,16]{1,0:T(8,128)S(1)} %bitcast.114, f32[8]{0:T(128)S(1)} %convert_multiply_fusion.2), kind=kOutput, calls=%fused_computation.4.clone.1 | convolution fusion | flops 95531520 | bytes 2028064 | tf_op jit(solution)/shard_map/while/body/eval_jaxpr/bqc,qcn->bcn/dot_general | solution.py:25
  168.0 1.8 dynamic-slice_bitcast_fusion.2
  170.2 6.6 %fusion.160 = f32[480,16]{1,0:T(8,128)S(1)} fusion(f32[8,128,480]{1,0,2:T(8,128)S(1)} %bitcast.111, f32[128]{0:T(128)S(1)} %convert_subtract_fusion.2, f32[480,16]{1,0:T(8,128)S(1)} %bitcast.114, f32[8]{0:T(128)S(1)} %convert_multiply_fusion.2), kind=kOutput, calls=%fused_computation.4.clone.1 | convolution fusion | flops 95531520 | bytes 2028064 | tf_op jit(solution)/shard_map/while/body/eval_jaxpr/bqc,qcn->bcn/dot_general | solution.py:25
  177.0 1.8 dynamic-slice_bitcast_fusion.2
  179.3 6.6 %fusion.160 = f32[480,16]{1,0:T(8,128)S(1)} fusion(f32[8,128,480]{1,0,2:T(8,128)S(1)} %bitcast.111, f32[128]{0:T(128)S(1)} %convert_subtract_fusion.2, f32[480,16]{1,0:T(8,128)S(1)} %bitcast.114, f32[8]{0:T(128)S(1)} %convert_multiply_fusion.2), kind=kOutput, calls=%fused_computation.4.clone.1 | convolution fusion | flops 95531520 | bytes 2028064 | tf_op jit(solution)/shard_map/while/body/eval_jaxpr/bqc,qcn->bcn/dot_general | solution.py:25
  186.1 1.8 dynamic-slice_bitcast_fusion.2
  188.3 6.6 %fusion.160 = f32[480,16]{1,0:T(8,128)S(1)} fusion(f32[8,128,480]{1,0,2:T(8,128)S(1)} %bitcast.111, f32[128]{0:T(128)S(1)} %convert_subtract_fusion.2, f32[480,16]{1,0:T(8,128)S(1)} %bitcast.114, f32[8]{0:T(128)S(1)} %convert_multiply_fusion.2), kind=kOutput, calls=%fused_computation.4.clone.1 | convolution fusion | flops 95531520 | bytes 2028064 | tf_op jit(solution)/shard_map/while/body/eval_jaxpr/bqc,qcn->bcn/dot_general | solution.py:25
  195.1 6.9 %fusion.110 = f32[480,8,128]{2,1,0:T(8,128)S(1)} fusion(f32[480,16,8]{1,2,0:T(8,128)} %copy.31, f32[128]{0:T(128)S(1)} %iota_convert_fusion.1, f32[480,16]{1,0:T(8,128)S(1)} %copy-done.5, f32[480,16]{1,0:T(8,128)S(1)} %get-tuple-element.295, f32[480,16]{1,0:T(8,128)S(1)} %get-tuple-element.138, f32[8]{0:T(128)S(1)} %iota_convert_fusion, ...), kind=kOutput, calls=%fused_computation.120 | convolution fusion | flops 96522240 | bytes 2335264 | tf_op jit(solution)/shard_map/qcn,bcn->bqc/dot_general | solution.py:58
  202.1 127.5 %fusion.134 = f32[480,8,128]{2,1,0:T(8,128)S(1)} fusion(f32[480,8,128]{2,1,0:T(8,128)S(1)} %fusion.110, f32[8,128,480]{1,0,2:T(8,128)S(1)} %bitcast.113, f32[480]{0:T(512)S(1)} %bitcast.147, f32[480]{0:T(512)S(1)} %bitcast.117, f32[480]{0:T(512)S(1)} %bitcast.133, f32[480]{0:T(512)S(1)} %bitcast.118, f32[480]{0:T(512)S(1)} %bitcast.134, ...), kind=kOutput, calls=%fused_computation.152 | convolution fusion | flops 1132953600 | bytes 6041600 | tf_op jit(solution)/shard_map/tsc,bsc->btc/dot_general | solution.py:44
  329.7 5.7 %convolution_convert_fusion = bf16[1024,1920]{0,1:T(8,128)(2,1)} fusion(bf16[480,1920]{1,0:T(8,128)(2,1)S(1)} %copy-done, f32[60,8,8,128]{3,2,1,0:T(8,128)S(1)} %bitcast.148, f32[1024,3,480]{0,2,1:T(8,128)} %copy-done.1), kind=kOutput, calls=%fused_computation.127 | convolution fusion | flops 1890385920 | bytes 9707520 | tf_op jit(solution)/shard_map/dot_general | solution.py:99
  335.4 72.8 %reduce-scatter.2.cloned.1.call-done = bf16[1024,480]{0,1:T(8,128)(2,1)} async-done(((bf16[1024,1920]{0,1:T(8,128)(2,1)}), bf16[1024,480]{0,1:T(8,128)(2,1)}) %reduce-scatter.2.cloned.1.call-update) | async-done | bytes 983056 | tf_op jit(solution)/shard_map/reduce_scatter | solution.py:100
  (61 shorter events, 3.9 us)
Async XLA Ops:
  6.5 323.1 %copy-start = (bf16[480,1920]{1,0:T(8,128)(2,1)S(1)}, bf16[480,1920]{1,0:T(8,128)(2,1)}, u32[]{:S(2)}) copy-start(bf16[480,1920]{1,0:T(8,128)(2,1)} %param.13) | copy-start | bytes 5529604
  6.5 81.5 %all-gather.4.cloned.1.call-start = ((), (), s32[]{:S(2)}) async-start(), calls=%async_computation.1 | async-start | bytes 4915200 | tf_op jit(solution)/shard_map/all_gather | solution.py:67
  7.3 145.1 %all-gather.6.cloned.1.call-start = ((), (), s32[]{:S(2)}) async-start(), calls=%async_computation.3 | async-start | bytes 4915200 | tf_op jit(solution)/shard_map/all_gather | solution.py:84
  97.7 2.9 collective-permute-start
  110.1 2.6 copy-start.1
  112.7 2.3 copy-start.4
  112.7 3.3 copy-start.7
  114.8 293.4 %reduce-scatter.2.cloned.1.call-start = ((), (), s32[]{:S(2)}) async-start(), calls=%async_computation.2 | async-start | bytes 4915200 | tf_op jit(solution)/shard_map/reduce_scatter | solution.py:100
  119.9 1.3 copy-start.2
  133.7 24.9 %copy-start.6 = (f32[1,480,16]{2,1,0:T(8,128)S(1)}, f32[1,480,16]{2,1,0:T(8,128)}, u32[]{:S(2)}) copy-start(f32[1,480,16]{2,1,0:T(8,128)} %get-tuple-element.263) | copy-start | bytes 92164
  158.6 36.6 %copy-start.5 = (f32[480,16]{1,0:T(8,128)S(1)}, f32[480,16]{1,0:T(8,128)}, u32[]{:S(2)}) copy-start(f32[480,16]{1,0:T(8,128)} %copy.23) | copy-start | bytes 92164
  195.1 7.0 %copy-start.3 = (f32[60,8,8,128]{3,2,1,0:T(8,128)S(1)}, f32[60,8,8,128]{3,2,1,0:T(8,128)}, u32[]{:S(2)}) copy-start(f32[60,8,8,128]{3,2,1,0:T(8,128)} %copy-done.2) | copy-start | bytes 5898244
  195.1 7.0 %copy-start.8 = (f32[480,1]{0,1:T(1,128)S(1)}, f32[480,1]{0,1:T(1,128)}, u32[]{:S(2)}) copy-start(f32[480,1]{0,1:T(1,128)} %get-tuple-element.205) | copy-start | bytes 5764
  195.1 7.0 %copy-start.9 = (f32[480,1]{0,1:T(1,128)S(1)}, f32[480,1]{0,1:T(1,128)}, u32[]{:S(2)}) copy-start(f32[480,1]{0,1:T(1,128)} %get-tuple-element.206) | copy-start | bytes 5764
  195.1 7.0 %copy-start.10 = (f32[480,1]{0,1:T(1,128)S(1)}, f32[480,1]{0,1:T(1,128)}, u32[]{:S(2)}) copy-start(f32[480,1]{0,1:T(1,128)} %get-tuple-element.207) | copy-start | bytes 5764
  195.1 7.0 %copy-start.11 = (f32[480,1]{0,1:T(1,128)S(1)}, f32[480,1]{0,1:T(1,128)}, u32[]{:S(2)}) copy-start(f32[480,1]{0,1:T(1,128)} %get-tuple-element.208) | copy-start | bytes 5764
Sparse Core Ops, SparseCore 0:
  8.9 79.1 all-gather.3
  114.9 37.4 all-gather.5
  335.5 72.6 reduce-scatter.1
where the time goes:
time: 419 us; the launch traced here: 415 us
  matrix products  184 us (44%)
  waiting for transfers between devices  173 us (41%)
  other arithmetic  21.6 us (5%)
  local copies, waits for them, and re-layouts  20 us (5%)
  between operations  13.6 us (3%)
    dot_general x1, matrix products, local_conv(): inside = jnp.einsum('tsc,bsc->btc', toeplitz, blocks, precision=HIGH)  128 us
    all_gather x1, waiting for transfers between devices, per_device(): lax.all_gather(tokens, 'tensor', axis=1, tiled=True)  79.7 us
    reduce_scatter x1, waiting for transfers between devices, per_device(): lax.psum_scatter(partial_sums.astype(jnp.bfloat16), 'tensor', scatter_dim...  72.8 us
    dot_general x4, matrix products, block_end(): ends = jnp.einsum('bqc,qcn->bcn', blocks, end_weights, precision=HIGH)  26.5 us
    all_gather x1, waiting for transfers between devices, per_device(): lax.all_gather(drive.astype(jnp.bfloat16), 'context', axis=0, tiled=True)  18.7 us
    add x1, other arithmetic, per_device(): filtered + short_filter[tap_number].astype(jnp.float32)[None] * padded[be...  9.55 us
    dot_general x1, matrix products, per_device(): jnp.einsum('td,dkc->tkc', lax.all_gather(tokens, 'tensor', axis=1, tiled=...  9.42 us
    while x8, local copies, waits for them, and re-layouts  8.8 us
  transfers between devices with their start and end apart: 4, of which 4 were waited for; matrix products, arithmetic and copies ran while one was open for 4% of the time, Pallas kernels for 0%

commit v1 on v0

v1 whole, which is shorter than its diff:
```python
import jax
import jax.numpy as jnp
from jax import lax
from jax.experimental import pallas as pl
from jax.experimental.pallas import tpu as pltpu
from jax.sharding import PartitionSpec as P

TAPS = 7
CHUNK = 8


def shifted(array, axis, by):
    size = lax.axis_size(axis)
    pairs = [(i, i + by) for i in range(size) if 0 <= i + by < size]
    return lax.ppermute(array, axis, pairs)


def local_kernel(d_ref, hcol_ref, w_ref, g_ref, a8_ref, conv_ref, end_ref, s_ref):
    rows = d_ref.shape[0]
    modes = a8_ref.shape[0]
    s_ref[...] = jnp.zeros(s_ref.shape, jnp.float32)

    def body(b, carry):
        start = pl.multiple_of(b * CHUNK, CHUNK)
        state = s_ref[...]
        chunk = d_ref[pl.ds(start, CHUNK), :]
        acc = jnp.zeros(chunk.shape, jnp.float32)
        for n in range(modes):
            acc = acc + g_ref[n] * state[n : n + 1, :]
        new_state = a8_ref[...] * state
        for j in range(CHUNK):
            row = chunk[j : j + 1, :]
            acc = acc + hcol_ref[j] * row
            new_state = new_state + w_ref[j] * row
        conv_ref[pl.ds(start, CHUNK), :] = acc
        s_ref[...] = new_state
        return carry

    lax.fori_loop(0, rows // CHUNK, body, 0)
    end_ref[...] = s_ref[...]


def gate_kernel(conv_ref, q_ref, g_ref, a8_ref, sin_ref, out_ref, s_ref):
    rows = conv_ref.shape[0]
    modes = a8_ref.shape[0]
    s_ref[...] = sin_ref[...]

    def body(b, carry):
        start = pl.multiple_of(b * CHUNK, CHUNK)
        state = s_ref[...]
        acc = conv_ref[pl.ds(start, CHUNK), :]
        for n in range(modes):
            acc = acc + g_ref[n] * state[n : n + 1, :]
        out_ref[pl.ds(start, CHUNK), :] = q_ref[pl.ds(start, CHUNK), :] * acc
        s_ref[...] = a8_ref[...] * state
        return carry

    lax.fori_loop(0, rows // CHUNK, body, 0)


def vmem_spec():
    return pl.BlockSpec(memory_space=pltpu.VMEM)


def per_device(tokens, in_weight, short_filter, mode_weight, decay_rate, out_weight):
    tok_rows = tokens.shape[0]
    channels = in_weight.shape[2]
    modes = decay_rate.shape[1]
    proj = jnp.einsum(
        "td,dkc->tkc",
        lax.all_gather(tokens, "tensor", axis=1, tiled=True),
        in_weight,
        preferred_element_type=jnp.float32,
    ).astype(jnp.bfloat16)
    rim = shifted(proj[tok_rows - (TAPS - 1) :], "context", 1)
    padded = jnp.concatenate([rim, proj], 0)
    filtered = jnp.zeros((tok_rows, 3, channels), jnp.float32)
    for tap_number in range(TAPS):
        begin = TAPS - 1 - tap_number
        filtered = filtered + short_filter[tap_number].astype(jnp.float32)[None] * padded[
            begin : begin + tok_rows
        ].astype(jnp.float32)
    query = filtered[:, 0]
    drive = filtered[:, 1] * filtered[:, 2]

    lam = decay_rate.T
    amp = (mode_weight * jnp.sqrt(2.0 * decay_rate)).T
    steps = jnp.arange(CHUNK).astype(jnp.float32)
    g_tab = amp[:, None, :] * jnp.exp(-lam[:, None, :] * steps[None, :, None])
    w_tab = jnp.exp(-lam[None, :, :] * (CHUNK - steps)[:, None, None])
    h_short = jnp.sum(g_tab, axis=0)
    lag = steps[None, :] - steps[:, None]
    lag_index = jnp.clip(lag, 0, CHUNK - 1).astype(jnp.int32)
    hcol = jnp.where((lag >= 0)[:, :, None], h_short[lag_index], 0.0)
    a8 = jnp.exp(-lam * CHUNK)

    conv_local, end_state = pl.pallas_call(
        local_kernel,
        out_shape=(
            jax.ShapeDtypeStruct((tok_rows, channels), jnp.float32),
            jax.ShapeDtypeStruct((modes, channels), jnp.float32),
        ),
        in_specs=[vmem_spec() for _ in range(5)],
        out_specs=(vmem_spec(), vmem_spec()),
        scratch_shapes=[pltpu.VMEM((modes, channels), jnp.float32)],
    )(drive, hcol, w_tab, g_tab, a8)

    ends = lax.all_gather(end_state, "context", axis=0, tiled=False)
    block_count = ends.shape[0]
    me = lax.axis_index("context")
    gap = (me - 1 - jnp.arange(block_count)).astype(jnp.float32)
    factor = jnp.where(
        (gap >= 0.0)[:, None, None],
        jnp.exp(-lam[None] * (tok_rows * jnp.maximum(gap, 0.0))[:, None, None]),
        0.0,
    )
    state_in = jnp.sum(factor * ends, axis=0)

    gated = pl.pallas_call(
        gate_kernel,
        out_shape=jax.ShapeDtypeStruct((tok_rows, channels), jnp.float32),
        in_specs=[vmem_spec() for _ in range(5)],
        out_specs=vmem_spec(),
        scratch_shapes=[pltpu.VMEM((modes, channels), jnp.float32)],
    )(conv_local, query, g_tab, a8, state_in)
    gated = gated.astype(jnp.bfloat16)
    partial_sums = jnp.dot(gated, out_weight, preferred_element_type=jnp.float32)
    summed = lax.psum_scatter(
        partial_sums.astype(jnp.bfloat16), "tensor", scatter_dimension=1, tiled=True
    )
    return summed


def solution(mesh):
    placed = (
        P(("groups", "context"), "tensor"),
        P(None, None, "tensor"),
        P(None, None, "tensor"),
        P("tensor", None),
        P("tensor", None),
        P("tensor", None),
    )
    return jax.shard_map(
        per_device,
        mesh=mesh,
        in_specs=placed,
        out_specs=P(("groups", "context"), "tensor"),
        check_vma=False,
    )
```

time: 419 us -> 223 us (0.53)
  matrix products: 184 us -> 15.8 us
  waiting for transfers between devices: 173 us -> 147 us
  Pallas kernels: 0 us -> 20.4 us
  local copies, waits for them, and re-layouts: 20 us -> 0.77 us
  blocking collectives: 0 us -> 7.93 us
  other arithmetic: 21.6 us -> 14.9 us
    dot_general x7 -> x0, matrix products: 169 us -> none  [the longest x1 128 us: local_conv(): inside = jnp.einsum('tsc,bsc->btc', toeplitz, blocks, precision=HIGH)]
    pallas_call x0 -> x2, Pallas kernels: none -> 20.4 us  [the longest x1 12.5 us: per_device(): pl.pallas_call(local_kernel, out_shape=(jax.ShapeDtypeStruct((tok_rows, c...]
    all_gather x1 -> x0, waiting for transfers between devices: 18.7 us -> none  [per_device(): lax.all_gather(drive.astype(jnp.bfloat16), 'context', axis=0, tiled=True)]
    while x8 -> x0, local copies, waits for them, and re-layouts: 8.8 us -> none
    convert_element_type x4 -> x1, other arithmetic: 8.24 us -> 0.01 us  [per_device(): steps = jnp.arange(CHUNK).astype(jnp.float32)]
    unnamed x31 -> x6, local copies, waits for them, and re-layouts: 8.14 us -> 0.03 us
    all_gather x0 -> x1, blocking collectives: none -> 7.93 us  [per_device(): ends = lax.all_gather(end_state, 'context', axis=0, tiled=False)]
    all_gather x1, waiting for transfers between devices: 79.7 us -> 74.2 us  [per_device(): lax.all_gather(tokens, 'tensor', axis=1, tiled=True)]
  transfers between devices with their start and end apart: 4 -> 3, of which waited for: 4 -> 3; matrix products, arithmetic and copies ran while one was open for 4% -> 3% of each run, Pallas kernels for 0% -> 0%
where the time goes in v1:
time: 223 us; the launch traced here: 222 us
  waiting for transfers between devices  147 us (66%)
  Pallas kernels  20.4 us (9%)
  matrix products  15.8 us (7%)
  other arithmetic  14.9 us (7%)
  between operations  13.5 us (6%)
  blocking collectives  7.93 us (4%)
    all_gather x1, waiting for transfers between devices, per_device(): lax.all_gather(tokens, 'tensor', axis=1, tiled=True)  74.2 us
    reduce_scatter x1, waiting for transfers between devices, per_device(): lax.psum_scatter(partial_sums.astype(jnp.bfloat16), 'tensor', scatter_dim...  71.7 us
    pallas_call x1, Pallas kernels, per_device(): pl.pallas_call(local_kernel, out_shape=(jax.ShapeDtypeStruct((tok_rows, c...  12.5 us
    dot_general x1, matrix products, per_device(): jnp.einsum('td,dkc->tkc', lax.all_gather(tokens, 'tensor', axis=1, tiled=...  10.1 us
    all_gather x1, blocking collectives, per_device(): ends = lax.all_gather(end_state, 'context', axis=0, tiled=False)  7.93 us
    pallas_call x1, Pallas kernels, per_device(): pl.pallas_call(gate_kernel, out_shape=jax.ShapeDtypeStruct((tok_rows, cha...  7.88 us
    add x1, other arithmetic, per_device(): filtered + short_filter[tap_number].astype(jnp.float32)[None] * padded[be...  5.82 us
    dot_general x1, matrix products, per_device(): jnp.dot(gated, out_weight, preferred_element_type=jnp.float32)  5.72 us
  transfers between devices with their start and end apart: 3, of which 3 were waited for; matrix products, arithmetic and copies ran while one was open for 3% of the time, Pallas kernels for 0%

profile of v1, /device:TPU:0, one launch (start us, length us, event | category | flops | bytes accessed | tf_op | source)
XLA Modules:
  0.0 222.4 jit_solution(16414208395472254232)
XLA Ops:
  6.5 0.0 copy-start
  6.5 0.0 all-gather.3.cloned.1.call-start
  6.5 0.7 all-gather.3.cloned.1.call-update
  7.3 0.0 reduce-scatter.2.cloned.1.call-start
  7.3 0.1 compare_select_fusion
  7.4 0.1 reshape.127
  7.5 0.8 multiply_bitcast_fusion
  8.3 0.8 exponential_multiply_fusion
  9.1 0.7 gather_fusion
  9.8 0.1 subtract_compare_fusion
  9.9 1.0 slice_convert_fusion.6
  10.9 1.4 multiply_exponential_fusion.1.a8_ref
  12.3 0.7 bitcast_select_fusion.hcol_ref
  13.0 0.8 multiply_exponential_fusion.w_ref
  13.8 74.2 %all-gather.3.cloned.1.call-done = bf16[1024,1920]{0,1:T(8,128)(2,1)} async-done(((bf16[1024,480]{0,1:T(8,128)(2,1)}), bf16[1024,1920]{0,1:T(8,128)(2,1)}) %all-gather.3.cloned.1.call-update) | async-done | bytes 3932176 | tf_op jit(solution)/shard_map/all_gather | solution.py:71
  88.1 10.1 %fusion.7 = bf16[1024,3,480]{2,0,1:T(8,128)(2,1)S(1)} fusion(bf16[1920,3,480]{0,2,1:T(8,128)(2,1)} %param.7, bf16[1024,1920]{0,1:T(8,128)(2,1)} %all-gather.3.cloned.1.call-done), kind=kOutput, calls=%fused_computation.19 | convolution fusion | flops 5663784960 | bytes 12410880 | tf_op jit(solution)/shard_map/td,dkc->tkc/dot_general | solution.py:69
  98.2 1.6 collective-permute-start
  99.8 0.8 collective-permute-done
  100.6 5.8 %multiply_add_fusion = f32[1024,3,480]{2,0,1:T(8,128)S(1)} fusion(bf16[1024,3,480]{2,0,1:T(8,128)(2,1)S(1)} %fusion.7, bf16[6,3,480]{2,0,1:T(8,128)(2,1)S(1)} %collective-permute-done, f32[3,480]{1,0:T(4,128)S(1)} %get-tuple-element.22, f32[3,480]{1,0:T(4,128)S(1)} %get-tuple-element.23, f32[3,480]{1,0:T(4,128)S(1)} %get-tuple-element.24, ...), kind=kLoop, calls=%fused_computation.6 | loop fusion | flops 56033280 | bytes 8904960 | tf_op jit(solution)/shard_map/add | solution.py:80
  106.4 2.7 %slice_bitcast_fusion = (f32[1024,480]{1,0:T(8,128)}, f32[1024,480]{1,0:T(8,128)}) fusion(f32[1024,3,480]{2,0,1:T(8,128)S(1)} %multiply_add_fusion), kind=kLoop, calls=%fused_computation.20 | loop fusion | flops 491520 | bytes 9830400 | tf_op jit(solution)/shard_map/squeeze | solution.py:83
  109.1 12.5 %shard_map.64 = (f32[1024,480]{1,0:T(8,128)}, f32[16,480]{1,0:T(8,128)}) custom-call(f32[1024,480]{1,0:T(8,128)} %get-tuple-element.10.d_ref, f32[8,8,480]{2,1,0:T(8,128)} %bitcast_select_fusion.hcol_ref, f32[8,16,480]{2,1,0:T(8,128)} %multiply_exponential_fusion.w_ref, f32[16,8,480]{2,1,0:T(8,128)} %get-tuple-element.11.g_ref, ...), custom_call_target="tpu_custom_call" | custom-call | tf_op jit(solution)/shard_map/pallas_call | solution.py:97
  121.6 7.9 %all-gather = f32[64,480]{1,0:T(8,128)S(1)} all-gather(f32[16,480]{1,0:T(8,128)} %get-tuple-element.8), channel_id=2, replica_groups=mesh['groups'=2,'context'=4,'tensor'=4] {'context'}, dimensions={0}, use_global_device_ids=true | all-gather | bytes 153600 | tf_op jit(solution)/shard_map/all_gather | solution.py:108
  129.6 0.7 multiply_reduce_fusion.sin_ref
  130.2 7.9 %shard_map.65 = f32[1024,480]{1,0:T(8,128)} custom-call(f32[1024,480]{1,0:T(8,128)} %get-tuple-element.7.conv_ref, f32[1024,480]{1,0:T(8,128)} %get-tuple-element.9.q_ref, f32[16,8,480]{2,1,0:T(8,128)} %get-tuple-element.11.g_ref, f32[16,480]{1,0:T(8,128)} %multiply_exponential_fusion.1.a8_ref, f32[16,480]{1,0:T(8,128)} %multiply_reduce_fusion.sin_ref), custom_call_target="tpu_custom_call" | custom-call | tf_op jit(solution)/shard_map/pallas_call | solution.py:119
  138.1 0.0 copy-done
  138.1 5.7 %convolution_convert_fusion = bf16[1024,1920]{0,1:T(8,128)(2,1)} fusion(bf16[480,1920]{1,0:T(8,128)(2,1)S(1)} %copy-done, f32[1024,480]{1,0:T(8,128)} %shard_map.65), kind=kOutput, calls=%fused_computation.9 | convolution fusion | flops 1889894400 | bytes 7741440 | tf_op jit(solution)/shard_map/dot_general | solution.py:127
  143.9 0.0 reduce-scatter.2.cloned.1.call-update
  143.9 71.7 %reduce-scatter.2.cloned.1.call-done = bf16[1024,480]{0,1:T(8,128)(2,1)} async-done(((bf16[1024,1920]{0,1:T(8,128)(2,1)}), bf16[1024,480]{0,1:T(8,128)(2,1)}) %reduce-scatter.2.cloned.1.call-update) | async-done | bytes 983056 | tf_op jit(solution)/shard_map/reduce_scatter | solution.py:128
  (10 shorter events, 0.1 us)
Async XLA Ops:
  6.5 131.6 %copy-start = (bf16[480,1920]{1,0:T(8,128)(2,1)S(1)}, bf16[480,1920]{1,0:T(8,128)(2,1)}, u32[]{:S(2)}) copy-start(bf16[480,1920]{1,0:T(8,128)(2,1)} %param.11) | copy-start | bytes 5529604
  6.5 81.5 %all-gather.3.cloned.1.call-start = ((), (), s32[]{:S(2)}) async-start(), calls=%async_computation.1 | async-start | bytes 4915200 | tf_op jit(solution)/shard_map/all_gather | solution.py:71
  7.3 208.3 %reduce-scatter.2.cloned.1.call-start = ((), (), s32[]{:S(2)}) async-start(), calls=%async_computation.2 | async-start | bytes 4915200 | tf_op jit(solution)/shard_map/reduce_scatter | solution.py:128
  98.2 2.4 %collective-permute-start = (bf16[6,3,480]{2,0,1:T(8,128)(2,1)S(1)}, bf16[6,3,480]{2,0,1:T(8,128)(2,1)S(1)}, u32[]{:S(2)}, u32[]{:S(2)}) collective-permute-start(bf16[6,3,480]{2,0,1:T(8,128)(2,1)S(1)} %slice.70), channel_id=1, source_target_pairs={{0,4},{4,8},{8,12},{1,5},{5,9},{9,13},{2,6},{6,10},{10,14},{3,7},{... | collective-permute-start | bytes 51848 | tf_op jit(solution)/shard_map/ppermute | solution.py:15
Sparse Core Ops, SparseCore 0:
  8.9 79.1 all-gather.2
  144.0 71.5 reduce-scatter.1

commit v2 on v1

--- a/solution.py
+++ b/solution.py
@@ -62,27 +62,10 @@
     return pl.BlockSpec(memory_space=pltpu.VMEM)
 
 
-def per_device(tokens, in_weight, short_filter, mode_weight, decay_rate, out_weight):
-    tok_rows = tokens.shape[0]
-    channels = in_weight.shape[2]
-    modes = decay_rate.shape[1]
-    proj = jnp.einsum(
-        "td,dkc->tkc",
-        lax.all_gather(tokens, "tensor", axis=1, tiled=True),
-        in_weight,
-        preferred_element_type=jnp.float32,
-    ).astype(jnp.bfloat16)
-    rim = shifted(proj[tok_rows - (TAPS - 1) :], "context", 1)
-    padded = jnp.concatenate([rim, proj], 0)
-    filtered = jnp.zeros((tok_rows, 3, channels), jnp.float32)
-    for tap_number in range(TAPS):
-        begin = TAPS - 1 - tap_number
-        filtered = filtered + short_filter[tap_number].astype(jnp.float32)[None] * padded[
-            begin : begin + tok_rows
-        ].astype(jnp.float32)
-    query = filtered[:, 0]
-    drive = filtered[:, 1] * filtered[:, 2]
+NCH = 2
 
+
+def chunk_tables(decay_rate, mode_weight):
     lam = decay_rate.T
     amp = (mode_weight * jnp.sqrt(2.0 * decay_rate)).T
     steps = jnp.arange(CHUNK).astype(jnp.float32)
@@ -93,11 +76,16 @@
     lag_index = jnp.clip(lag, 0, CHUNK - 1).astype(jnp.int32)
     hcol = jnp.where((lag >= 0)[:, :, None], h_short[lag_index], 0.0)
     a8 = jnp.exp(-lam * CHUNK)
+    return lam, g_tab, w_tab, hcol, a8
 
-    conv_local, end_state = pl.pallas_call(
+
+def local_conv(drive, hcol, w_tab, g_tab, a8):
+    rows, channels = drive.shape
+    modes = a8.shape[0]
+    return pl.pallas_call(
         local_kernel,
         out_shape=(
-            jax.ShapeDtypeStruct((tok_rows, channels), jnp.float32),
+            jax.ShapeDtypeStruct((rows, channels), jnp.float32),
             jax.ShapeDtypeStruct((modes, channels), jnp.float32),
         ),
         in_specs=[vmem_spec() for _ in range(5)],
@@ -105,30 +93,69 @@
         scratch_shapes=[pltpu.VMEM((modes, channels), jnp.float32)],
     )(drive, hcol, w_tab, g_tab, a8)
 
-    ends = lax.all_gather(end_state, "context", axis=0, tiled=False)
-    block_count = ends.shape[0]
-    me = lax.axis_index("context")
-    gap = (me - 1 - jnp.arange(block_count)).astype(jnp.float32)
-    factor = jnp.where(
-        (gap >= 0.0)[:, None, None],
-        jnp.exp(-lam[None] * (tok_rows * jnp.maximum(gap, 0.0))[:, None, None]),
-        0.0,
-    )
-    state_in = jnp.sum(factor * ends, axis=0)
 
-    gated = pl.pallas_call(
+def gate(conv_local, query, g_tab, a8, state_in):
+    rows, channels = conv_local.shape
+    modes = a8.shape[0]
+    return pl.pallas_call(
         gate_kernel,
-        out_shape=jax.ShapeDtypeStruct((tok_rows, channels), jnp.float32),
+        out_shape=jax.ShapeDtypeStruct((rows, channels), jnp.float32),
         in_specs=[vmem_spec() for _ in range(5)],
         out_specs=vmem_spec(),
         scratch_shapes=[pltpu.VMEM((modes, channels), jnp.float32)],
     )(conv_local, query, g_tab, a8, state_in)
-    gated = gated.astype(jnp.bfloat16)
-    partial_sums = jnp.dot(gated, out_weight, preferred_element_type=jnp.float32)
-    summed = lax.psum_scatter(
-        partial_sums.astype(jnp.bfloat16), "tensor", scatter_dimension=1, tiled=True
-    )
-    return summed
+
+
+def per_device(tokens, in_weight, short_filter, mode_weight, decay_rate, out_weight):
+    tok_rows = tokens.shape[0]
+    channels = in_weight.shape[2]
+    rim_rows = TAPS - 1
+    piece = tok_rows // NCH
+    lam, g_tab, w_tab, hcol, a8 = chunk_tables(decay_rate, mode_weight)
+    taps = short_filter.astype(jnp.float32)
+
+    rim = shifted(tokens[tok_rows - rim_rows :], "context", 1)
+    queries, convs, ends = [], [], []
+    for k in range(NCH):
+        before = rim if k == 0 else tokens[k * piece - rim_rows : k * piece]
+        ext = jnp.concatenate([before, tokens[k * piece : (k + 1) * piece]], 0)
+        full = lax.all_gather(ext, "tensor", axis=1, tiled=True)
+        proj = jnp.einsum(
+            "td,dkc->tkc", full, in_weight, preferred_element_type=jnp.float32
+        ).astype(jnp.bfloat16)
+        filtered = jnp.zeros((piece, 3, channels), jnp.float32)
+        for tap_number in range(TAPS):
+            begin = rim_rows - tap_number
+            filtered = filtered + taps[tap_number][None] * proj[begin : begin + piece].astype(
+                jnp.float32
+            )
+        drive = filtered[:, 1] * filtered[:, 2]
+        conv_local, end_state = local_conv(drive, hcol, w_tab, g_tab, a8)
+        queries.append(filtered[:, 0])
+        convs.append(conv_local)
+        ends.append(end_state)
+
+    piece_decay = jnp.exp(-lam * piece)
+    block_end = jnp.zeros_like(ends[0])
+    for k in range(NCH):
+        block_end = piece_decay * block_end + ends[k]
+    state_in = jnp.zeros_like(block_end)
+    for by in range(1, lax.axis_size("context")):
+        earlier = shifted(block_end, "context", by)
+        state_in = state_in + jnp.exp(-lam * (tok_rows * (by - 1))) * earlier
+
+    outs = []
+    state = state_in
+    for k in range(NCH):
+        gated = gate(convs[k], queries[k], g_tab, a8, state).astype(jnp.bfloat16)
+        state = piece_decay * state + ends[k]
+        partial_sums = jnp.dot(gated, out_weight, preferred_element_type=jnp.float32)
+        outs.append(
+            lax.psum_scatter(
+                partial_sums.astype(jnp.bfloat16), "tensor", scatter_dimension=1, tiled=True
+            )
+        )
+    return jnp.concatenate(outs, 0)
 
 
 def solution(mesh):

time: 223 us -> 244 us (1.094)
  local copies, waits for them, and re-layouts: 0.77 us -> 23.6 us
  waiting for transfers between devices: 147 us -> 136 us
  blocking collectives: 7.93 us -> 0 us
  starting transfers between devices: 1.63 us -> 8.52 us
  matrix products: 15.8 us -> 20.9 us
  Pallas kernels: 20.4 us -> 23.7 us
  other arithmetic: 14.9 us -> 17.5 us
    all_gather x1 -> x2, waiting for transfers between devices: 74.2 us -> 59.1 us  [per_device(): full = lax.all_gather(ext, 'tensor', axis=1, tiled=True)]
    unnamed x6 -> x19, local copies, waits for them, and re-layouts: 0.03 us -> 12.3 us
    all_gather x0 -> x2, local copies, waits for them, and re-layouts: none -> 8.08 us  [per_device(): full = lax.all_gather(ext, 'tensor', axis=1, tiled=True)]
    all_gather x1 -> x0, blocking collectives: 7.93 us -> none  [per_device(): ends = lax.all_gather(end_state, 'context', axis=0, tiled=False)]
    ppermute x1 -> x4, starting transfers between devices: 1.59 us -> 8.36 us  [shifted(): return lax.ppermute(array, axis, pairs)]
    reduce_scatter x1 -> x2, waiting for transfers between devices: 71.7 us -> 76 us  [per_device(): lax.psum_scatter(partial_sums.astype(jnp.bfloat16), 'tensor', scatter_dim...]
    pallas_call x2 -> x4, Pallas kernels: 20.4 us -> 23.7 us  [the longest x2 14.3 us: local_conv(): pl.pallas_call(local_kernel, out_shape=(jax.ShapeDtypeStruct((rows, chann...]
    dot_general x1 -> x2, matrix products: 10.1 us -> 13.3 us  [per_device(): jnp.einsum('td,dkc->tkc', full, in_weight, preferred_element_type=jnp.flo...]
  transfers between devices with their start and end apart: 3 -> 8, of which waited for: 3 -> 5; matrix products, arithmetic and copies ran while one was open for 3% -> 13% of each run, Pallas kernels for 0% -> 5%
where the time goes in v2:
time: 244 us
  waiting for transfers between devices  136 us (56%)
  Pallas kernels  23.7 us (10%)
  local copies, waits for them, and re-layouts  23.6 us (10%)
  matrix products  20.9 us (9%)
  other arithmetic  17.5 us (7%)
  between operations  13.3 us (5%)
  starting transfers between devices  8.52 us (3%)
    reduce_scatter x2, waiting for transfers between devices, per_device(): lax.psum_scatter(partial_sums.astype(jnp.bfloat16), 'tensor', scatter_dim...  76 us
    all_gather x2, waiting for transfers between devices, per_device(): full = lax.all_gather(ext, 'tensor', axis=1, tiled=True)  59.1 us
    pallas_call x2, Pallas kernels, local_conv(): pl.pallas_call(local_kernel, out_shape=(jax.ShapeDtypeStruct((rows, chann...  14.3 us
    dot_general x2, matrix products, per_device(): jnp.einsum('td,dkc->tkc', full, in_weight, preferred_element_type=jnp.flo...  13.3 us
    unnamed x19, local copies, waits for them, and re-layouts  12.3 us
    pallas_call x2, Pallas kernels, gate(): pl.pallas_call(gate_kernel, out_shape=jax.ShapeDtypeStruct((rows, channel...  9.46 us
    ppermute x4, starting transfers between devices, shifted(): return lax.ppermute(array, axis, pairs)  8.36 us
    all_gather x2, local copies, waits for them, and re-layouts, per_device(): full = lax.all_gather(ext, 'tensor', axis=1, tiled=True)  8.08 us
  transfers between devices with their start and end apart: 8, of which 5 were waited for; matrix products, arithmetic and copies ran while one was open for 13% of the time, Pallas kernels for 5%

profile of v2, /device:TPU:0, one launch (start us, length us, event | category | flops | bytes accessed | tf_op | source)
XLA Modules:
  0.0 243.6 jit_solution(14213229259831065044)
XLA Ops:
  6.6 1.5 concatenate.10
  8.1 1.0 copy.25
  9.2 1.0 slice.98
  10.3 2.4 collective-permute-start
  13.0 0.8 exponential_multiply_fusion
  14.7 1.0 maximum_bitcast_fusion
  18.0 40.2 %all-gather.7.cloned.1.call-done = bf16[4,480,518]{1,2,0:T(8,128)(2,1)} async-done(((bf16[1,480,518]{1,2,0:T(8,128)(2,1)}), bf16[4,480,518]{1,2,0:T(8,128)(2,1)}) %all-gather.7.cloned.1.call-update) | async-done | bytes 1989136 | tf_op jit(solution)/shard_map/all_gather | solution.py:122
  58.2 4.1 %copy.15 = bf16[4,480,518]{1,0,2:T(4,128)(2,1)} copy(bf16[4,480,518]{1,2,0:T(8,128)(2,1)} %all-gather.7.cloned.1.call-done) | data formatting | bytes 3978240 | tf_op jit(solution)/shard_map/all_gather | solution.py:122
  62.3 5.5 %reshape.123 = bf16[1920,518,1]{0,1,2:T(8,128)(2,1)} reshape(bf16[4,480,518]{1,0,2:T(4,128)(2,1)} %copy.15) | data formatting | bytes 3978240
  67.7 6.7 %convolution_convert_fusion.2 = bf16[518,3,480]{2,0,1:T(8,128)(2,1)S(1)} fusion(bf16[1920,518,1]{0,1,2:T(8,128)(2,1)} %reshape.123, bf16[1920,3,480]{0,2,1:T(8,128)(2,1)} %param.7), kind=kOutput, calls=%fused_computation.5 | convolution fusion | flops 2865078784 | bytes 9010560 | tf_op jit(solution)/shard_map/td,dkc->tkc/dot_general | solution.py:123
  74.4 2.7 %multiply_add_fusion = f32[512,3,480]{2,0,1:T(8,128)S(1)} fusion(bf16[518,3,480]{2,0,1:T(8,128)(2,1)S(1)} %convolution_convert_fusion.2, f32[3,480]{1,0:T(4,128)S(1)} %get-tuple-element.30, f32[3,480]{1,0:T(4,128)S(1)} %get-tuple-element.31, f32[3,480]{1,0:T(4,128)S(1)} %get-tuple-element.32, f32[3,480]{1,0:T(4,128)S(1)} %get-tuple-element.33, ...), kind=kLoop, calls=%fused_computation.1 | loop fusion | flops 14745600 | bytes 13311360 | tf_op jit(solution)/shard_map/add | solution.py:129
  77.1 1.7 slice_bitcast_fusion
  78.8 7.1 %shard_map.65 = (f32[512,480]{1,0:T(8,128)}, f32[16,480]{1,0:T(8,128)}) custom-call(f32[512,480]{1,0:T(8,128)} %get-tuple-element.18.d_ref, f32[8,8,480]{2,1,0:T(8,128)} %bitcast_select_fusion.hcol_ref, f32[8,16,480]{2,1,0:T(8,128)} %multiply_exponential_fusion.w_ref, f32[16,8,480]{2,1,0:T(8,128)} %get-tuple-element.19.g_ref, ...), custom_call_target="tpu_custom_call" | custom-call | tf_op jit(solution)/shard_map/pallas_call | solution.py:85
  85.9 18.9 %all-gather.5.cloned.1.call-done = bf16[4,480,518]{1,2,0:T(8,128)(2,1)} async-done(((bf16[1,480,518]{1,2,0:T(8,128)(2,1)}), bf16[4,480,518]{1,2,0:T(8,128)(2,1)}) %all-gather.5.cloned.1.call-update) | async-done | bytes 1989136 | tf_op jit(solution)/shard_map/all_gather | solution.py:122
  104.8 4.0 %copy.13 = bf16[4,480,518]{1,0,2:T(4,128)(2,1)} copy(bf16[4,480,518]{1,2,0:T(8,128)(2,1)} %all-gather.5.cloned.1.call-done) | data formatting | bytes 3978240 | tf_op jit(solution)/shard_map/all_gather | solution.py:122
  108.8 5.5 %reshape.122 = bf16[1920,518,1]{0,1,2:T(8,128)(2,1)} reshape(bf16[4,480,518]{1,0,2:T(4,128)(2,1)} %copy.13) | data formatting | bytes 3978240
  114.3 6.7 %convolution_convert_fusion.3 = bf16[518,3,480]{2,0,1:T(8,128)(2,1)S(1)} fusion(bf16[1920,518,1]{0,1,2:T(8,128)(2,1)} %reshape.122, bf16[1920,3,480]{0,2,1:T(8,128)(2,1)} %param.7), kind=kOutput, calls=%fused_computation.6 | convolution fusion | flops 2865078784 | bytes 9010560 | tf_op jit(solution)/shard_map/td,dkc->tkc/dot_general | solution.py:123
  121.0 2.9 %multiply_add_fusion.1 = f32[512,3,480]{2,0,1:T(8,128)S(1)} fusion(bf16[518,3,480]{2,0,1:T(8,128)(2,1)S(1)} %convolution_convert_fusion.3, f32[3,480]{1,0:T(4,128)S(1)} %get-tuple-element.30, f32[3,480]{1,0:T(4,128)S(1)} %get-tuple-element.31, f32[3,480]{1,0:T(4,128)S(1)} %get-tuple-element.32, f32[3,480]{1,0:T(4,128)S(1)} %get-tuple-element.33, ...), kind=kLoop, calls=%fused_computation.2 | loop fusion | flops 14745600 | bytes 13311360 | tf_op jit(solution)/shard_map/add | solution.py:129
  123.9 1.7 slice_bitcast_fusion.1
  125.6 7.1 %shard_map.64 = (f32[512,480]{1,0:T(8,128)}, f32[16,480]{1,0:T(8,128)}) custom-call(f32[512,480]{1,0:T(8,128)} %get-tuple-element.16.d_ref, f32[8,8,480]{2,1,0:T(8,128)} %bitcast_select_fusion.hcol_ref, f32[8,16,480]{2,1,0:T(8,128)} %multiply_exponential_fusion.w_ref, f32[16,8,480]{2,1,0:T(8,128)} %get-tuple-element.19.g_ref, ...), custom_call_target="tpu_custom_call" | custom-call | tf_op jit(solution)/shard_map/pallas_call | solution.py:85
  133.5 2.6 %collective-permute-start.3 = (f32[16,480]{1,0:T(8,128)S(1)}, f32[16,480]{1,0:T(8,128)S(1)}, u32[]{:S(2)}, u32[]{:S(2)}) collective-permute-start(f32[16,480]{1,0:T(8,128)S(1)} %multiply_add_fusion.4), channel_id=1, source_target_pairs={{0,12},{1,13},{2,14},{3,15},{16,28},{17,29},{18,30},{19,31}} | collective-permute-start | bytes 92168 | tf_op jit(solution)/shard_map/ppermute | solution.py:15
  136.1 1.4 collective-permute-start.2
  137.5 1.9 collective-permute-start.1
  139.5 0.8 collective-permute-done.1
  140.3 1.4 multiply_add_fusion.2
  141.7 4.7 %shard_map.67 = f32[512,480]{1,0:T(8,128)} custom-call(f32[512,480]{1,0:T(8,128)} %get-tuple-element.12.conv_ref, f32[512,480]{1,0:T(8,128)} %get-tuple-element.17.q_ref, f32[16,8,480]{2,1,0:T(8,128)} %get-tuple-element.19.g_ref, f32[16,480]{1,0:T(8,128)} %multiply_exponential_fusion.2.a8_ref, f32[16,480]{1,0:T(8,128)} %get-tuple-element.13.sin_ref), custom_call_target="tpu_custom_call" | custom-call | tf_op jit(solution)/shard_map/pallas_call | solution.py:100
  146.4 3.8 %convolution_convert_fusion = bf16[512,1920]{0,1:T(8,128)(2,1)} fusion(bf16[480,1920]{1,0:T(8,128)(2,1)S(1)} %copy-done, f32[512,480]{1,0:T(8,128)} %shard_map.67), kind=kOutput, calls=%fused_computation.3 | convolution fusion | flops 944947200 | bytes 4792320 | tf_op jit(solution)/shard_map/dot_general | solution.py:152
  150.3 4.7 %shard_map.66 = f32[512,480]{1,0:T(8,128)} custom-call(f32[512,480]{1,0:T(8,128)} %get-tuple-element.9.conv_ref, f32[512,480]{1,0:T(8,128)} %get-tuple-element.15.q_ref, f32[16,8,480]{2,1,0:T(8,128)} %get-tuple-element.19.g_ref, f32[16,480]{1,0:T(8,128)} %multiply_exponential_fusion.2.a8_ref, f32[16,480]{1,0:T(8,128)} %get-tuple-element.14.sin_ref), custom_call_target="tpu_custom_call" | custom-call | tf_op jit(solution)/shard_map/pallas_call | solution.py:100
  155.0 3.8 %convolution_convert_fusion.1 = bf16[512,1920]{0,1:T(8,128)(2,1)} fusion(bf16[480,1920]{1,0:T(8,128)(2,1)S(1)} %copy-done, f32[512,480]{1,0:T(8,128)} %shard_map.66), kind=kOutput, calls=%fused_computation.4 | convolution fusion | flops 944947200 | bytes 4792320 | tf_op jit(solution)/shard_map/dot_general | solution.py:152
  158.8 33.1 %reduce-scatter.5.cloned.1.call-done = bf16[512,480]{0,1:T(8,128)(2,1)} async-done(((bf16[512,1920]{0,1:T(8,128)(2,1)}), bf16[512,480]{0,1:T(8,128)(2,1)}) %reduce-scatter.5.cloned.1.call-update) | async-done | bytes 491536 | tf_op jit(solution)/shard_map/reduce_scatter | solution.py:154
  191.9 42.9 %reduce-scatter.3.cloned.1.call-done = bf16[512,480]{0,1:T(8,128)(2,1)} async-done(((bf16[512,1920]{0,1:T(8,128)(2,1)}), bf16[512,480]{0,1:T(8,128)(2,1)}) %reduce-scatter.3.cloned.1.call-update) | async-done | bytes 491536 | tf_op jit(solution)/shard_map/reduce_scatter | solution.py:154
  234.8 2.2 pad_maximum_fusion
  (42 shorter events, 4.5 us)
Async XLA Ops:
  6.5 139.9 %copy-start = (bf16[480,1920]{1,0:T(8,128)(2,1)S(1)}, bf16[480,1920]{1,0:T(8,128)(2,1)}, u32[]{:S(2)}) copy-start(bf16[480,1920]{1,0:T(8,128)(2,1)} %param.11) | copy-start | bytes 5529604
  6.5 7.3 %slice-start = ((bf16[1024,480]{0,1:T(8,128)(2,1)}), bf16[512,480]{0,1:T(8,128)(2,1)S(1)}, s32[]{:S(2)}) async-start(bf16[1024,480]{0,1:T(8,128)(2,1)} %param.6), calls=%async_computation.6 | async-start | bytes 983040 | tf_op jit(solution)/shard_map/slice | solution.py:121
  6.5 6.4 %copy-start.2 = (bf16[7,3,480]{2,0,1:T(8,128)(2,1)S(1)}, bf16[7,3,480]{2,0,1:T(8,128)(2,1)}, u32[]{:S(2)}) copy-start(bf16[7,3,480]{2,0,1:T(8,128)(2,1)} %param.8) | copy-start | bytes 60484
  6.5 6.4 %copy-start.1 = (f32[480,16]{0,1:T(8,128)S(1)}, f32[480,16]{0,1:T(8,128)}, u32[]{:S(2)}) copy-start(f32[480,16]{0,1:T(8,128)} %param.10) | copy-start | bytes 92164
  6.5 6.4 %copy-start.3 = (f32[480,16]{0,1:T(8,128)S(1)}, f32[480,16]{0,1:T(8,128)}, u32[]{:S(2)}) copy-start(f32[480,16]{0,1:T(8,128)} %param.9) | copy-start | bytes 92164
  6.5 51.7 %all-gather.7.cloned.1.call-start = ((), (), s32[]{:S(2)}) async-start(), calls=%async_computation.5 | async-start | bytes 2662400 | tf_op jit(solution)/shard_map/all_gather | solution.py:122
  9.1 95.7 %all-gather.5.cloned.1.call-start = ((), (), s32[]{:S(2)}) async-start(), calls=%async_computation.4 | async-start | bytes 2662400 | tf_op jit(solution)/shard_map/all_gather | solution.py:122
  10.3 4.4 %collective-permute-start = (bf16[6,480]{1,0:T(8,128)(2,1)S(1)}, bf16[6,480]{1,0:T(8,128)(2,1)S(1)}, u32[]{:S(2)}, u32[]{:S(2)}) collective-permute-start(bf16[6,480]{1,0:T(8,128)(2,1)S(1)} %copy.23), channel_id=1, source_target_pairs={{0,4},{4,8},{8,12},{1,5},{5,9},{9,13},{2,6},{6,10},{10,14},{3,7},{... | collective-permute-start | bytes 17288 | tf_op jit(solution)/shard_map/ppermute | solution.py:15
  15.7 176.2 %reduce-scatter.5.cloned.1.call-start = ((), (), s32[]{:S(2)}) async-start(), calls=%async_computation.3 | async-start | bytes 2457600 | tf_op jit(solution)/shard_map/reduce_scatter | solution.py:154
  123.9 8.8 %copy-start.4 = (f32[16,480]{1,0:T(8,128)S(1)}, f32[16,480]{1,0:T(8,128)}, u32[]{:S(2)}) copy-start(f32[16,480]{1,0:T(8,128)} %get-tuple-element.11) | copy-start | bytes 92164
  133.5 6.0 %collective-permute-start.3 = (f32[16,480]{1,0:T(8,128)S(1)}, f32[16,480]{1,0:T(8,128)S(1)}, u32[]{:S(2)}, u32[]{:S(2)}) collective-permute-start(f32[16,480]{1,0:T(8,128)S(1)} %multiply_add_fusion.4), channel_id=1, source_target_pairs={{0,12},{1,13},{2,14},{3,15},{16,28},{17,29},{18,30},{19,31}} | collective-permute-start | bytes 92168 | tf_op jit(solution)/shard_map/ppermute | solution.py:15
  136.1 3.3 %collective-permute-start.2 = (f32[16,480]{1,0:T(8,128)S(1)}, f32[16,480]{1,0:T(8,128)S(1)}, u32[]{:S(2)}, u32[]{:S(2)}) collective-permute-start(f32[16,480]{1,0:T(8,128)S(1)} %multiply_add_fusion.4), channel_id=1, source_target_pairs={{0,8},{4,12},{1,9},{5,13},{2,10},{6,14},{3,11},{7,15},{16,24},{20,... | collective-permute-start | bytes 92168 | tf_op jit(solution)/shard_map/ppermute | solution.py:15
  137.5 2.8 %collective-permute-start.1 = (f32[16,480]{1,0:T(8,128)S(1)}, f32[16,480]{1,0:T(8,128)S(1)}, u32[]{:S(2)}, u32[]{:S(2)}) collective-permute-start(f32[16,480]{1,0:T(8,128)S(1)} %multiply_add_fusion.4), channel_id=1, source_target_pairs={{0,4},{4,8},{8,12},{1,5},{5,9},{9,13},{2,6},{6,10},{10,14},{3,7},{... | collective-permute-start | bytes 92168 | tf_op jit(solution)/shard_map/ppermute | solution.py:15
  150.2 84.6 %reduce-scatter.3.cloned.1.call-start = ((), (), s32[]{:S(2)}) async-start(), calls=%async_computation.2 | async-start | bytes 2457600 | tf_op jit(solution)/shard_map/reduce_scatter | solution.py:154
Sparse Core Ops, SparseCore 0:
  9.3 48.9 all-gather.6
  59.8 44.9 all-gather.4
  150.4 41.5 reduce-scatter.4
  194.1 40.6 reduce-scatter.2

commit v3 on v2

--- a/solution.py
+++ b/solution.py
@@ -62,9 +62,6 @@
     return pl.BlockSpec(memory_space=pltpu.VMEM)
 
 
-NCH = 2
-
-
 def chunk_tables(decay_rate, mode_weight):
     lam = decay_rate.T
     amp = (mode_weight * jnp.sqrt(2.0 * decay_rate)).T
@@ -106,56 +103,66 @@
     )(conv_local, query, g_tab, a8, state_in)
 
 
+def relay_pairs(size, step, forward):
+    if forward:
+        return [(i, i + 1) for i in range(step - 1, size - 1)]
+    return [(i, i - 1) for i in range(1, size - step + 1)]
+
+
+def gathered_projection(tokens, in_weight):
+    size = lax.axis_size("tensor")
+    me = lax.axis_index("tensor")
+    feats = tokens.shape[1]
+
+    def rows_of(owner):
+        owner = jnp.clip(owner, 0, size - 1)
+        return lax.dynamic_slice_in_dim(in_weight, owner * feats, feats, 0)
+
+    acc = jnp.einsum("td,dkc->tkc", tokens, rows_of(me), preferred_element_type=jnp.float32)
+    fwd = tokens
+    bwd = tokens
+    for step in range(1, size):
+        fwd = lax.ppermute(fwd, "tensor", relay_pairs(size, step, True))
+        bwd = lax.ppermute(bwd, "tensor", relay_pairs(size, step, False))
+        acc = acc + jnp.einsum(
+            "td,dkc->tkc", fwd, rows_of(me - step), preferred_element_type=jnp.float32
+        )
+        acc = acc + jnp.einsum(
+            "td,dkc->tkc", bwd, rows_of(me + step), preferred_element_type=jnp.float32
+        )
+    return acc.astype(jnp.bfloat16)
+
+
 def per_device(tokens, in_weight, short_filter, mode_weight, decay_rate, out_weight):
     tok_rows = tokens.shape[0]
     channels = in_weight.shape[2]
     rim_rows = TAPS - 1
-    piece = tok_rows // NCH
     lam, g_tab, w_tab, hcol, a8 = chunk_tables(decay_rate, mode_weight)
     taps = short_filter.astype(jnp.float32)
 
-    rim = shifted(tokens[tok_rows - rim_rows :], "context", 1)
-    queries, convs, ends = [], [], []
-    for k in range(NCH):
-        before = rim if k == 0 else tokens[k * piece - rim_rows : k * piece]
-        ext = jnp.concatenate([before, tokens[k * piece : (k + 1) * piece]], 0)
-        full = lax.all_gather(ext, "tensor", axis=1, tiled=True)
-        proj = jnp.einsum(
-            "td,dkc->tkc", full, in_weight, preferred_element_type=jnp.float32
-        ).astype(jnp.bfloat16)
-        filtered = jnp.zeros((piece, 3, channels), jnp.float32)
-        for tap_number in range(TAPS):
-            begin = rim_rows - tap_number
-            filtered = filtered + taps[tap_number][None] * proj[begin : begin + piece].astype(
-                jnp.float32
-            )
-        drive = filtered[:, 1] * filtered[:, 2]
-        conv_local, end_state = local_conv(drive, hcol, w_tab, g_tab, a8)
-        queries.append(filtered[:, 0])
-        convs.append(conv_local)
-        ends.append(end_state)
+    proj = gathered_projection(tokens, in_weight)
+    rim = shifted(proj[tok_rows - rim_rows :], "context", 1)
+    padded = jnp.concatenate([rim, proj], 0)
+    filtered = jnp.zeros((tok_rows, 3, channels), jnp.float32)
+    for tap_number in range(TAPS):
+        begin = rim_rows - tap_number
+        filtered = filtered + taps[tap_number][None] * padded[begin : begin + tok_rows].astype(
+            jnp.float32
+        )
+    query = filtered[:, 0]
+    drive = filtered[:, 1] * filtered[:, 2]
+    conv_local, block_end = local_conv(drive, hcol, w_tab, g_tab, a8)
 
-    piece_decay = jnp.exp(-lam * piece)
-    block_end = jnp.zeros_like(ends[0])
-    for k in range(NCH):
-        block_end = piece_decay * block_end + ends[k]
     state_in = jnp.zeros_like(block_end)
     for by in range(1, lax.axis_size("context")):
         earlier = shifted(block_end, "context", by)
         state_in = state_in + jnp.exp(-lam * (tok_rows * (by - 1))) * earlier
 
-    outs = []
-    state = state_in
-    for k in range(NCH):
-        gated = gate(convs[k], queries[k], g_tab, a8, state).astype(jnp.bfloat16)
-        state = piece_decay * state + ends[k]
-        partial_sums = jnp.dot(gated, out_weight, preferred_element_type=jnp.float32)
-        outs.append(
-            lax.psum_scatter(
-                partial_sums.astype(jnp.bfloat16), "tensor", scatter_dimension=1, tiled=True
-            )
-        )
-    return jnp.concatenate(outs, 0)
+    gated = gate(conv_local, query, g_tab, a8, state_in).astype(jnp.bfloat16)
+    partial_sums = jnp.dot(gated, out_weight, preferred_element_type=jnp.float32)
+    return lax.psum_scatter(
+        partial_sums.astype(jnp.bfloat16), "tensor", scatter_dimension=1, tiled=True
+    )
 
 
 def solution(mesh):

time: 244 us -> 248 us (1.016)
  matrix products: 20.9 us -> 58.6 us
  waiting for transfers between devices: 136 us -> 101 us
  starting transfers between devices: 8.52 us -> 23.5 us
  local copies, waits for them, and re-layouts: 23.6 us -> 9.04 us
  other arithmetic: 17.5 us -> 21.2 us
  Pallas kernels: 23.7 us -> 20.4 us
    all_gather x2 -> x0, waiting for transfers between devices: 59.1 us -> none  [per_device(): full = lax.all_gather(ext, 'tensor', axis=1, tiled=True)]
    dot_general x2 -> x7, matrix products: 13.3 us -> 52.9 us  [the longest x3 26.3 us: gathered_projection(): jnp.einsum('td,dkc->tkc', bwd, rows_of(me + step), preferred_element_type...]
    ppermute x0 -> x6, waiting for transfers between devices: none -> 24 us  [the longest x3 16.6 us: gathered_projection(): bwd = lax.ppermute(bwd, 'tensor', relay_pairs(size, step, False))]
    ppermute x0 -> x6, starting transfers between devices: none -> 12.4 us  [the longest x3 8.35 us: gathered_projection(): fwd = lax.ppermute(fwd, 'tensor', relay_pairs(size, step, True))]
    unnamed x19 -> x12, local copies, waits for them, and re-layouts: 12.3 us -> 0.04 us
    all_gather x2 -> x0, local copies, waits for them, and re-layouts: 8.08 us -> none  [per_device(): full = lax.all_gather(ext, 'tensor', axis=1, tiled=True)]
    add x0 -> x1, local copies, waits for them, and re-layouts: none -> 6.5 us  [gathered_projection(): acc + jnp.einsum('td,dkc->tkc', fwd, rows_of(me - step), preferred_elemen...]
    add x4 -> x2, other arithmetic: 7.8 us -> 13.8 us  [the longest x1 13.2 us: per_device(): filtered + taps[tap_number][None] * padded[begin:begin + tok_rows].astype...]
  transfers between devices with their start and end apart: 8 -> 11, of which waited for: 5 -> 8; matrix products, arithmetic and copies ran while one was open for 13% -> 21% of each run, Pallas kernels for 5% -> 0%
where the time goes in v3:
time: 248 us; the launch traced here: 247 us
  waiting for transfers between devices  101 us (41%)
  matrix products  58.6 us (24%)
  starting transfers between devices  23.5 us (9%)
  other arithmetic  21.2 us (9%)
  Pallas kernels  20.4 us (8%)
  between operations  13.6 us (5%)
  local copies, waits for them, and re-layouts  9.04 us (4%)
    reduce_scatter x1, waiting for transfers between devices, per_device(): lax.psum_scatter(partial_sums.astype(jnp.bfloat16), 'tensor', scatter_dim...  74.4 us
    dot_general x3, matrix products, gathered_projection(): jnp.einsum('td,dkc->tkc', bwd, rows_of(me + step), preferred_element_type...  26.3 us
    dot_general x3, matrix products, gathered_projection(): jnp.einsum('td,dkc->tkc', fwd, rows_of(me - step), preferred_element_type...  20.6 us
    ppermute x3, waiting for transfers between devices, gathered_projection(): bwd = lax.ppermute(bwd, 'tensor', relay_pairs(size, step, False))  16.6 us
    add x1, other arithmetic, per_device(): filtered + taps[tap_number][None] * padded[begin:begin + tok_rows].astype...  13.2 us
    pallas_call x1, Pallas kernels, local_conv(): pl.pallas_call(local_kernel, out_shape=(jax.ShapeDtypeStruct((rows, chann...  12.5 us
    ppermute x4, starting transfers between devices, shifted(): return lax.ppermute(array, axis, pairs)  11.1 us
    ppermute x3, starting transfers between devices, gathered_projection(): fwd = lax.ppermute(fwd, 'tensor', relay_pairs(size, step, True))  8.35 us
  transfers between devices with their start and end apart: 11, of which 8 were waited for; matrix products, arithmetic and copies ran while one was open for 21% of the time, Pallas kernels for 0%

profile of v3, /device:TPU:0, one launch (start us, length us, event | category | flops | bytes accessed | tf_op | source)
XLA Modules:
  0.0 247.2 jit_solution(1628050388770492926)
XLA Ops:
  6.5 5.1 %collective-permute-start = (bf16[1024,480]{0,1:T(8,128)(2,1)}, bf16[1024,480]{0,1:T(8,128)(2,1)S(1)}, u32[]{:S(2)}, u32[]{:S(2)}) collective-permute-start(bf16[1024,480]{0,1:T(8,128)(2,1)} %param.6), channel_id=1, source_target_pairs={{0,1},{1,2},{2,3},{4,5},{5,6},{6,7},{8,9},{9,10},{10,11},{12,13},{... | collective-permute-start | bytes 2949128 | tf_op jit(solution)/shard_map/ppermute | solution.py:125
  11.7 1.3 collective-permute-start.1
  14.0 0.8 exponential_multiply_fusion
  16.2 1.0 fusion.38
  17.3 1.4 multiply_exponential_fusion.1.a8_ref
  19.5 6.0 %fusion.20 = f32[3,480,1024]{2,1,0:T(8,128)} fusion(bf16[1920,3,480]{0,2,1:T(8,128)(2,1)} %param.7, s32[]{:T(128)S(6)} %select_n.35, bf16[1024,480]{0,1:T(8,128)(2,1)} %param.6), kind=kOutput, calls=%fused_computation.34 | convolution fusion | flops 1415577600 | bytes 8355844 | tf_op jit(solution)/shard_map/td,dkc->tkc/dot_general | solution.py:121
  25.5 7.5 %collective-permute-done = bf16[1024,480]{0,1:T(8,128)(2,1)S(1)} collective-permute-done((bf16[1024,480]{0,1:T(8,128)(2,1)}, bf16[1024,480]{0,1:T(8,128)(2,1)S(1)}, u32[]{:S(2)}, u32[]{:S(2)}) %collective-permute-start) | collective-permute-done | bytes 983072 | tf_op jit(solution)/shard_map/ppermute | solution.py:125
  32.9 1.6 collective-permute-start.2
  34.5 2.6 %collective-permute-done.1 = bf16[1024,480]{0,1:T(8,128)(2,1)} collective-permute-done((bf16[1024,480]{0,1:T(8,128)(2,1)}, bf16[1024,480]{0,1:T(8,128)(2,1)}, u32[]{:S(2)}, u32[]{:S(2)}) %collective-permute-start.1) | collective-permute-done | bytes 983072 | tf_op jit(solution)/shard_map/ppermute | solution.py:126
  37.1 1.3 collective-permute-start.3
  38.4 7.5 %convolution_add_fusion = f32[3,480,1024]{2,1,0:T(8,128)} fusion(f32[3,480,1024]{2,1,0:T(8,128)} %fusion.20, bf16[1920,3,480]{0,2,1:T(8,128)(2,1)} %param.7, s32[]{:T(128)S(6)} %select_n.36, bf16[1024,480]{0,1:T(8,128)(2,1)S(1)} %collective-permute-done), kind=kOutput, calls=%fused_computation.19 | convolution fusion | flops 1417052160 | bytes 14254084 | tf_op jit(solution)/shard_map/td,dkc->tkc/dot_general | solution.py:127
  46.0 1.6 collective-permute-start.4
  47.6 6.4 %fusion.17 = f32[3,480,1024]{1,2,0:T(8,128)} fusion(bf16[1920,3,480]{0,2,1:T(8,128)(2,1)} %param.7, s32[]{:T(128)S(6)} %select_n.37, bf16[1024,480]{0,1:T(8,128)(2,1)} %collective-permute-done.1), kind=kOutput, calls=%fused_computation.31 | convolution fusion | flops 1415577600 | bytes 8355844 | tf_op jit(solution)/shard_map/td,dkc->tkc/dot_general | solution.py:130
  54.0 6.5 %copy.21 = f32[3,480,1024]{1,2,0:T(8,128)} copy(f32[3,480,1024]{2,1,0:T(8,128)} %convolution_add_fusion) | data formatting | bytes 11796480 | tf_op jit(solution)/shard_map/add | solution.py:127
  60.5 2.2 collective-permute-done.3
  62.7 1.5 collective-permute-start.5
  64.1 6.3 %fusion.13 = f32[3,480,1024]{1,2,0:T(8,128)} fusion(bf16[1920,3,480]{0,2,1:T(8,128)(2,1)} %param.7, s32[]{:T(128)S(6)} %select_n.39, bf16[1024,480]{0,1:T(8,128)(2,1)} %collective-permute-done.3), kind=kOutput, calls=%fused_computation.27 | convolution fusion | flops 1415577600 | bytes 8355844 | tf_op jit(solution)/shard_map/td,dkc->tkc/dot_general | solution.py:130
  70.5 6.4 %fusion.15 = f32[3,480,1024]{1,2,0:T(8,128)} fusion(bf16[1920,3,480]{0,2,1:T(8,128)(2,1)} %param.7, s32[]{:T(128)S(6)} %select_n.38, bf16[1024,480]{0,1:T(8,128)(2,1)} %collective-permute-done.2), kind=kOutput, calls=%fused_computation.29 | convolution fusion | flops 1415577600 | bytes 8355844 | tf_op jit(solution)/shard_map/td,dkc->tkc/dot_general | solution.py:127
  76.9 6.6 %fusion.11 = f32[3,480,1024]{1,2,0:T(8,128)} fusion(bf16[1920,3,480]{0,2,1:T(8,128)(2,1)} %param.7, s32[]{:T(128)S(6)} %select_n.40, bf16[1024,480]{0,1:T(8,128)(2,1)} %collective-permute-done.4), kind=kOutput, calls=%fused_computation.25 | convolution fusion | flops 1415577600 | bytes 8355844 | tf_op jit(solution)/shard_map/td,dkc->tkc/dot_general | solution.py:127
  83.5 11.8 %collective-permute-done.5 = bf16[1024,480]{0,1:T(8,128)(2,1)} collective-permute-done((bf16[1024,480]{0,1:T(8,128)(2,1)}, bf16[1024,480]{0,1:T(8,128)(2,1)}, u32[]{:S(2)}, u32[]{:S(2)}) %collective-permute-start.5) | collective-permute-done | bytes 983072 | tf_op jit(solution)/shard_map/ppermute | solution.py:126
  95.2 13.6 %fusion = bf16[1024,3,480]{2,0,1:T(8,128)(2,1)} fusion(f32[3,480,1024]{1,2,0:T(8,128)} %fusion.11, f32[3,480,1024]{1,2,0:T(8,128)} %fusion.13, f32[3,480,1024]{1,2,0:T(8,128)} %fusion.15, f32[3,480,1024]{1,2,0:T(8,128)S(1)} %bitcast.56, f32[3,480,1024]{1,2,0:T(8,128)} %fusion.17, bf16[1920,3,480]{0,2,1:T(8,128)(2,1)} %param.7, s32[]{:T(128)S(6)} %select_n.41, ...), kind=kOutput, calls=%fused_computation.9 | convolution fusion | flops 1424424960 | bytes 36470788 | tf_op jit(solution)/shard_map/td,dkc->tkc/dot_general | solution.py:130
  109.6 1.5 collective-permute-start.6
  111.7 13.2 %multiply_add_fusion = f32[1024,3,480]{2,0,1:T(8,128)S(1)} fusion(bf16[1024,3,480]{2,0,1:T(8,128)(2,1)} %fusion, bf16[6,3,480]{2,0,1:T(8,128)(2,1)S(1)} %collective-permute-done.6, f32[3,480]{1,0:T(4,128)S(1)} %get-tuple-element.22, f32[3,480]{1,0:T(4,128)S(1)} %get-tuple-element.23, f32[3,480]{1,0:T(4,128)S(1)} %get-tuple-element.24, ...), kind=kLoop, calls=%fused_computation.7 | loop fusion | flops 56033280 | bytes 8904960 | tf_op jit(solution)/shard_map/add | solution.py:149
  124.9 2.7 %slice_bitcast_fusion = (f32[1024,480]{1,0:T(8,128)}, f32[1024,480]{1,0:T(8,128)}) fusion(f32[1024,3,480]{2,0,1:T(8,128)S(1)} %multiply_add_fusion), kind=kLoop, calls=%fused_computation.20 | loop fusion | flops 491520 | bytes 9830400 | tf_op jit(solution)/shard_map/squeeze | solution.py:152
  127.7 12.5 %shard_map.64 = (f32[1024,480]{1,0:T(8,128)}, f32[16,480]{1,0:T(8,128)}) custom-call(f32[1024,480]{1,0:T(8,128)} %get-tuple-element.10.d_ref, f32[8,8,480]{2,1,0:T(8,128)} %bitcast_select_fusion.hcol_ref, f32[8,16,480]{2,1,0:T(8,128)} %multiply_exponential_fusion.w_ref, f32[16,8,480]{2,1,0:T(8,128)} %get-tuple-element.11.g_ref, ...), custom_call_target="tpu_custom_call" | custom-call | tf_op jit(solution)/shard_map/pallas_call | solution.py:82
  140.1 4.2 %collective-permute-start.7 = (f32[16,480]{1,0:T(8,128)}, f32[16,480]{1,0:T(8,128)S(1)}, u32[]{:S(2)}, u32[]{:S(2)}) collective-permute-start(f32[16,480]{1,0:T(8,128)} %get-tuple-element.8), channel_id=1, source_target_pairs={{0,4},{4,8},{8,12},{1,5},{5,9},{9,13},{2,6},{6,10},{10,14},{3,7},{... | collective-permute-start | bytes 92168 | tf_op jit(solution)/shard_map/ppermute | solution.py:15
  144.4 4.1 %collective-permute-start.8 = (f32[16,480]{1,0:T(8,128)}, f32[16,480]{1,0:T(8,128)S(1)}, u32[]{:S(2)}, u32[]{:S(2)}) collective-permute-start(f32[16,480]{1,0:T(8,128)} %get-tuple-element.8), channel_id=1, source_target_pairs={{0,8},{4,12},{1,9},{5,13},{2,10},{6,14},{3,11},{7,15},{16,24},{20,... | collective-permute-start | bytes 92168 | tf_op jit(solution)/shard_map/ppermute | solution.py:15
  148.5 1.3 collective-permute-start.9
  150.4 1.3 collective-permute-done.9
  152.3 7.9 %shard_map.65 = f32[1024,480]{1,0:T(8,128)} custom-call(f32[1024,480]{1,0:T(8,128)} %get-tuple-element.7.conv_ref, f32[1024,480]{1,0:T(8,128)} %get-tuple-element.9.q_ref, f32[16,8,480]{2,1,0:T(8,128)} %get-tuple-element.11.g_ref, f32[16,480]{1,0:T(8,128)} %multiply_exponential_fusion.1.a8_ref, f32[16,480]{1,0:T(8,128)} %multiply_add_fusion.1.sin_ref), custom_call_target="tpu_custom_call" | custom-call | tf_op jit(solution)/shard_map/pallas_call | solution.py:97
  160.2 5.7 %convolution_convert_fusion = bf16[1024,1920]{0,1:T(8,128)(2,1)} fusion(bf16[480,1920]{1,0:T(8,128)(2,1)S(1)} %copy-done, f32[1024,480]{1,0:T(8,128)} %shard_map.65), kind=kOutput, calls=%fused_computation.8 | convolution fusion | flops 1889894400 | bytes 7741440 | tf_op jit(solution)/shard_map/dot_general | solution.py:162
  165.9 74.4 %reduce-scatter.2.cloned.1.call-done = bf16[1024,480]{0,1:T(8,128)(2,1)} async-done(((bf16[1024,1920]{0,1:T(8,128)(2,1)}), bf16[1024,480]{0,1:T(8,128)(2,1)}) %reduce-scatter.2.cloned.1.call-update) | async-done | bytes 983056 | tf_op jit(solution)/shard_map/reduce_scatter | solution.py:163
  (32 shorter events, 5.8 us)
Async XLA Ops:
  6.5 153.7 %copy-start = (bf16[480,1920]{1,0:T(8,128)(2,1)S(1)}, bf16[480,1920]{1,0:T(8,128)(2,1)}, u32[]{:S(2)}) copy-start(bf16[480,1920]{1,0:T(8,128)(2,1)} %param.11) | copy-start | bytes 5529604
  6.5 233.8 %reduce-scatter.2.cloned.1.call-start = ((), (), s32[]{:S(2)}) async-start(), calls=%async_computation.1 | async-start | bytes 4915200 | tf_op jit(solution)/shard_map/reduce_scatter | solution.py:163
  6.5 26.4 %collective-permute-start = (bf16[1024,480]{0,1:T(8,128)(2,1)}, bf16[1024,480]{0,1:T(8,128)(2,1)S(1)}, u32[]{:S(2)}, u32[]{:S(2)}) collective-permute-start(bf16[1024,480]{0,1:T(8,128)(2,1)} %param.6), channel_id=1, source_target_pairs={{0,1},{1,2},{2,3},{4,5},{5,6},{6,7},{8,9},{9,10},{10,11},{12,13},{... | collective-permute-start | bytes 2949128 | tf_op jit(solution)/shard_map/ppermute | solution.py:125
  11.7 25.4 %collective-permute-start.1 = (bf16[1024,480]{0,1:T(8,128)(2,1)}, bf16[1024,480]{0,1:T(8,128)(2,1)}, u32[]{:S(2)}, u32[]{:S(2)}) collective-permute-start(bf16[1024,480]{0,1:T(8,128)(2,1)} %param.6), channel_id=1, source_target_pairs={{1,0},{2,1},{3,2},{5,4},{6,5},{7,6},{9,8},{10,9},{11,10},{13,12},{... | collective-permute-start | bytes 2949128 | tf_op jit(solution)/shard_map/ppermute | solution.py:126
  32.9 13.1 %collective-permute-start.2 = (bf16[1024,480]{0,1:T(8,128)(2,1)S(1)}, bf16[1024,480]{0,1:T(8,128)(2,1)}, u32[]{:S(2)}, u32[]{:S(2)}) collective-permute-start(bf16[1024,480]{0,1:T(8,128)(2,1)S(1)} %collective-permute-done), channel_id=1, source_target_pairs={{1,2},{2,3},{5,6},{6,7},{9,10},{10,11},{13,14},{14,15},{17,18},{18... | collective-permute-start | bytes 2949128 | tf_op jit(solution)/shard_map/ppermute | solution.py:125
  37.1 25.6 %collective-permute-start.3 = (bf16[1024,480]{0,1:T(8,128)(2,1)}, bf16[1024,480]{0,1:T(8,128)(2,1)}, u32[]{:S(2)}, u32[]{:S(2)}) collective-permute-start(bf16[1024,480]{0,1:T(8,128)(2,1)} %collective-permute-done.1), channel_id=1, source_target_pairs={{1,0},{2,1},{5,4},{6,5},{9,8},{10,9},{13,12},{14,13},{17,16},{18,1... | collective-permute-start | bytes 2949128 | tf_op jit(solution)/shard_map/ppermute | solution.py:126
  46.0 30.9 %collective-permute-start.4 = (bf16[1024,480]{0,1:T(8,128)(2,1)}, bf16[1024,480]{0,1:T(8,128)(2,1)}, u32[]{:S(2)}, u32[]{:S(2)}) collective-permute-start(bf16[1024,480]{0,1:T(8,128)(2,1)} %collective-permute-done.2), channel_id=1, source_target_pairs={{2,3},{6,7},{10,11},{14,15},{18,19},{22,23},{26,27},{30,31}} | collective-permute-start | bytes 2949128 | tf_op jit(solution)/shard_map/ppermute | solution.py:125
  62.7 32.6 %collective-permute-start.5 = (bf16[1024,480]{0,1:T(8,128)(2,1)}, bf16[1024,480]{0,1:T(8,128)(2,1)}, u32[]{:S(2)}, u32[]{:S(2)}) collective-permute-start(bf16[1024,480]{0,1:T(8,128)(2,1)} %collective-permute-done.3), channel_id=1, source_target_pairs={{1,0},{5,4},{9,8},{13,12},{17,16},{21,20},{25,24},{29,28}} | collective-permute-start | bytes 2949128 | tf_op jit(solution)/shard_map/ppermute | solution.py:126
  70.5 24.8 %slice-start = ((s8[6291456]{0:T(1024)(128)(4,1)}), s8[4194304]{0:T(1024)(128)(4,1)S(1)}, s32[]{:S(2)}) async-start(s8[6291456]{0:T(1024)(128)(4,1)} %bitcast.55), calls=%async_computation.2 | async-start | bytes 8388608
  76.9 18.3 %slice-start.1 = ((s8[6291456]{0:T(1024)(128)(4,1)}), s8[2097152]{0:T(1024)(128)(4,1)S(1)}, s32[]{:S(2)}) async-start(s8[6291456]{0:T(1024)(128)(4,1)} %bitcast.55), calls=%async_computation.3 | async-start | bytes 4194304
  109.6 2.1 collective-permute-start.6
  124.9 26.8 %copy-start.1 = (f32[480,16]{0,1:T(8,128)S(1)}, f32[480,16]{0,1:T(8,128)}, u32[]{:S(2)}) copy-start(f32[480,16]{0,1:T(8,128)} %param.10) | copy-start | bytes 92164
  140.1 9.6 %collective-permute-start.7 = (f32[16,480]{1,0:T(8,128)}, f32[16,480]{1,0:T(8,128)S(1)}, u32[]{:S(2)}, u32[]{:S(2)}) collective-permute-start(f32[16,480]{1,0:T(8,128)} %get-tuple-element.8), channel_id=1, source_target_pairs={{0,4},{4,8},{8,12},{1,5},{5,9},{9,13},{2,6},{6,10},{10,14},{3,7},{... | collective-permute-start | bytes 92168 | tf_op jit(solution)/shard_map/ppermute | solution.py:15
  144.4 6.0 %collective-permute-start.8 = (f32[16,480]{1,0:T(8,128)}, f32[16,480]{1,0:T(8,128)S(1)}, u32[]{:S(2)}, u32[]{:S(2)}) collective-permute-start(f32[16,480]{1,0:T(8,128)} %get-tuple-element.8), channel_id=1, source_target_pairs={{0,8},{4,12},{1,9},{5,13},{2,10},{6,14},{3,11},{7,15},{16,24},{20,... | collective-permute-start | bytes 92168 | tf_op jit(solution)/shard_map/ppermute | solution.py:15
  148.5 3.2 %collective-permute-start.9 = (f32[16,480]{1,0:T(8,128)}, f32[16,480]{1,0:T(8,128)S(1)}, u32[]{:S(2)}, u32[]{:S(2)}) collective-permute-start(f32[16,480]{1,0:T(8,128)} %get-tuple-element.8), channel_id=1, source_target_pairs={{0,12},{1,13},{2,14},{3,15},{16,28},{17,29},{18,30},{19,31}} | collective-permute-start | bytes 92168 | tf_op jit(solution)/shard_map/ppermute | solution.py:15
Sparse Core Ops, SparseCore 0:
  166.1 74.1 reduce-scatter.1

commit v4 on v3

--- a/solution.py
+++ b/solution.py
@@ -103,60 +103,41 @@
     )(conv_local, query, g_tab, a8, state_in)
 
 
-def relay_pairs(size, step, forward):
-    if forward:
-        return [(i, i + 1) for i in range(step - 1, size - 1)]
-    return [(i, i - 1) for i in range(1, size - step + 1)]
-
-
-def gathered_projection(tokens, in_weight):
-    size = lax.axis_size("tensor")
-    me = lax.axis_index("tensor")
-    feats = tokens.shape[1]
-
-    def rows_of(owner):
-        owner = jnp.clip(owner, 0, size - 1)
-        return lax.dynamic_slice_in_dim(in_weight, owner * feats, feats, 0)
-
-    acc = jnp.einsum("td,dkc->tkc", tokens, rows_of(me), preferred_element_type=jnp.float32)
-    fwd = tokens
-    bwd = tokens
-    for step in range(1, size):
-        fwd = lax.ppermute(fwd, "tensor", relay_pairs(size, step, True))
-        bwd = lax.ppermute(bwd, "tensor", relay_pairs(size, step, False))
-        acc = acc + jnp.einsum(
-            "td,dkc->tkc", fwd, rows_of(me - step), preferred_element_type=jnp.float32
-        )
-        acc = acc + jnp.einsum(
-            "td,dkc->tkc", bwd, rows_of(me + step), preferred_element_type=jnp.float32
-        )
-    return acc.astype(jnp.bfloat16)
-
-
 def per_device(tokens, in_weight, short_filter, mode_weight, decay_rate, out_weight):
     tok_rows = tokens.shape[0]
-    channels = in_weight.shape[2]
     rim_rows = TAPS - 1
     lam, g_tab, w_tab, hcol, a8 = chunk_tables(decay_rate, mode_weight)
     taps = short_filter.astype(jnp.float32)
-
-    proj = gathered_projection(tokens, in_weight)
-    rim = shifted(proj[tok_rows - rim_rows :], "context", 1)
-    padded = jnp.concatenate([rim, proj], 0)
-    filtered = jnp.zeros((tok_rows, 3, channels), jnp.float32)
-    for tap_number in range(TAPS):
-        begin = rim_rows - tap_number
-        filtered = filtered + taps[tap_number][None] * padded[begin : begin + tok_rows].astype(
-            jnp.float32
-        )
-    query = filtered[:, 0]
-    drive = filtered[:, 1] * filtered[:, 2]
+    full = lax.all_gather(tokens, "tensor", axis=1, tiled=True)
+    projs = [
+        jnp.dot(full, in_weight[:, k, :], preferred_element_type=jnp.float32).astype(jnp.bfloat16)
+        for k in range(3)
+    ]
+    tails = jnp.stack([p[tok_rows - rim_rows :] for p in projs], 0)
+    rims = shifted(tails, "context", 1)
+    streams = []
+    for k in range(3):
+        padded = jnp.concatenate([rims[k], projs[k]], 0)
+        acc = jnp.zeros(projs[k].shape, jnp.float32)
+        for tap_number in range(TAPS):
+            begin = rim_rows - tap_number
+            acc = acc + taps[tap_number, k][None] * padded[begin : begin + tok_rows].astype(
+                jnp.float32
+            )
+        streams.append(acc)
+    query = streams[0]
+    drive = streams[1] * streams[2]
     conv_local, block_end = local_conv(drive, hcol, w_tab, g_tab, a8)
 
-    state_in = jnp.zeros_like(block_end)
-    for by in range(1, lax.axis_size("context")):
-        earlier = shifted(block_end, "context", by)
-        state_in = state_in + jnp.exp(-lam * (tok_rows * (by - 1))) * earlier
+    ends = lax.all_gather(block_end, "context", axis=0, tiled=False)
+    me = lax.axis_index("context")
+    gap = (me - 1 - jnp.arange(ends.shape[0])).astype(jnp.float32)
+    factor = jnp.where(
+        (gap >= 0.0)[:, None, None],
+        jnp.exp(-lam[None] * (tok_rows * jnp.maximum(gap, 0.0))[:, None, None]),
+        0.0,
+    )
+    state_in = jnp.sum(factor * ends, axis=0)
 
     gated = gate(conv_local, query, g_tab, a8, state_in).astype(jnp.bfloat16)
     partial_sums = jnp.dot(gated, out_weight, preferred_element_type=jnp.float32)

time: 248 us -> 225 us (0.907)
  waiting for transfers between devices: 101 us -> 149 us
  matrix products: 58.6 us -> 18.7 us
  starting transfers between devices: 23.5 us -> 1.63 us
  other arithmetic: 21.2 us -> 12.3 us
  local copies, waits for them, and re-layouts: 9.04 us -> 0.8 us
  blocking collectives: 0 us -> 8.11 us
    all_gather x0 -> x1, waiting for transfers between devices: none -> 76 us  [per_device(): full = lax.all_gather(tokens, 'tensor', axis=1, tiled=True)]
    dot_general x7 -> x3, matrix products: 52.9 us -> 13 us  [per_device(): jnp.dot(full, in_weight[:, k, :], preferred_element_type=jnp.float32)]
    ppermute x6 -> x0, waiting for transfers between devices: 24 us -> none  [the longest x3 16.6 us: gathered_projection(): bwd = lax.ppermute(bwd, 'tensor', relay_pairs(size, step, False))]
    ppermute x6 -> x0, starting transfers between devices: 12.4 us -> none  [the longest x3 8.35 us: gathered_projection(): fwd = lax.ppermute(fwd, 'tensor', relay_pairs(size, step, True))]
    add x2 -> x1, other arithmetic: 13.8 us -> 2.93 us  [per_device(): acc + taps[tap_number, k][None] * padded[begin:begin + tok_rows].astype(j...]
    ppermute x4 -> x1, starting transfers between devices: 11.1 us -> 1.59 us  [shifted(): return lax.ppermute(array, axis, pairs)]
    all_gather x0 -> x1, blocking collectives: none -> 8.11 us  [per_device(): ends = lax.all_gather(block_end, 'context', axis=0, tiled=False)]
    add x1 -> x0, local copies, waits for them, and re-layouts: 6.5 us -> none  [gathered_projection(): acc + jnp.einsum('td,dkc->tkc', fwd, rows_of(me - step), preferred_elemen...]
  transfers between devices with their start and end apart: 11 -> 3, of which waited for: 8 -> 3; matrix products, arithmetic and copies ran while one was open for 21% -> 2% of each run, Pallas kernels for 0% -> 0%
where the time goes in v4:
time: 225 us
  waiting for transfers between devices  149 us (66%)
  Pallas kernels  20.4 us (9%)
  matrix products  18.7 us (8%)
  between operations  13.5 us (6%)
  other arithmetic  12.3 us (5%)
  blocking collectives  8.11 us (4%)
    all_gather x1, waiting for transfers between devices, per_device(): full = lax.all_gather(tokens, 'tensor', axis=1, tiled=True)  76 us
    reduce_scatter x1, waiting for transfers between devices, per_device(): lax.psum_scatter(partial_sums.astype(jnp.bfloat16), 'tensor', scatter_dim...  71.7 us
    dot_general x3, matrix products, per_device(): jnp.dot(full, in_weight[:, k, :], preferred_element_type=jnp.float32)  13 us
    pallas_call x1, Pallas kernels, local_conv(): pl.pallas_call(local_kernel, out_shape=(jax.ShapeDtypeStruct((rows, chann...  12.5 us
    all_gather x1, blocking collectives, per_device(): ends = lax.all_gather(block_end, 'context', axis=0, tiled=False)  8.11 us
    pallas_call x1, Pallas kernels, gate(): pl.pallas_call(gate_kernel, out_shape=jax.ShapeDtypeStruct((rows, channel...  7.89 us
    dot_general x1, matrix products, per_device(): jnp.dot(gated, out_weight, preferred_element_type=jnp.float32)  5.71 us
    mul x1, other arithmetic, per_device(): drive = streams[1] * streams[2]  4.75 us
  transfers between devices with their start and end apart: 3, of which 3 were waited for; matrix products, arithmetic and copies ran while one was open for 2% of the time, Pallas kernels for 0%

profile of v4, /device:TPU:0, one launch (start us, length us, event | category | flops | bytes accessed | tf_op | source)
XLA Modules:
  0.0 224.8 jit_solution(13837235614790392617)
XLA Ops:
  6.5 0.0 copy-start
  6.5 0.0 all-gather.3.cloned.1.call-start
  6.5 0.7 all-gather.3.cloned.1.call-update
  7.3 0.0 reduce-scatter.2.cloned.1.call-start
  7.3 0.1 compare_select_fusion
  7.4 0.1 reshape.140
  7.5 0.8 multiply_bitcast_fusion
  8.3 0.8 exponential_multiply_fusion
  9.1 0.7 gather_fusion
  9.8 0.1 subtract_compare_fusion
  9.9 0.0 copy-done.2
  9.9 0.0 copy-done.1
  9.9 0.6 multiply_exponential_fusion.1.a8_ref
  10.5 0.7 bitcast_select_fusion.hcol_ref
  11.3 0.8 multiply_exponential_fusion.w_ref
  12.1 76.0 %all-gather.3.cloned.1.call-done = bf16[1024,1920]{0,1:T(8,128)(2,1)} async-done(((bf16[1024,480]{0,1:T(8,128)(2,1)}), bf16[1024,1920]{0,1:T(8,128)(2,1)}) %all-gather.3.cloned.1.call-update) | async-done | bytes 3932176 | tf_op jit(solution)/shard_map/all_gather | solution.py:111
  88.1 5.2 %fusion.12 = bf16[1024,480]{1,0:T(8,128)(2,1)S(1)} fusion(bf16[1024,1920]{0,1:T(8,128)(2,1)} %all-gather.3.cloned.1.call-done, bf16[1920,3,480]{0,2,1:T(8,128)(2,1)} %param.7), kind=kOutput, calls=%fused_computation.29 | convolution fusion | flops 1887928320 | bytes 6758400 | tf_op jit(solution)/shard_map/dot_general | solution.py:113
  93.3 0.0 copy-done.3
  93.3 3.9 %fusion.15 = bf16[1024,480]{1,0:T(8,128)(2,1)S(1)} fusion(bf16[1024,1920]{0,1:T(8,128)(2,1)S(1)} %copy-done.3, bf16[1920,3,480]{0,2,1:T(8,128)(2,1)} %param.7), kind=kOutput, calls=%fused_computation.30 | convolution fusion | flops 1887928320 | bytes 6758400 | tf_op jit(solution)/shard_map/dot_general | solution.py:113
  97.2 3.9 %fusion.9 = bf16[1024,480]{1,0:T(8,128)(2,1)S(1)} fusion(bf16[1024,1920]{0,1:T(8,128)(2,1)S(1)} %copy-done.3, bf16[1920,3,480]{0,2,1:T(8,128)(2,1)} %param.7), kind=kOutput, calls=%fused_computation.28 | convolution fusion | flops 1887928320 | bytes 6758400 | tf_op jit(solution)/shard_map/dot_general | solution.py:113
  101.2 1.6 collective-permute-start
  102.8 0.8 collective-permute-done
  103.6 4.7 %add_multiply_fusion.d_ref = f32[1024,480]{1,0:T(8,128)} fusion(bf16[1024,480]{1,0:T(8,128)(2,1)S(1)} %fusion.15, bf16[1024,480]{1,0:T(8,128)(2,1)S(1)} %fusion.9, bf16[6,480]{1,0:T(8,128)(2,1)S(1)} %get-tuple-element.33, bf16[6,480]{1,0:T(8,128)(2,1)S(1)} %get-tuple-element.34, f32[480]{0:T(512)S(1)} %bitcast.77, f32[480]{0:T(512)S(1)} %bitcast.76, ...), kind=kLoop, calls=%fused_computation.18 | loop fusion | flops 37847040 | bytes 3970560 | tf_op jit(solution)/shard_map/mul | solution.py:129
  108.4 12.5 %shard_map.64 = (f32[1024,480]{1,0:T(8,128)}, f32[16,480]{1,0:T(8,128)}) custom-call(f32[1024,480]{1,0:T(8,128)} %add_multiply_fusion.d_ref, f32[8,8,480]{2,1,0:T(8,128)} %bitcast_select_fusion.hcol_ref, f32[8,16,480]{2,1,0:T(8,128)} %multiply_exponential_fusion.w_ref, f32[16,8,480]{2,1,0:T(8,128)} %get-tuple-element.9.g_ref, ...), custom_call_target="tpu_custom_call" | custom-call | tf_op jit(solution)/shard_map/pallas_call | solution.py:82
  120.9 8.1 %all-gather = f32[64,480]{1,0:T(8,128)S(1)} all-gather(f32[16,480]{1,0:T(8,128)} %get-tuple-element.8), channel_id=2, replica_groups=mesh['groups'=2,'context'=4,'tensor'=4] {'context'}, dimensions={0}, use_global_device_ids=true | all-gather | bytes 153600 | tf_op jit(solution)/shard_map/all_gather | solution.py:132
  129.0 0.7 multiply_reduce_fusion.sin_ref
  129.7 2.9 %multiply_add_fusion.q_ref = f32[1024,480]{1,0:T(8,128)} fusion(bf16[1024,480]{1,0:T(8,128)(2,1)S(1)} %fusion.12, bf16[6,480]{1,0:T(8,128)(2,1)S(1)} %get-tuple-element.32, f32[480]{0:T(512)S(1)} %bitcast.84, f32[480]{0:T(512)S(1)} %bitcast.83, f32[480]{0:T(512)S(1)} %bitcast.82, f32[480]{0:T(512)S(1)} %bitcast.81, f32[480]{0:T(512)S(1)} %bitcast.80, ...), kind=kLoop, calls=%fused_computation.17 | loop fusion | flops 18677760 | bytes 2968320 | tf_op jit(solution)/shard_map/add | solution.py:124
  132.7 7.9 %shard_map.65 = f32[1024,480]{1,0:T(8,128)} custom-call(f32[1024,480]{1,0:T(8,128)} %get-tuple-element.7.conv_ref, f32[1024,480]{1,0:T(8,128)} %multiply_add_fusion.q_ref, f32[16,8,480]{2,1,0:T(8,128)} %get-tuple-element.9.g_ref, f32[16,480]{1,0:T(8,128)} %multiply_exponential_fusion.1.a8_ref, f32[16,480]{1,0:T(8,128)} %multiply_reduce_fusion.sin_ref), custom_call_target="tpu_custom_call" | custom-call | tf_op jit(solution)/shard_map/pallas_call | solution.py:97
  140.5 0.0 copy-done
  140.5 5.7 %convolution_convert_fusion = bf16[1024,1920]{0,1:T(8,128)(2,1)} fusion(bf16[480,1920]{1,0:T(8,128)(2,1)S(1)} %copy-done, f32[1024,480]{1,0:T(8,128)} %shard_map.65), kind=kOutput, calls=%fused_computation.1 | convolution fusion | flops 1889894400 | bytes 7741440 | tf_op jit(solution)/shard_map/dot_general | solution.py:143
  146.3 0.0 reduce-scatter.2.cloned.1.call-update
  146.3 71.7 %reduce-scatter.2.cloned.1.call-done = bf16[1024,480]{0,1:T(8,128)(2,1)} async-done(((bf16[1024,1920]{0,1:T(8,128)(2,1)}), bf16[1024,480]{0,1:T(8,128)(2,1)}) %reduce-scatter.2.cloned.1.call-update) | async-done | bytes 983056 | tf_op jit(solution)/shard_map/reduce_scatter | solution.py:144
  (14 shorter events, 0.1 us)
Async XLA Ops:
  6.5 134.0 %copy-start = (bf16[480,1920]{1,0:T(8,128)(2,1)S(1)}, bf16[480,1920]{1,0:T(8,128)(2,1)}, u32[]{:S(2)}) copy-start(bf16[480,1920]{1,0:T(8,128)(2,1)} %param.11) | copy-start | bytes 5529604
  6.5 3.4 %copy-start.1 = (f32[480,16]{0,1:T(8,128)S(1)}, f32[480,16]{0,1:T(8,128)}, u32[]{:S(2)}) copy-start(f32[480,16]{0,1:T(8,128)} %param.10) | copy-start | bytes 92164
  6.5 3.3 %copy-start.2 = (bf16[7,3,480]{2,0,1:T(8,128)(2,1)S(1)}, bf16[7,3,480]{2,0,1:T(8,128)(2,1)}, u32[]{:S(2)}) copy-start(bf16[7,3,480]{2,0,1:T(8,128)(2,1)} %param.8) | copy-start | bytes 60484
  6.5 81.5 %all-gather.3.cloned.1.call-start = ((), (), s32[]{:S(2)}) async-start(), calls=%async_computation.1 | async-start | bytes 4915200 | tf_op jit(solution)/shard_map/all_gather | solution.py:111
  7.3 210.7 %reduce-scatter.2.cloned.1.call-start = ((), (), s32[]{:S(2)}) async-start(), calls=%async_computation.2 | async-start | bytes 4915200 | tf_op jit(solution)/shard_map/reduce_scatter | solution.py:144
  88.1 5.2 %copy-start.3 = (bf16[1024,1920]{0,1:T(8,128)(2,1)S(1)}, bf16[1024,1920]{0,1:T(8,128)(2,1)}, u32[]{:S(2)}) copy-start(bf16[1024,1920]{0,1:T(8,128)(2,1)} %all-gather.3.cloned.1.call-done) | copy-start | bytes 11796484
  101.2 2.4 %collective-permute-start = (bf16[3,6,480]{2,1,0:T(8,128)(2,1)S(1)}, bf16[3,6,480]{2,1,0:T(8,128)(2,1)S(1)}, u32[]{:S(2)}, u32[]{:S(2)}) collective-permute-start(bf16[3,6,480]{2,1,0:T(8,128)(2,1)S(1)} %pad_maximum_fusion.3), channel_id=1, source_target_pairs={{0,4},{4,8},{8,12},{1,5},{5,9},{9,13},{2,6},{6,10},{10,14},{3,7},{... | collective-permute-start | bytes 51848 | tf_op jit(solution)/shard_map/ppermute | solution.py:15
Sparse Core Ops, SparseCore 0:
  8.9 79.1 all-gather.2
  146.4 71.5 reduce-scatter.1

commit v5 on v1

--- a/solution.py
+++ b/solution.py
@@ -15,32 +15,30 @@
     return lax.ppermute(array, axis, pairs)
 
 
-def local_kernel(d_ref, hcol_ref, w_ref, g_ref, a8_ref, conv_ref, end_ref, s_ref):
+def local_kernel(d_ref, hcol_ref, w_ref, a8_ref, conv_ref, sums_ref, end_ref, s_ref):
     rows = d_ref.shape[0]
     modes = a8_ref.shape[0]
     s_ref[...] = jnp.zeros(s_ref.shape, jnp.float32)
 
     def body(b, carry):
         start = pl.multiple_of(b * CHUNK, CHUNK)
-        state = s_ref[...]
         chunk = d_ref[pl.ds(start, CHUNK), :]
         acc = jnp.zeros(chunk.shape, jnp.float32)
-        for n in range(modes):
-            acc = acc + g_ref[n] * state[n : n + 1, :]
-        new_state = a8_ref[...] * state
+        piece = jnp.zeros(s_ref.shape, jnp.float32)
         for j in range(CHUNK):
             row = chunk[j : j + 1, :]
             acc = acc + hcol_ref[j] * row
-            new_state = new_state + w_ref[j] * row
+            piece = piece + w_ref[j] * row
         conv_ref[pl.ds(start, CHUNK), :] = acc
-        s_ref[...] = new_state
+        sums_ref[pl.ds(pl.multiple_of(b * modes, modes), modes), :] = piece
+        s_ref[...] = a8_ref[...] * s_ref[...] + piece
         return carry
 
     lax.fori_loop(0, rows // CHUNK, body, 0)
     end_ref[...] = s_ref[...]
 
 
-def gate_kernel(conv_ref, q_ref, g_ref, a8_ref, sin_ref, out_ref, s_ref):
+def gate_kernel(conv_ref, q_ref, sums_ref, g_ref, a8_ref, sin_ref, out_ref, s_ref):
     rows = conv_ref.shape[0]
     modes = a8_ref.shape[0]
     s_ref[...] = sin_ref[...]
@@ -52,7 +50,8 @@
         for n in range(modes):
             acc = acc + g_ref[n] * state[n : n + 1, :]
         out_ref[pl.ds(start, CHUNK), :] = q_ref[pl.ds(start, CHUNK), :] * acc
-        s_ref[...] = a8_ref[...] * state
+        piece = sums_ref[pl.ds(pl.multiple_of(b * modes, modes), modes), :]
+        s_ref[...] = a8_ref[...] * state + piece
         return carry
 
     lax.fori_loop(0, rows // CHUNK, body, 0)
@@ -94,16 +93,17 @@
     hcol = jnp.where((lag >= 0)[:, :, None], h_short[lag_index], 0.0)
     a8 = jnp.exp(-lam * CHUNK)
 
-    conv_local, end_state = pl.pallas_call(
+    conv_local, sums, end_state = pl.pallas_call(
         local_kernel,
         out_shape=(
             jax.ShapeDtypeStruct((tok_rows, channels), jnp.float32),
+            jax.ShapeDtypeStruct((tok_rows // CHUNK * modes, channels), jnp.float32),
             jax.ShapeDtypeStruct((modes, channels), jnp.float32),
         ),
-        in_specs=[vmem_spec() for _ in range(5)],
-        out_specs=(vmem_spec(), vmem_spec()),
+        in_specs=[vmem_spec() for _ in range(4)],
+        out_specs=(vmem_spec(), vmem_spec(), vmem_spec()),
         scratch_shapes=[pltpu.VMEM((modes, channels), jnp.float32)],
-    )(drive, hcol, w_tab, g_tab, a8)
+    )(drive, hcol, w_tab, a8)
 
     ends = lax.all_gather(end_state, "context", axis=0, tiled=False)
     block_count = ends.shape[0]
@@ -119,10 +119,10 @@
     gated = pl.pallas_call(
         gate_kernel,
         out_shape=jax.ShapeDtypeStruct((tok_rows, channels), jnp.float32),
-        in_specs=[vmem_spec() for _ in range(5)],
+        in_specs=[vmem_spec() for _ in range(6)],
         out_specs=vmem_spec(),
         scratch_shapes=[pltpu.VMEM((modes, channels), jnp.float32)],
-    )(conv_local, query, g_tab, a8, state_in)
+    )(conv_local, query, sums, g_tab, a8, state_in)
     gated = gated.astype(jnp.bfloat16)
     partial_sums = jnp.dot(gated, out_weight, preferred_element_type=jnp.float32)
     summed = lax.psum_scatter(

time: 223 us -> 222 us (level)
    pallas_call x1, Pallas kernels: 12.5 us -> 9.62 us  [per_device(): pl.pallas_call(local_kernel, out_shape=(jax.ShapeDtypeStruct((tok_rows, c...]
where the time goes in v5:
time: 222 us; the launch traced here: 221 us
  waiting for transfers between devices  147 us (66%)
  Pallas kernels  19 us (9%)
  matrix products  15.8 us (7%)
  other arithmetic  15 us (7%)
  between operations  13.5 us (6%)
  blocking collectives  7.93 us (4%)
    all_gather x1, waiting for transfers between devices, per_device(): lax.all_gather(tokens, 'tensor', axis=1, tiled=True)  74.2 us
    reduce_scatter x1, waiting for transfers between devices, per_device(): lax.psum_scatter(partial_sums.astype(jnp.bfloat16), 'tensor', scatter_dim...  71.7 us
    dot_general x1, matrix products, per_device(): jnp.einsum('td,dkc->tkc', lax.all_gather(tokens, 'tensor', axis=1, tiled=...  10.1 us
    pallas_call x1, Pallas kernels, per_device(): pl.pallas_call(local_kernel, out_shape=(jax.ShapeDtypeStruct((tok_rows, c...  9.62 us
    pallas_call x1, Pallas kernels, per_device(): pl.pallas_call(gate_kernel, out_shape=jax.ShapeDtypeStruct((tok_rows, cha...  9.41 us
    all_gather x1, blocking collectives, per_device(): ends = lax.all_gather(end_state, 'context', axis=0, tiled=False)  7.93 us
    add x1, other arithmetic, per_device(): filtered + short_filter[tap_number].astype(jnp.float32)[None] * padded[be...  5.82 us
    dot_general x1, matrix products, per_device(): jnp.dot(gated, out_weight, preferred_element_type=jnp.float32)  5.72 us
  transfers between devices with their start and end apart: 3, of which 3 were waited for; matrix products, arithmetic and copies ran while one was open for 3% of the time, Pallas kernels for 0%

profile of v5, /device:TPU:0, one launch (start us, length us, event | category | flops | bytes accessed | tf_op | source)
XLA Modules:
  0.0 221.2 jit_solution(16263919544549561980)
XLA Ops:
  6.5 0.0 copy-start
  6.5 0.0 all-gather.3.cloned.1.call-start
  6.5 0.7 all-gather.3.cloned.1.call-update
  7.3 0.0 reduce-scatter.2.cloned.1.call-start
  7.3 0.1 compare_select_fusion
  7.4 0.1 reshape.127
  7.5 0.8 multiply_bitcast_fusion
  8.3 0.8 exponential_multiply_fusion
  9.1 0.7 gather_fusion
  9.8 0.1 subtract_compare_fusion
  9.9 1.0 slice_convert_fusion.6
  10.9 1.4 multiply_exponential_fusion.1.a8_ref
  12.3 0.7 bitcast_select_fusion.hcol_ref
  13.0 0.8 multiply_exponential_fusion.w_ref
  13.9 74.2 %all-gather.3.cloned.1.call-done = bf16[1024,1920]{0,1:T(8,128)(2,1)} async-done(((bf16[1024,480]{0,1:T(8,128)(2,1)}), bf16[1024,1920]{0,1:T(8,128)(2,1)}) %all-gather.3.cloned.1.call-update) | async-done | bytes 3932176 | tf_op jit(solution)/shard_map/all_gather | solution.py:70
  88.1 10.1 %fusion.7 = bf16[1024,3,480]{2,0,1:T(8,128)(2,1)S(1)} fusion(bf16[1920,3,480]{0,2,1:T(8,128)(2,1)} %param.7, bf16[1024,1920]{0,1:T(8,128)(2,1)} %all-gather.3.cloned.1.call-done), kind=kOutput, calls=%fused_computation.19 | convolution fusion | flops 5663784960 | bytes 12410880 | tf_op jit(solution)/shard_map/td,dkc->tkc/dot_general | solution.py:68
  98.2 1.6 collective-permute-start
  99.8 0.8 collective-permute-done
  100.6 5.8 %multiply_add_fusion = f32[1024,3,480]{2,0,1:T(8,128)S(1)} fusion(bf16[1024,3,480]{2,0,1:T(8,128)(2,1)S(1)} %fusion.7, bf16[6,3,480]{2,0,1:T(8,128)(2,1)S(1)} %collective-permute-done, f32[3,480]{1,0:T(4,128)S(1)} %get-tuple-element.24, f32[3,480]{1,0:T(4,128)S(1)} %get-tuple-element.25, f32[3,480]{1,0:T(4,128)S(1)} %get-tuple-element.26, ...), kind=kLoop, calls=%fused_computation.6 | loop fusion | flops 56033280 | bytes 8904960 | tf_op jit(solution)/shard_map/add | solution.py:79
  106.4 2.8 %slice_bitcast_fusion = (f32[1024,480]{1,0:T(8,128)}, f32[1024,480]{1,0:T(8,128)}) fusion(f32[1024,3,480]{2,0,1:T(8,128)S(1)} %multiply_add_fusion), kind=kLoop, calls=%fused_computation.20 | loop fusion | flops 491520 | bytes 9830400 | tf_op jit(solution)/shard_map/squeeze | solution.py:82
  109.2 9.6 %shard_map.64 = (f32[1024,480]{1,0:T(8,128)}, f32[2048,480]{1,0:T(8,128)}, f32[16,480]{1,0:T(8,128)}) custom-call(f32[1024,480]{1,0:T(8,128)} %get-tuple-element.12.d_ref, f32[8,8,480]{2,1,0:T(8,128)} %bitcast_select_fusion.hcol_ref, f32[8,16,480]{2,1,0:T(8,128)} %multiply_exponential_fusion.w_ref, f32[16,480]{1,0:T(8,128)} %multiply_exponential_fusion.1.a8_ref), custom_call_target="tpu_custom_call" | custom-call | tf_op jit(solution)/shard_map/pallas_call | solution.py:96
  118.8 7.9 %all-gather = f32[64,480]{1,0:T(8,128)S(1)} all-gather(f32[16,480]{1,0:T(8,128)} %get-tuple-element.10), channel_id=2, replica_groups=mesh['groups'=2,'context'=4,'tensor'=4] {'context'}, dimensions={0}, use_global_device_ids=true | all-gather | bytes 153600 | tf_op jit(solution)/shard_map/all_gather | solution.py:108
  126.8 0.7 multiply_reduce_fusion.sin_ref
  127.5 9.4 %shard_map.65 = f32[1024,480]{1,0:T(8,128)} custom-call(f32[1024,480]{1,0:T(8,128)} %get-tuple-element.8.conv_ref, f32[1024,480]{1,0:T(8,128)} %get-tuple-element.11.q_ref, f32[2048,480]{1,0:T(8,128)} %get-tuple-element.9.sums_ref, f32[16,8,480]{2,1,0:T(8,128)} %get-tuple-element.13.g_ref, f32[16,480]{1,0:T(8,128)} %multiply_exponential_fusion.1.a8_ref, ...), custom_call_target="tpu_custom_call" | custom-call | tf_op jit(solution)/shard_map/pallas_call | solution.py:119
  136.9 0.0 copy-done
  136.9 5.7 %convolution_convert_fusion = bf16[1024,1920]{0,1:T(8,128)(2,1)} fusion(bf16[480,1920]{1,0:T(8,128)(2,1)S(1)} %copy-done, f32[1024,480]{1,0:T(8,128)} %shard_map.65), kind=kOutput, calls=%fused_computation.9 | convolution fusion | flops 1889894400 | bytes 7741440 | tf_op jit(solution)/shard_map/dot_general | solution.py:127
  142.6 0.0 reduce-scatter.2.cloned.1.call-update
  142.6 71.7 %reduce-scatter.2.cloned.1.call-done = bf16[1024,480]{0,1:T(8,128)(2,1)} async-done(((bf16[1024,1920]{0,1:T(8,128)(2,1)}), bf16[1024,480]{0,1:T(8,128)(2,1)}) %reduce-scatter.2.cloned.1.call-update) | async-done | bytes 983056 | tf_op jit(solution)/shard_map/reduce_scatter | solution.py:128
  (10 shorter events, 0.1 us)
Async XLA Ops:
  6.5 130.3 %copy-start = (bf16[480,1920]{1,0:T(8,128)(2,1)S(1)}, bf16[480,1920]{1,0:T(8,128)(2,1)}, u32[]{:S(2)}) copy-start(bf16[480,1920]{1,0:T(8,128)(2,1)} %param.11) | copy-start | bytes 5529604
  6.5 81.5 %all-gather.3.cloned.1.call-start = ((), (), s32[]{:S(2)}) async-start(), calls=%async_computation.1 | async-start | bytes 4915200 | tf_op jit(solution)/shard_map/all_gather | solution.py:70
  7.3 207.1 %reduce-scatter.2.cloned.1.call-start = ((), (), s32[]{:S(2)}) async-start(), calls=%async_computation.2 | async-start | bytes 4915200 | tf_op jit(solution)/shard_map/reduce_scatter | solution.py:128
  98.2 2.4 %collective-permute-start = (bf16[6,3,480]{2,0,1:T(8,128)(2,1)S(1)}, bf16[6,3,480]{2,0,1:T(8,128)(2,1)S(1)}, u32[]{:S(2)}, u32[]{:S(2)}) collective-permute-start(bf16[6,3,480]{2,0,1:T(8,128)(2,1)S(1)} %slice.70), channel_id=1, source_target_pairs={{0,4},{4,8},{8,12},{1,5},{5,9},{9,13},{2,6},{6,10},{10,14},{3,7},{... | collective-permute-start | bytes 51848 | tf_op jit(solution)/shard_map/ppermute | solution.py:15
Sparse Core Ops, SparseCore 0:
  8.9 79.1 all-gather.2
  142.7 71.5 reduce-scatter.1

commit v6 on v5

--- a/solution.py
+++ b/solution.py
@@ -38,7 +38,7 @@
     end_ref[...] = s_ref[...]
 
 
-def gate_kernel(conv_ref, q_ref, sums_ref, g_ref, a8_ref, sin_ref, out_ref, s_ref):
+def gate_kernel(conv_ref, sums_ref, g_ref, a8_ref, sin_ref, out_ref, s_ref):
     rows = conv_ref.shape[0]
     modes = a8_ref.shape[0]
     s_ref[...] = sin_ref[...]
@@ -49,7 +49,7 @@
         acc = conv_ref[pl.ds(start, CHUNK), :]
         for n in range(modes):
             acc = acc + g_ref[n] * state[n : n + 1, :]
-        out_ref[pl.ds(start, CHUNK), :] = q_ref[pl.ds(start, CHUNK), :] * acc
+        out_ref[pl.ds(start, CHUNK), :] = acc
         piece = sums_ref[pl.ds(pl.multiple_of(b * modes, modes), modes), :]
         s_ref[...] = a8_ref[...] * state + piece
         return carry
@@ -119,11 +119,11 @@
     gated = pl.pallas_call(
         gate_kernel,
         out_shape=jax.ShapeDtypeStruct((tok_rows, channels), jnp.float32),
-        in_specs=[vmem_spec() for _ in range(6)],
+        in_specs=[vmem_spec() for _ in range(5)],
         out_specs=vmem_spec(),
         scratch_shapes=[pltpu.VMEM((modes, channels), jnp.float32)],
-    )(conv_local, query, sums, g_tab, a8, state_in)
-    gated = gated.astype(jnp.bfloat16)
+    )(conv_local, sums, g_tab, a8, state_in)
+    gated = (query * gated).astype(jnp.bfloat16)
     partial_sums = jnp.dot(gated, out_weight, preferred_element_type=jnp.float32)
     summed = lax.psum_scatter(
         partial_sums.astype(jnp.bfloat16), "tensor", scatter_dimension=1, tiled=True

time: 222 us -> 223 us (level)
  local copies, waits for them, and re-layouts: 0.77 us -> 3.42 us
    squeeze x1 -> x0, other arithmetic: 2.79 us -> none  [per_device(): query = filtered[:, 0]]
    unnamed x6 -> x8, local copies, waits for them, and re-layouts: 0.03 us -> 2.68 us
where the time goes in v6:
time: 223 us
  waiting for transfers between devices  147 us (66%)
  Pallas kernels  18.3 us (8%)
  matrix products  16.5 us (7%)
  other arithmetic  14.1 us (6%)
  between operations  13.5 us (6%)
  blocking collectives  7.93 us (4%)
  local copies, waits for them, and re-layouts  3.42 us (2%)
    all_gather x1, waiting for transfers between devices, per_device(): lax.all_gather(tokens, 'tensor', axis=1, tiled=True)  74.2 us
    reduce_scatter x1, waiting for transfers between devices, per_device(): lax.psum_scatter(partial_sums.astype(jnp.bfloat16), 'tensor', scatter_dim...  71.7 us
    dot_general x1, matrix products, per_device(): jnp.einsum('td,dkc->tkc', lax.all_gather(tokens, 'tensor', axis=1, tiled=...  10.1 us
    pallas_call x1, Pallas kernels, per_device(): pl.pallas_call(local_kernel, out_shape=(jax.ShapeDtypeStruct((tok_rows, c...  9.69 us
    pallas_call x1, Pallas kernels, per_device(): pl.pallas_call(gate_kernel, out_shape=jax.ShapeDtypeStruct((tok_rows, cha...  8.6 us
    all_gather x1, blocking collectives, per_device(): ends = lax.all_gather(end_state, 'context', axis=0, tiled=False)  7.93 us
    dot_general x1, matrix products, per_device(): jnp.dot(gated, out_weight, preferred_element_type=jnp.float32)  6.43 us
    add x1, other arithmetic, per_device(): filtered + short_filter[tap_number].astype(jnp.float32)[None] * padded[be...  5.82 us
  transfers between devices with their start and end apart: 3, of which 3 were waited for; matrix products, arithmetic and copies ran while one was open for 3% of the time, Pallas kernels for 0%

profile of v6, /device:TPU:0, one launch (start us, length us, event | category | flops | bytes accessed | tf_op | source)
XLA Modules:
  0.0 222.8 jit_solution(15721771415258490699)
XLA Ops:
  6.5 0.0 copy-start
  6.5 0.0 all-gather.3.cloned.1.call-start
  6.5 0.7 all-gather.3.cloned.1.call-update
  7.3 0.0 reduce-scatter.2.cloned.1.call-start
  7.3 0.1 compare_select_fusion
  7.4 0.1 reshape.127
  7.5 0.8 multiply_bitcast_fusion
  8.3 0.8 exponential_multiply_fusion
  9.1 0.7 gather_fusion
  9.8 0.1 subtract_compare_fusion
  9.9 1.0 slice_convert_fusion.6
  10.9 1.4 multiply_exponential_fusion.1.a8_ref
  12.3 0.7 bitcast_select_fusion.hcol_ref
  13.0 0.8 multiply_exponential_fusion.w_ref
  13.9 74.2 %all-gather.3.cloned.1.call-done = bf16[1024,1920]{0,1:T(8,128)(2,1)} async-done(((bf16[1024,480]{0,1:T(8,128)(2,1)}), bf16[1024,1920]{0,1:T(8,128)(2,1)}) %all-gather.3.cloned.1.call-update) | async-done | bytes 3932176 | tf_op jit(solution)/shard_map/all_gather | solution.py:70
  88.1 10.1 %fusion.7 = bf16[1024,3,480]{2,0,1:T(8,128)(2,1)S(1)} fusion(bf16[1920,3,480]{0,2,1:T(8,128)(2,1)} %param.7, bf16[1024,1920]{0,1:T(8,128)(2,1)} %all-gather.3.cloned.1.call-done), kind=kOutput, calls=%fused_computation.19 | convolution fusion | flops 5663784960 | bytes 12410880 | tf_op jit(solution)/shard_map/td,dkc->tkc/dot_general | solution.py:68
  98.2 1.6 collective-permute-start
  99.8 0.8 collective-permute-done
  100.6 5.8 %multiply_add_fusion = f32[1024,3,480]{2,0,1:T(8,128)S(1)} fusion(bf16[1024,3,480]{2,0,1:T(8,128)(2,1)S(1)} %fusion.7, bf16[6,3,480]{2,0,1:T(8,128)(2,1)S(1)} %collective-permute-done, f32[3,480]{1,0:T(4,128)S(1)} %get-tuple-element.22, f32[3,480]{1,0:T(4,128)S(1)} %get-tuple-element.23, f32[3,480]{1,0:T(4,128)S(1)} %get-tuple-element.24, ...), kind=kLoop, calls=%fused_computation.6 | loop fusion | flops 56033280 | bytes 8904960 | tf_op jit(solution)/shard_map/add | solution.py:79
  106.4 0.0 copy-start.1
  106.4 2.6 %copy-done.1 = f32[1024,3,480]{2,0,1:T(8,128)} copy-done((f32[1024,3,480]{2,0,1:T(8,128)}, f32[1024,3,480]{2,0,1:T(8,128)S(1)}, u32[]{:S(2)}) %copy-start.1) | copy-done | bytes 5898264
  109.1 1.8 fusion.10.d_ref
  110.9 9.7 %shard_map.64 = (f32[1024,480]{1,0:T(8,128)}, f32[2048,480]{1,0:T(8,128)}, f32[16,480]{1,0:T(8,128)}) custom-call(f32[1024,480]{1,0:T(8,128)} %fusion.10.d_ref, f32[8,8,480]{2,1,0:T(8,128)} %bitcast_select_fusion.hcol_ref, f32[8,16,480]{2,1,0:T(8,128)} %multiply_exponential_fusion.w_ref, f32[16,480]{1,0:T(8,128)} %multiply_exponential_fusion.1.a8_ref), custom_call_target="tpu_custom_call" | custom-call | tf_op jit(solution)/shard_map/pallas_call | solution.py:96
  120.6 7.9 %all-gather = f32[64,480]{1,0:T(8,128)S(1)} all-gather(f32[16,480]{1,0:T(8,128)} %get-tuple-element.10), channel_id=2, replica_groups=mesh['groups'=2,'context'=4,'tensor'=4] {'context'}, dimensions={0}, use_global_device_ids=true | all-gather | bytes 153600 | tf_op jit(solution)/shard_map/all_gather | solution.py:108
  128.5 0.7 multiply_reduce_fusion.sin_ref
  129.2 8.6 %shard_map.65 = f32[1024,480]{1,0:T(8,128)} custom-call(f32[1024,480]{1,0:T(8,128)} %get-tuple-element.8.conv_ref, f32[2048,480]{1,0:T(8,128)} %get-tuple-element.9.sums_ref, f32[16,8,480]{2,1,0:T(8,128)} %get-tuple-element.11.g_ref, f32[16,480]{1,0:T(8,128)} %multiply_exponential_fusion.1.a8_ref, f32[16,480]{1,0:T(8,128)} %multiply_reduce_fusion.sin_ref), custom_call_target="tpu_custom_call" | custom-call | tf_op jit(solution)/shard_map/pallas_call | solution.py:119
  137.8 0.0 copy-done
  137.8 6.4 %convolution_convert_fusion = bf16[1024,1920]{0,1:T(8,128)(2,1)} fusion(bf16[480,1920]{1,0:T(8,128)(2,1)S(1)} %copy-done, f32[1024,480]{1,0:T(8,128)} %shard_map.65, f32[1024,3,480]{2,0,1:T(8,128)} %copy-done.1), kind=kOutput, calls=%fused_computation.9 | convolution fusion | flops 1890385920 | bytes 9969664 | tf_op jit(solution)/shard_map/dot_general | solution.py:127
  144.2 0.0 reduce-scatter.2.cloned.1.call-update
  144.3 71.7 %reduce-scatter.2.cloned.1.call-done = bf16[1024,480]{0,1:T(8,128)(2,1)} async-done(((bf16[1024,1920]{0,1:T(8,128)(2,1)}), bf16[1024,480]{0,1:T(8,128)(2,1)}) %reduce-scatter.2.cloned.1.call-update) | async-done | bytes 983056 | tf_op jit(solution)/shard_map/reduce_scatter | solution.py:128
  (10 shorter events, 0.1 us)
Async XLA Ops:
  6.5 131.3 %copy-start = (bf16[480,1920]{1,0:T(8,128)(2,1)S(1)}, bf16[480,1920]{1,0:T(8,128)(2,1)}, u32[]{:S(2)}) copy-start(bf16[480,1920]{1,0:T(8,128)(2,1)} %param.11) | copy-start | bytes 5529604
  6.5 81.5 %all-gather.3.cloned.1.call-start = ((), (), s32[]{:S(2)}) async-start(), calls=%async_computation.1 | async-start | bytes 4915200 | tf_op jit(solution)/shard_map/all_gather | solution.py:70
  7.3 208.7 %reduce-scatter.2.cloned.1.call-start = ((), (), s32[]{:S(2)}) async-start(), calls=%async_computation.2 | async-start | bytes 4915200 | tf_op jit(solution)/shard_map/reduce_scatter | solution.py:128
  98.2 2.4 %collective-permute-start = (bf16[6,3,480]{2,0,1:T(8,128)(2,1)S(1)}, bf16[6,3,480]{2,0,1:T(8,128)(2,1)S(1)}, u32[]{:S(2)}, u32[]{:S(2)}) collective-permute-start(bf16[6,3,480]{2,0,1:T(8,128)(2,1)S(1)} %slice.70), channel_id=1, source_target_pairs={{0,4},{4,8},{8,12},{1,5},{5,9},{9,13},{2,6},{6,10},{10,14},{3,7},{... | collective-permute-start | bytes 51848 | tf_op jit(solution)/shard_map/ppermute | solution.py:15
  106.4 2.7 %copy-start.1 = (f32[1024,3,480]{2,0,1:T(8,128)}, f32[1024,3,480]{2,0,1:T(8,128)S(1)}, u32[]{:S(2)}) copy-start(f32[1024,3,480]{2,0,1:T(8,128)S(1)} %multiply_add_fusion) | copy-start | bytes 17694724
Sparse Core Ops, SparseCore 0:
  8.9 79.1 all-gather.2
  144.4 71.5 reduce-scatter.1

commit v7 on v5

--- a/solution.py
+++ b/solution.py
@@ -21,20 +21,27 @@
     s_ref[...] = jnp.zeros(s_ref.shape, jnp.float32)
 
     def body(b, carry):
-        start = pl.multiple_of(b * CHUNK, CHUNK)
-        chunk = d_ref[pl.ds(start, CHUNK), :]
-        acc = jnp.zeros(chunk.shape, jnp.float32)
-        piece = jnp.zeros(s_ref.shape, jnp.float32)
+        start = pl.multiple_of(b * (2 * CHUNK), 2 * CHUNK)
+        pair = d_ref[pl.ds(start, 2 * CHUNK), :]
+        halves = (pair[:CHUNK], pair[CHUNK:])
+        accs = [jnp.zeros(halves[0].shape, jnp.float32) for _ in range(2)]
+        pieces = [jnp.zeros(s_ref.shape, jnp.float32) for _ in range(2)]
         for j in range(CHUNK):
-            row = chunk[j : j + 1, :]
-            acc = acc + hcol_ref[j] * row
-            piece = piece + w_ref[j] * row
-        conv_ref[pl.ds(start, CHUNK), :] = acc
-        sums_ref[pl.ds(pl.multiple_of(b * modes, modes), modes), :] = piece
-        s_ref[...] = a8_ref[...] * s_ref[...] + piece
+            hj = hcol_ref[j]
+            wj = w_ref[j]
+            for h in range(2):
+                row = halves[h][j : j + 1, :]
+                accs[h] = accs[h] + hj * row
+                pieces[h] = pieces[h] + wj * row
+        conv_ref[pl.ds(start, 2 * CHUNK), :] = jnp.concatenate(accs, 0)
+        sums_ref[pl.ds(pl.multiple_of(b * (2 * modes), 2 * modes), 2 * modes), :] = jnp.concatenate(
+            pieces, 0
+        )
+        a8 = a8_ref[...]
+        s_ref[...] = a8 * (a8 * s_ref[...] + pieces[0]) + pieces[1]
         return carry
 
-    lax.fori_loop(0, rows // CHUNK, body, 0)
+    lax.fori_loop(0, rows // (2 * CHUNK), body, 0)
     end_ref[...] = s_ref[...]
 
 
@@ -44,17 +51,24 @@
     s_ref[...] = sin_ref[...]
 
     def body(b, carry):
-        start = pl.multiple_of(b * CHUNK, CHUNK)
-        state = s_ref[...]
-        acc = conv_ref[pl.ds(start, CHUNK), :]
+        start = pl.multiple_of(b * (2 * CHUNK), 2 * CHUNK)
+        a8 = a8_ref[...]
+        first = s_ref[...]
+        pieces = sums_ref[pl.ds(pl.multiple_of(b * (2 * modes), 2 * modes), 2 * modes), :]
+        second = a8 * first + pieces[:modes]
+        pair = conv_ref[pl.ds(start, 2 * CHUNK), :]
+        accs = [pair[:CHUNK], pair[CHUNK:]]
         for n in range(modes):
-            acc = acc + g_ref[n] * state[n : n + 1, :]
-        out_ref[pl.ds(start, CHUNK), :] = q_ref[pl.ds(start, CHUNK), :] * acc
-        piece = sums_ref[pl.ds(pl.multiple_of(b * modes, modes), modes), :]
-        s_ref[...] = a8_ref[...] * state + piece
+            gn = g_ref[n]
+            accs[0] = accs[0] + gn * first[n : n + 1, :]
+            accs[1] = accs[1] + gn * second[n : n + 1, :]
+        out_ref[pl.ds(start, 2 * CHUNK), :] = q_ref[pl.ds(start, 2 * CHUNK), :] * jnp.concatenate(
+            accs, 0
+        )
+        s_ref[...] = a8 * second + pieces[modes:]
         return carry
 
-    lax.fori_loop(0, rows // CHUNK, body, 0)
+    lax.fori_loop(0, rows // (2 * CHUNK), body, 0)
 
 
 def vmem_spec():

time: 222 us -> 221 us (level)
  no operation moved by 1% of the time
where the time goes in v7:
time: 221 us
  waiting for transfers between devices  147 us (67%)
  Pallas kernels  18.7 us (8%)
  matrix products  15.8 us (7%)
  other arithmetic  15 us (7%)
  between operations  13.5 us (6%)
  blocking collectives  7.93 us (4%)
    all_gather x1, waiting for transfers between devices, per_device(): lax.all_gather(tokens, 'tensor', axis=1, tiled=True)  74.2 us
    reduce_scatter x1, waiting for transfers between devices, per_device(): lax.psum_scatter(partial_sums.astype(jnp.bfloat16), 'tensor', scatter_dim...  71.7 us
    dot_general x1, matrix products, per_device(): jnp.einsum('td,dkc->tkc', lax.all_gather(tokens, 'tensor', axis=1, tiled=...  10.1 us
    pallas_call x1, Pallas kernels, per_device(): pl.pallas_call(gate_kernel, out_shape=jax.ShapeDtypeStruct((tok_rows, cha...  9.48 us
    pallas_call x1, Pallas kernels, per_device(): pl.pallas_call(local_kernel, out_shape=(jax.ShapeDtypeStruct((tok_rows, c...  9.19 us
    all_gather x1, blocking collectives, per_device(): ends = lax.all_gather(end_state, 'context', axis=0, tiled=False)  7.93 us
    add x1, other arithmetic, per_device(): filtered + short_filter[tap_number].astype(jnp.float32)[None] * padded[be...  5.82 us
    dot_general x1, matrix products, per_device(): jnp.dot(gated, out_weight, preferred_element_type=jnp.float32)  5.72 us
  transfers between devices with their start and end apart: 3, of which 3 were waited for; matrix products, arithmetic and copies ran while one was open for 3% of the time, Pallas kernels for 0%

profile of v7, /device:TPU:0, one launch (start us, length us, event | category | flops | bytes accessed | tf_op | source)
XLA Modules:
  0.0 220.8 jit_solution(1718732867510427467)
XLA Ops:
  6.5 0.0 copy-start
  6.5 0.0 all-gather.3.cloned.1.call-start
  6.5 0.7 all-gather.3.cloned.1.call-update
  7.3 0.0 reduce-scatter.2.cloned.1.call-start
  7.3 0.1 compare_select_fusion
  7.4 0.1 reshape.127
  7.5 0.8 multiply_bitcast_fusion
  8.3 0.8 exponential_multiply_fusion
  9.1 0.7 gather_fusion
  9.8 0.1 subtract_compare_fusion
  9.9 1.0 slice_convert_fusion.6
  10.9 1.4 multiply_exponential_fusion.1.a8_ref
  12.3 0.7 bitcast_select_fusion.hcol_ref
  13.0 0.8 multiply_exponential_fusion.w_ref
  13.9 74.2 %all-gather.3.cloned.1.call-done = bf16[1024,1920]{0,1:T(8,128)(2,1)} async-done(((bf16[1024,480]{0,1:T(8,128)(2,1)}), bf16[1024,1920]{0,1:T(8,128)(2,1)}) %all-gather.3.cloned.1.call-update) | async-done | bytes 3932176 | tf_op jit(solution)/shard_map/all_gather | solution.py:84
  88.1 10.1 %fusion.7 = bf16[1024,3,480]{2,0,1:T(8,128)(2,1)S(1)} fusion(bf16[1920,3,480]{0,2,1:T(8,128)(2,1)} %param.7, bf16[1024,1920]{0,1:T(8,128)(2,1)} %all-gather.3.cloned.1.call-done), kind=kOutput, calls=%fused_computation.19 | convolution fusion | flops 5663784960 | bytes 12410880 | tf_op jit(solution)/shard_map/td,dkc->tkc/dot_general | solution.py:82
  98.2 1.6 collective-permute-start
  99.8 0.8 collective-permute-done
  100.6 5.8 %multiply_add_fusion = f32[1024,3,480]{2,0,1:T(8,128)S(1)} fusion(bf16[1024,3,480]{2,0,1:T(8,128)(2,1)S(1)} %fusion.7, bf16[6,3,480]{2,0,1:T(8,128)(2,1)S(1)} %collective-permute-done, f32[3,480]{1,0:T(4,128)S(1)} %get-tuple-element.24, f32[3,480]{1,0:T(4,128)S(1)} %get-tuple-element.25, f32[3,480]{1,0:T(4,128)S(1)} %get-tuple-element.26, ...), kind=kLoop, calls=%fused_computation.6 | loop fusion | flops 56033280 | bytes 8904960 | tf_op jit(solution)/shard_map/add | solution.py:93
  106.4 2.8 %slice_bitcast_fusion = (f32[1024,480]{1,0:T(8,128)}, f32[1024,480]{1,0:T(8,128)}) fusion(f32[1024,3,480]{2,0,1:T(8,128)S(1)} %multiply_add_fusion), kind=kLoop, calls=%fused_computation.20 | loop fusion | flops 491520 | bytes 9830400 | tf_op jit(solution)/shard_map/squeeze | solution.py:96
  109.2 9.2 %shard_map.64 = (f32[1024,480]{1,0:T(8,128)}, f32[2048,480]{1,0:T(8,128)}, f32[16,480]{1,0:T(8,128)}) custom-call(f32[1024,480]{1,0:T(8,128)} %get-tuple-element.12.d_ref, f32[8,8,480]{2,1,0:T(8,128)} %bitcast_select_fusion.hcol_ref, f32[8,16,480]{2,1,0:T(8,128)} %multiply_exponential_fusion.w_ref, f32[16,480]{1,0:T(8,128)} %multiply_exponential_fusion.1.a8_ref), custom_call_target="tpu_custom_call" | custom-call | tf_op jit(solution)/shard_map/pallas_call | solution.py:110
  118.4 7.9 %all-gather = f32[64,480]{1,0:T(8,128)S(1)} all-gather(f32[16,480]{1,0:T(8,128)} %get-tuple-element.10), channel_id=2, replica_groups=mesh['groups'=2,'context'=4,'tensor'=4] {'context'}, dimensions={0}, use_global_device_ids=true | all-gather | bytes 153600 | tf_op jit(solution)/shard_map/all_gather | solution.py:122
  126.3 0.7 multiply_reduce_fusion.sin_ref
  127.0 9.5 %shard_map.65 = f32[1024,480]{1,0:T(8,128)} custom-call(f32[1024,480]{1,0:T(8,128)} %get-tuple-element.8.conv_ref, f32[1024,480]{1,0:T(8,128)} %get-tuple-element.11.q_ref, f32[2048,480]{1,0:T(8,128)} %get-tuple-element.9.sums_ref, f32[16,8,480]{2,1,0:T(8,128)} %get-tuple-element.13.g_ref, f32[16,480]{1,0:T(8,128)} %multiply_exponential_fusion.1.a8_ref, ...), custom_call_target="tpu_custom_call" | custom-call | tf_op jit(solution)/shard_map/pallas_call | solution.py:133
  136.5 0.0 copy-done
  136.5 5.7 %convolution_convert_fusion = bf16[1024,1920]{0,1:T(8,128)(2,1)} fusion(bf16[480,1920]{1,0:T(8,128)(2,1)S(1)} %copy-done, f32[1024,480]{1,0:T(8,128)} %shard_map.65), kind=kOutput, calls=%fused_computation.9 | convolution fusion | flops 1889894400 | bytes 7741440 | tf_op jit(solution)/shard_map/dot_general | solution.py:141
  142.2 0.0 reduce-scatter.2.cloned.1.call-update
  142.3 71.7 %reduce-scatter.2.cloned.1.call-done = bf16[1024,480]{0,1:T(8,128)(2,1)} async-done(((bf16[1024,1920]{0,1:T(8,128)(2,1)}), bf16[1024,480]{0,1:T(8,128)(2,1)}) %reduce-scatter.2.cloned.1.call-update) | async-done | bytes 983056 | tf_op jit(solution)/shard_map/reduce_scatter | solution.py:142
  (10 shorter events, 0.1 us)
Async XLA Ops:
  6.5 130.0 %copy-start = (bf16[480,1920]{1,0:T(8,128)(2,1)S(1)}, bf16[480,1920]{1,0:T(8,128)(2,1)}, u32[]{:S(2)}) copy-start(bf16[480,1920]{1,0:T(8,128)(2,1)} %param.11) | copy-start | bytes 5529604
  6.5 81.5 %all-gather.3.cloned.1.call-start = ((), (), s32[]{:S(2)}) async-start(), calls=%async_computation.1 | async-start | bytes 4915200 | tf_op jit(solution)/shard_map/all_gather | solution.py:84
  7.3 206.7 %reduce-scatter.2.cloned.1.call-start = ((), (), s32[]{:S(2)}) async-start(), calls=%async_computation.2 | async-start | bytes 4915200 | tf_op jit(solution)/shard_map/reduce_scatter | solution.py:142
  98.2 2.4 %collective-permute-start = (bf16[6,3,480]{2,0,1:T(8,128)(2,1)S(1)}, bf16[6,3,480]{2,0,1:T(8,128)(2,1)S(1)}, u32[]{:S(2)}, u32[]{:S(2)}) collective-permute-start(bf16[6,3,480]{2,0,1:T(8,128)(2,1)S(1)} %slice.70), channel_id=1, source_target_pairs={{0,4},{4,8},{8,12},{1,5},{5,9},{9,13},{2,6},{6,10},{10,14},{3,7},{... | collective-permute-start | bytes 51848 | tf_op jit(solution)/shard_map/ppermute | solution.py:15
Sparse Core Ops, SparseCore 0:
  8.9 79.1 all-gather.2
  142.4 71.5 reduce-scatter.1

commit v8 on v5

--- a/solution.py
+++ b/solution.py
@@ -34,7 +34,7 @@
         s_ref[...] = a8_ref[...] * s_ref[...] + piece
         return carry
 
-    lax.fori_loop(0, rows // CHUNK, body, 0)
+    lax.fori_loop(0, rows // CHUNK, body, 0, unroll=4)
     end_ref[...] = s_ref[...]
 
 
@@ -54,7 +54,7 @@
         s_ref[...] = a8_ref[...] * state + piece
         return carry
 
-    lax.fori_loop(0, rows // CHUNK, body, 0)
+    lax.fori_loop(0, rows // CHUNK, body, 0, unroll=4)
 
 
 def vmem_spec():

time: 222 us -> 220 us (level)
  no operation moved by 1% of the time
where the time goes in v8:
time: 220 us
  waiting for transfers between devices  147 us (67%)
  Pallas kernels  17.4 us (8%)
  matrix products  15.8 us (7%)
  other arithmetic  15 us (7%)
  between operations  13.5 us (6%)
  blocking collectives  7.93 us (4%)
    all_gather x1, waiting for transfers between devices, per_device(): lax.all_gather(tokens, 'tensor', axis=1, tiled=True)  74.2 us
    reduce_scatter x1, waiting for transfers between devices, per_device(): lax.psum_scatter(partial_sums.astype(jnp.bfloat16), 'tensor', scatter_dim...  71.7 us
    dot_general x1, matrix products, per_device(): jnp.einsum('td,dkc->tkc', lax.all_gather(tokens, 'tensor', axis=1, tiled=...  10.1 us
    pallas_call x1, Pallas kernels, per_device(): pl.pallas_call(gate_kernel, out_shape=jax.ShapeDtypeStruct((tok_rows, cha...  8.87 us
    pallas_call x1, Pallas kernels, per_device(): pl.pallas_call(local_kernel, out_shape=(jax.ShapeDtypeStruct((tok_rows, c...  8.53 us
    all_gather x1, blocking collectives, per_device(): ends = lax.all_gather(end_state, 'context', axis=0, tiled=False)  7.93 us
    add x1, other arithmetic, per_device(): filtered + short_filter[tap_number].astype(jnp.float32)[None] * padded[be...  5.82 us
    dot_general x1, matrix products, per_device(): jnp.dot(gated, out_weight, preferred_element_type=jnp.float32)  5.71 us
  transfers between devices with their start and end apart: 3, of which 3 were waited for; matrix products, arithmetic and copies ran while one was open for 3% of the time, Pallas kernels for 0%

profile of v8, /device:TPU:0, one launch (start us, length us, event | category | flops | bytes accessed | tf_op | source)
XLA Modules:
  0.0 219.6 jit_solution(8644833958962651581)
XLA Ops:
  6.5 0.0 copy-start
  6.5 0.0 all-gather.3.cloned.1.call-start
  6.5 0.7 all-gather.3.cloned.1.call-update
  7.3 0.0 reduce-scatter.2.cloned.1.call-start
  7.3 0.1 compare_select_fusion
  7.4 0.1 reshape.127
  7.5 0.8 multiply_bitcast_fusion
  8.3 0.8 exponential_multiply_fusion
  9.1 0.7 gather_fusion
  9.8 0.1 subtract_compare_fusion
  9.9 1.0 slice_convert_fusion.6
  10.9 1.4 multiply_exponential_fusion.1.a8_ref
  12.3 0.7 bitcast_select_fusion.hcol_ref
  13.0 0.8 multiply_exponential_fusion.w_ref
  13.9 74.2 %all-gather.3.cloned.1.call-done = bf16[1024,1920]{0,1:T(8,128)(2,1)} async-done(((bf16[1024,480]{0,1:T(8,128)(2,1)}), bf16[1024,1920]{0,1:T(8,128)(2,1)}) %all-gather.3.cloned.1.call-update) | async-done | bytes 3932176 | tf_op jit(solution)/shard_map/all_gather | solution.py:70
  88.1 10.1 %fusion.7 = bf16[1024,3,480]{2,0,1:T(8,128)(2,1)S(1)} fusion(bf16[1920,3,480]{0,2,1:T(8,128)(2,1)} %param.7, bf16[1024,1920]{0,1:T(8,128)(2,1)} %all-gather.3.cloned.1.call-done), kind=kOutput, calls=%fused_computation.19 | convolution fusion | flops 5663784960 | bytes 12410880 | tf_op jit(solution)/shard_map/td,dkc->tkc/dot_general | solution.py:68
  98.2 1.6 collective-permute-start
  99.8 0.8 collective-permute-done
  100.6 5.8 %multiply_add_fusion = f32[1024,3,480]{2,0,1:T(8,128)S(1)} fusion(bf16[1024,3,480]{2,0,1:T(8,128)(2,1)S(1)} %fusion.7, bf16[6,3,480]{2,0,1:T(8,128)(2,1)S(1)} %collective-permute-done, f32[3,480]{1,0:T(4,128)S(1)} %get-tuple-element.24, f32[3,480]{1,0:T(4,128)S(1)} %get-tuple-element.25, f32[3,480]{1,0:T(4,128)S(1)} %get-tuple-element.26, ...), kind=kLoop, calls=%fused_computation.6 | loop fusion | flops 56033280 | bytes 8904960 | tf_op jit(solution)/shard_map/add | solution.py:79
  106.4 2.8 %slice_bitcast_fusion = (f32[1024,480]{1,0:T(8,128)}, f32[1024,480]{1,0:T(8,128)}) fusion(f32[1024,3,480]{2,0,1:T(8,128)S(1)} %multiply_add_fusion), kind=kLoop, calls=%fused_computation.20 | loop fusion | flops 491520 | bytes 9830400 | tf_op jit(solution)/shard_map/squeeze | solution.py:82
  109.2 8.5 %shard_map.64 = (f32[1024,480]{1,0:T(8,128)}, f32[2048,480]{1,0:T(8,128)}, f32[16,480]{1,0:T(8,128)}) custom-call(f32[1024,480]{1,0:T(8,128)} %get-tuple-element.12.d_ref, f32[8,8,480]{2,1,0:T(8,128)} %bitcast_select_fusion.hcol_ref, f32[8,16,480]{2,1,0:T(8,128)} %multiply_exponential_fusion.w_ref, f32[16,480]{1,0:T(8,128)} %multiply_exponential_fusion.1.a8_ref), custom_call_target="tpu_custom_call" | custom-call | tf_op jit(solution)/shard_map/pallas_call | solution.py:96
  117.7 7.9 %all-gather = f32[64,480]{1,0:T(8,128)S(1)} all-gather(f32[16,480]{1,0:T(8,128)} %get-tuple-element.10), channel_id=2, replica_groups=mesh['groups'=2,'context'=4,'tensor'=4] {'context'}, dimensions={0}, use_global_device_ids=true | all-gather | bytes 153600 | tf_op jit(solution)/shard_map/all_gather | solution.py:108
  125.7 0.7 multiply_reduce_fusion.sin_ref
  126.4 8.9 %shard_map.65 = f32[1024,480]{1,0:T(8,128)} custom-call(f32[1024,480]{1,0:T(8,128)} %get-tuple-element.8.conv_ref, f32[1024,480]{1,0:T(8,128)} %get-tuple-element.11.q_ref, f32[2048,480]{1,0:T(8,128)} %get-tuple-element.9.sums_ref, f32[16,8,480]{2,1,0:T(8,128)} %get-tuple-element.13.g_ref, f32[16,480]{1,0:T(8,128)} %multiply_exponential_fusion.1.a8_ref, ...), custom_call_target="tpu_custom_call" | custom-call | tf_op jit(solution)/shard_map/pallas_call | solution.py:119
  135.2 0.0 copy-done
  135.2 5.7 %convolution_convert_fusion = bf16[1024,1920]{0,1:T(8,128)(2,1)} fusion(bf16[480,1920]{1,0:T(8,128)(2,1)S(1)} %copy-done, f32[1024,480]{1,0:T(8,128)} %shard_map.65), kind=kOutput, calls=%fused_computation.9 | convolution fusion | flops 1889894400 | bytes 7741440 | tf_op jit(solution)/shard_map/dot_general | solution.py:127
  141.0 0.0 reduce-scatter.2.cloned.1.call-update
  141.0 71.7 %reduce-scatter.2.cloned.1.call-done = bf16[1024,480]{0,1:T(8,128)(2,1)} async-done(((bf16[1024,1920]{0,1:T(8,128)(2,1)}), bf16[1024,480]{0,1:T(8,128)(2,1)}) %reduce-scatter.2.cloned.1.call-update) | async-done | bytes 983056 | tf_op jit(solution)/shard_map/reduce_scatter | solution.py:128
  (10 shorter events, 0.1 us)
Async XLA Ops:
  6.5 128.7 %copy-start = (bf16[480,1920]{1,0:T(8,128)(2,1)S(1)}, bf16[480,1920]{1,0:T(8,128)(2,1)}, u32[]{:S(2)}) copy-start(bf16[480,1920]{1,0:T(8,128)(2,1)} %param.11) | copy-start | bytes 5529604
  6.5 81.5 %all-gather.3.cloned.1.call-start = ((), (), s32[]{:S(2)}) async-start(), calls=%async_computation.1 | async-start | bytes 4915200 | tf_op jit(solution)/shard_map/all_gather | solution.py:70
  7.3 205.5 %reduce-scatter.2.cloned.1.call-start = ((), (), s32[]{:S(2)}) async-start(), calls=%async_computation.2 | async-start | bytes 4915200 | tf_op jit(solution)/shard_map/reduce_scatter | solution.py:128
  98.2 2.4 %collective-permute-start = (bf16[6,3,480]{2,0,1:T(8,128)(2,1)S(1)}, bf16[6,3,480]{2,0,1:T(8,128)(2,1)S(1)}, u32[]{:S(2)}, u32[]{:S(2)}) collective-permute-start(bf16[6,3,480]{2,0,1:T(8,128)(2,1)S(1)} %slice.70), channel_id=1, source_target_pairs={{0,4},{4,8},{8,12},{1,5},{5,9},{9,13},{2,6},{6,10},{10,14},{3,7},{... | collective-permute-start | bytes 51848 | tf_op jit(solution)/shard_map/ppermute | solution.py:15
Sparse Core Ops, SparseCore 0:
  8.9 79.1 all-gather.2
  141.1 71.5 reduce-scatter.1

commit v9 on v8

--- a/solution.py
+++ b/solution.py
@@ -15,10 +15,16 @@
     return lax.ppermute(array, axis, pairs)
 
 
+BLOCK = 128
+
+
 def local_kernel(d_ref, hcol_ref, w_ref, a8_ref, conv_ref, sums_ref, end_ref, s_ref):
     rows = d_ref.shape[0]
     modes = a8_ref.shape[0]
-    s_ref[...] = jnp.zeros(s_ref.shape, jnp.float32)
+
+    @pl.when(pl.program_id(0) == 0)
+    def _():
+        s_ref[...] = jnp.zeros(s_ref.shape, jnp.float32)
 
     def body(b, carry):
         start = pl.multiple_of(b * CHUNK, CHUNK)
@@ -41,7 +47,10 @@
 def gate_kernel(conv_ref, q_ref, sums_ref, g_ref, a8_ref, sin_ref, out_ref, s_ref):
     rows = conv_ref.shape[0]
     modes = a8_ref.shape[0]
-    s_ref[...] = sin_ref[...]
+
+    @pl.when(pl.program_id(0) == 0)
+    def _():
+        s_ref[...] = sin_ref[...]
 
     def body(b, carry):
         start = pl.multiple_of(b * CHUNK, CHUNK)
@@ -57,14 +66,83 @@
     lax.fori_loop(0, rows // CHUNK, body, 0, unroll=4)
 
 
-def vmem_spec():
-    return pl.BlockSpec(memory_space=pltpu.VMEM)
+def rows_spec(rows, channels):
+    return pl.BlockSpec((rows, channels), lambda i: (i, 0))
+
+
+def whole_spec(shape):
+    return pl.BlockSpec(shape, lambda i: (0,) * len(shape))
+
+
+def sequential():
+    return pltpu.CompilerParams(dimension_semantics=("arbitrary",))
+
+
+def chunk_tables(decay_rate, mode_weight):
+    lam = decay_rate.T
+    amp = (mode_weight * jnp.sqrt(2.0 * decay_rate)).T
+    steps = jnp.arange(CHUNK).astype(jnp.float32)
+    g_tab = amp[:, None, :] * jnp.exp(-lam[:, None, :] * steps[None, :, None])
+    w_tab = jnp.exp(-lam[None, :, :] * (CHUNK - steps)[:, None, None])
+    h_short = jnp.sum(g_tab, axis=0)
+    lag = steps[None, :] - steps[:, None]
+    lag_index = jnp.clip(lag, 0, CHUNK - 1).astype(jnp.int32)
+    hcol = jnp.where((lag >= 0)[:, :, None], h_short[lag_index], 0.0)
+    a8 = jnp.exp(-lam * CHUNK)
+    return lam, g_tab, w_tab, hcol, a8
+
+
+def local_conv(drive, hcol, w_tab, a8):
+    rows, channels = drive.shape
+    modes = a8.shape[0]
+    blk = min(BLOCK, rows)
+    per = blk // CHUNK * modes
+    return pl.pallas_call(
+        local_kernel,
+        grid=(rows // blk,),
+        out_shape=(
+            jax.ShapeDtypeStruct((rows, channels), jnp.float32),
+            jax.ShapeDtypeStruct((rows // CHUNK * modes, channels), jnp.float32),
+            jax.ShapeDtypeStruct((modes, channels), jnp.float32),
+        ),
+        in_specs=[
+            rows_spec(blk, channels),
+            whole_spec(hcol.shape),
+            whole_spec(w_tab.shape),
+            whole_spec(a8.shape),
+        ],
+        out_specs=(rows_spec(blk, channels), rows_spec(per, channels), whole_spec(a8.shape)),
+        scratch_shapes=[pltpu.VMEM((modes, channels), jnp.float32)],
+        compiler_params=sequential(),
+    )(drive, hcol, w_tab, a8)
+
+
+def gate(conv_local, query, sums, g_tab, a8, state_in):
+    rows, channels = conv_local.shape
+    modes = a8.shape[0]
+    blk = min(BLOCK, rows)
+    per = blk // CHUNK * modes
+    return pl.pallas_call(
+        gate_kernel,
+        grid=(rows // blk,),
+        out_shape=jax.ShapeDtypeStruct((rows, channels), jnp.float32),
+        in_specs=[
+            rows_spec(blk, channels),
+            rows_spec(blk, channels),
+            rows_spec(per, channels),
+            whole_spec(g_tab.shape),
+            whole_spec(a8.shape),
+            whole_spec(state_in.shape),
+        ],
+        out_specs=rows_spec(blk, channels),
+        scratch_shapes=[pltpu.VMEM((modes, channels), jnp.float32)],
+        compiler_params=sequential(),
+    )(conv_local, query, sums, g_tab, a8, state_in)
 
 
 def per_device(tokens, in_weight, short_filter, mode_weight, decay_rate, out_weight):
     tok_rows = tokens.shape[0]
     channels = in_weight.shape[2]
-    modes = decay_rate.shape[1]
     proj = jnp.einsum(
         "td,dkc->tkc",
         lax.all_gather(tokens, "tensor", axis=1, tiled=True),
@@ -82,28 +160,8 @@
     query = filtered[:, 0]
     drive = filtered[:, 1] * filtered[:, 2]
 
-    lam = decay_rate.T
-    amp = (mode_weight * jnp.sqrt(2.0 * decay_rate)).T
-    steps = jnp.arange(CHUNK).astype(jnp.float32)
-    g_tab = amp[:, None, :] * jnp.exp(-lam[:, None, :] * steps[None, :, None])
-    w_tab = jnp.exp(-lam[None, :, :] * (CHUNK - steps)[:, None, None])
-    h_short = jnp.sum(g_tab, axis=0)
-    lag = steps[None, :] - steps[:, None]
-    lag_index = jnp.clip(lag, 0, CHUNK - 1).astype(jnp.int32)
-    hcol = jnp.where((lag >= 0)[:, :, None], h_short[lag_index], 0.0)
-    a8 = jnp.exp(-lam * CHUNK)
-
-    conv_local, sums, end_state = pl.pallas_call(
-        local_kernel,
-        out_shape=(
-            jax.ShapeDtypeStruct((tok_rows, channels), jnp.float32),
-            jax.ShapeDtypeStruct((tok_rows // CHUNK * modes, channels), jnp.float32),
-            jax.ShapeDtypeStruct((modes, channels), jnp.float32),
-        ),
-        in_specs=[vmem_spec() for _ in range(4)],
-        out_specs=(vmem_spec(), vmem_spec(), vmem_spec()),
-        scratch_shapes=[pltpu.VMEM((modes, channels), jnp.float32)],
-    )(drive, hcol, w_tab, a8)
+    lam, g_tab, w_tab, hcol, a8 = chunk_tables(decay_rate, mode_weight)
+    conv_local, sums, end_state = local_conv(drive, hcol, w_tab, a8)
 
     ends = lax.all_gather(end_state, "context", axis=0, tiled=False)
     block_count = ends.shape[0]
@@ -116,13 +174,7 @@
     )
     state_in = jnp.sum(factor * ends, axis=0)
 
-    gated = pl.pallas_call(
-        gate_kernel,
-        out_shape=jax.ShapeDtypeStruct((tok_rows, channels), jnp.float32),
-        in_specs=[vmem_spec() for _ in range(6)],
-        out_specs=vmem_spec(),
-        scratch_shapes=[pltpu.VMEM((modes, channels), jnp.float32)],
-    )(conv_local, query, sums, g_tab, a8, state_in)
+    gated = gate(conv_local, query, sums, g_tab, a8, state_in)
     gated = gated.astype(jnp.bfloat16)
     partial_sums = jnp.dot(gated, out_weight, preferred_element_type=jnp.float32)
     summed = lax.psum_scatter(

time: 220 us -> 220 us (level)
  no operation moved by 1% of the time
where the time goes in v9:
time: 220 us; the launch traced here: 219 us
  waiting for transfers between devices  147 us (67%)
  Pallas kernels  17.3 us (8%)
  matrix products  15.8 us (7%)
  other arithmetic  15 us (7%)
  between operations  13.5 us (6%)
  blocking collectives  7.94 us (4%)
    all_gather x1, waiting for transfers between devices, per_device(): lax.all_gather(tokens, 'tensor', axis=1, tiled=True)  74.2 us
    reduce_scatter x1, waiting for transfers between devices, per_device(): lax.psum_scatter(partial_sums.astype(jnp.bfloat16), 'tensor', scatter_dim...  71.7 us
    dot_general x1, matrix products, per_device(): jnp.einsum('td,dkc->tkc', lax.all_gather(tokens, 'tensor', axis=1, tiled=...  10.1 us
    pallas_call x1, Pallas kernels, gate(): pl.pallas_call(gate_kernel, grid=(rows // blk,), out_shape=jax.ShapeDtype...  8.84 us
    pallas_call x1, Pallas kernels, local_conv(): pl.pallas_call(local_kernel, grid=(rows // blk,), out_shape=(jax.ShapeDty...  8.44 us
    all_gather x1, blocking collectives, per_device(): ends = lax.all_gather(end_state, 'context', axis=0, tiled=False)  7.94 us
    add x1, other arithmetic, per_device(): filtered + short_filter[tap_number].astype(jnp.float32)[None] * padded[be...  5.82 us
    dot_general x1, matrix products, per_device(): jnp.dot(gated, out_weight, preferred_element_type=jnp.float32)  5.72 us
  transfers between devices with their start and end apart: 3, of which 3 were waited for; matrix products, arithmetic and copies ran while one was open for 3% of the time, Pallas kernels for 0%

profile of v9, /device:TPU:0, one launch (start us, length us, event | category | flops | bytes accessed | tf_op | source)
XLA Modules:
  0.0 219.4 jit_solution(9447705363559696670)
XLA Ops:
  6.5 0.0 copy-start
  6.5 0.0 all-gather.3.cloned.1.call-start
  6.5 0.7 all-gather.3.cloned.1.call-update
  7.3 0.0 reduce-scatter.2.cloned.1.call-start
  7.3 0.1 compare_select_fusion
  7.4 0.1 reshape.127
  7.5 0.8 multiply_bitcast_fusion
  8.3 0.8 exponential_multiply_fusion
  9.1 0.7 gather_fusion
  9.8 0.1 subtract_compare_fusion
  9.9 1.0 slice_convert_fusion.6
  10.9 1.4 multiply_exponential_fusion.1.a8_ref
  12.3 0.7 bitcast_select_fusion.hcol_ref
  13.0 0.8 multiply_exponential_fusion.w_ref
  13.9 74.2 %all-gather.3.cloned.1.call-done = bf16[1024,1920]{0,1:T(8,128)(2,1)} async-done(((bf16[1024,480]{0,1:T(8,128)(2,1)}), bf16[1024,1920]{0,1:T(8,128)(2,1)}) %all-gather.3.cloned.1.call-update) | async-done | bytes 3932176 | tf_op jit(solution)/shard_map/all_gather | solution.py:148
  88.1 10.1 %fusion.7 = bf16[1024,3,480]{2,0,1:T(8,128)(2,1)S(1)} fusion(bf16[1920,3,480]{0,2,1:T(8,128)(2,1)} %param.7, bf16[1024,1920]{0,1:T(8,128)(2,1)} %all-gather.3.cloned.1.call-done), kind=kOutput, calls=%fused_computation.19 | convolution fusion | flops 5663784960 | bytes 12410880 | tf_op jit(solution)/shard_map/td,dkc->tkc/dot_general | solution.py:146
  98.2 1.6 collective-permute-start
  99.8 0.8 collective-permute-done
  100.6 5.8 %multiply_add_fusion = f32[1024,3,480]{2,0,1:T(8,128)S(1)} fusion(bf16[1024,3,480]{2,0,1:T(8,128)(2,1)S(1)} %fusion.7, bf16[6,3,480]{2,0,1:T(8,128)(2,1)S(1)} %collective-permute-done, f32[3,480]{1,0:T(4,128)S(1)} %get-tuple-element.24, f32[3,480]{1,0:T(4,128)S(1)} %get-tuple-element.25, f32[3,480]{1,0:T(4,128)S(1)} %get-tuple-element.26, ...), kind=kLoop, calls=%fused_computation.6 | loop fusion | flops 56033280 | bytes 8904960 | tf_op jit(solution)/shard_map/add | solution.py:157
  106.4 2.8 %slice_bitcast_fusion = (f32[1024,480]{1,0:T(8,128)}, f32[1024,480]{1,0:T(8,128)}) fusion(f32[1024,3,480]{2,0,1:T(8,128)S(1)} %multiply_add_fusion), kind=kLoop, calls=%fused_computation.20 | loop fusion | flops 491520 | bytes 9830400 | tf_op jit(solution)/shard_map/squeeze | solution.py:160
  109.2 8.4 %shard_map.64 = (f32[1024,480]{1,0:T(8,128)}, f32[2048,480]{1,0:T(8,128)}, f32[16,480]{1,0:T(8,128)}) custom-call(f32[1024,480]{1,0:T(8,128)} %get-tuple-element.12.d_ref, f32[8,8,480]{2,1,0:T(8,128)} %bitcast_select_fusion.hcol_ref, f32[8,16,480]{2,1,0:T(8,128)} %multiply_exponential_fusion.w_ref, f32[16,480]{1,0:T(8,128)} %multiply_exponential_fusion.1.a8_ref), custom_call_target="tpu_custom_call" | custom-call | tf_op jit(solution)/shard_map/pallas_call | solution.py:100
  117.7 7.9 %all-gather = f32[64,480]{1,0:T(8,128)S(1)} all-gather(f32[16,480]{1,0:T(8,128)} %get-tuple-element.10), channel_id=2, replica_groups=mesh['groups'=2,'context'=4,'tensor'=4] {'context'}, dimensions={0}, use_global_device_ids=true | all-gather | bytes 153600 | tf_op jit(solution)/shard_map/all_gather | solution.py:166
  125.6 0.7 multiply_reduce_fusion.sin_ref
  126.3 8.8 %shard_map.65 = f32[1024,480]{1,0:T(8,128)} custom-call(f32[1024,480]{1,0:T(8,128)} %get-tuple-element.8.conv_ref, f32[1024,480]{1,0:T(8,128)} %get-tuple-element.11.q_ref, f32[2048,480]{1,0:T(8,128)} %get-tuple-element.9.sums_ref, f32[16,8,480]{2,1,0:T(8,128)} %get-tuple-element.13.g_ref, f32[16,480]{1,0:T(8,128)} %multiply_exponential_fusion.1.a8_ref, ...), custom_call_target="tpu_custom_call" | custom-call | tf_op jit(solution)/shard_map/pallas_call | solution.py:125
  135.1 0.0 copy-done
  135.1 5.7 %convolution_convert_fusion = bf16[1024,1920]{0,1:T(8,128)(2,1)} fusion(bf16[480,1920]{1,0:T(8,128)(2,1)S(1)} %copy-done, f32[1024,480]{1,0:T(8,128)} %shard_map.65), kind=kOutput, calls=%fused_computation.9 | convolution fusion | flops 1889894400 | bytes 7741440 | tf_op jit(solution)/shard_map/dot_general | solution.py:179
  140.9 0.0 reduce-scatter.2.cloned.1.call-update
  140.9 71.7 %reduce-scatter.2.cloned.1.call-done = bf16[1024,480]{0,1:T(8,128)(2,1)} async-done(((bf16[1024,1920]{0,1:T(8,128)(2,1)}), bf16[1024,480]{0,1:T(8,128)(2,1)}) %reduce-scatter.2.cloned.1.call-update) | async-done | bytes 983056 | tf_op jit(solution)/shard_map/reduce_scatter | solution.py:180
  (10 shorter events, 0.1 us)
Async XLA Ops:
  6.5 128.6 %copy-start = (bf16[480,1920]{1,0:T(8,128)(2,1)S(1)}, bf16[480,1920]{1,0:T(8,128)(2,1)}, u32[]{:S(2)}) copy-start(bf16[480,1920]{1,0:T(8,128)(2,1)} %param.11) | copy-start | bytes 5529604
  6.5 81.5 %all-gather.3.cloned.1.call-start = ((), (), s32[]{:S(2)}) async-start(), calls=%async_computation.1 | async-start | bytes 4915200 | tf_op jit(solution)/shard_map/all_gather | solution.py:148
  7.3 205.3 %reduce-scatter.2.cloned.1.call-start = ((), (), s32[]{:S(2)}) async-start(), calls=%async_computation.2 | async-start | bytes 4915200 | tf_op jit(solution)/shard_map/reduce_scatter | solution.py:180
  98.2 2.4 %collective-permute-start = (bf16[6,3,480]{2,0,1:T(8,128)(2,1)S(1)}, bf16[6,3,480]{2,0,1:T(8,128)(2,1)S(1)}, u32[]{:S(2)}, u32[]{:S(2)}) collective-permute-start(bf16[6,3,480]{2,0,1:T(8,128)(2,1)S(1)} %slice.70), channel_id=1, source_target_pairs={{0,4},{4,8},{8,12},{1,5},{5,9},{9,13},{2,6},{6,10},{10,14},{3,7},{... | collective-permute-start | bytes 51848 | tf_op jit(solution)/shard_map/ppermute | solution.py:15
Sparse Core Ops, SparseCore 0:
  8.9 79.1 all-gather.2
  141.0 71.5 reduce-scatter.1

commit v10 on v9

--- a/solution.py
+++ b/solution.py
@@ -151,14 +151,19 @@
     ).astype(jnp.bfloat16)
     rim = shifted(proj[tok_rows - (TAPS - 1) :], "context", 1)
     padded = jnp.concatenate([rim, proj], 0)
-    filtered = jnp.zeros((tok_rows, 3, channels), jnp.float32)
-    for tap_number in range(TAPS):
-        begin = TAPS - 1 - tap_number
-        filtered = filtered + short_filter[tap_number].astype(jnp.float32)[None] * padded[
-            begin : begin + tok_rows
-        ].astype(jnp.float32)
-    query = filtered[:, 0]
-    drive = filtered[:, 1] * filtered[:, 2]
+    taps = short_filter.astype(jnp.float32)
+
+    def stream(k):
+        acc = jnp.zeros((tok_rows, channels), jnp.float32)
+        for tap_number in range(TAPS):
+            begin = TAPS - 1 - tap_number
+            acc = acc + taps[tap_number, k][None] * padded[begin : begin + tok_rows, k].astype(
+                jnp.float32
+            )
+        return acc
+
+    query = stream(0)
+    drive = stream(1) * stream(2)
 
     lam, g_tab, w_tab, hcol, a8 = chunk_tables(decay_rate, mode_weight)
     conv_local, sums, end_state = local_conv(drive, hcol, w_tab, a8)

time: 220 us -> 223 us (1.014)
    mul x1, other arithmetic: 1.03 us -> 4.78 us  [per_device(): drive = stream(1) * stream(2)]
    squeeze x1 -> x0, other arithmetic: 2.79 us -> none  [per_device(): query = filtered[:, 0]]
  transfers between devices with their start and end apart: 3 -> 3, of which waited for: 3 -> 3; matrix products, arithmetic and copies ran while one was open for 3% -> 2% of each run, Pallas kernels for 0% -> 0%
where the time goes in v10:
time: 223 us; the launch traced here: 222 us
  waiting for transfers between devices  149 us (67%)
  Pallas kernels  17.2 us (8%)
  other arithmetic  15.9 us (7%)
  matrix products  15.8 us (7%)
  between operations  13.5 us (6%)
  blocking collectives  7.94 us (4%)
    all_gather x1, waiting for transfers between devices, per_device(): lax.all_gather(tokens, 'tensor', axis=1, tiled=True)  76 us
    reduce_scatter x1, waiting for transfers between devices, per_device(): lax.psum_scatter(partial_sums.astype(jnp.bfloat16), 'tensor', scatter_dim...  71.7 us
    dot_general x1, matrix products, per_device(): jnp.einsum('td,dkc->tkc', lax.all_gather(tokens, 'tensor', axis=1, tiled=...  10.1 us
    pallas_call x1, Pallas kernels, gate(): pl.pallas_call(gate_kernel, grid=(rows // blk,), out_shape=jax.ShapeDtype...  8.82 us
    pallas_call x1, Pallas kernels, local_conv(): pl.pallas_call(local_kernel, grid=(rows // blk,), out_shape=(jax.ShapeDty...  8.42 us
    all_gather x1, blocking collectives, per_device(): ends = lax.all_gather(end_state, 'context', axis=0, tiled=False)  7.94 us
    add x1, other arithmetic, stream(): acc + taps[tap_number, k][None] * padded[begin:begin + tok_rows, k].astyp...  6.47 us
    dot_general x1, matrix products, per_device(): jnp.dot(gated, out_weight, preferred_element_type=jnp.float32)  5.71 us
  transfers between devices with their start and end apart: 3, of which 3 were waited for; matrix products, arithmetic and copies ran while one was open for 2% of the time, Pallas kernels for 0%

profile of v10, /device:TPU:0, one launch (start us, length us, event | category | flops | bytes accessed | tf_op | source)
XLA Modules:
  0.0 222.1 jit_solution(232241840720508730)
XLA Ops:
  6.5 0.0 copy-start
  6.5 0.0 copy-start.2
  6.5 0.0 all-gather.3.cloned.1.call-start
  6.5 0.7 all-gather.3.cloned.1.call-update
  7.3 0.0 reduce-scatter.2.cloned.1.call-start
  7.3 0.1 compare_select_fusion
  7.4 0.1 reshape.203
  7.5 0.8 multiply_bitcast_fusion
  8.3 0.8 exponential_multiply_fusion
  9.1 0.7 gather_fusion
  9.8 0.1 subtract_compare_fusion
  9.9 0.0 copy-done.3
  9.9 0.0 copy-done.2
  9.9 0.6 multiply_exponential_fusion.1.a8_ref
  10.5 0.7 bitcast_select_fusion.hcol_ref
  11.3 0.8 multiply_exponential_fusion.w_ref
  12.1 76.0 %all-gather.3.cloned.1.call-done = bf16[1024,1920]{0,1:T(8,128)(2,1)} async-done(((bf16[1024,480]{0,1:T(8,128)(2,1)}), bf16[1024,1920]{0,1:T(8,128)(2,1)}) %all-gather.3.cloned.1.call-update) | async-done | bytes 3932176 | tf_op jit(solution)/shard_map/all_gather | solution.py:148
  88.1 10.1 %fusion.2 = bf16[1024,3,480]{2,0,1:T(8,128)(2,1)S(1)} fusion(bf16[1920,3,480]{0,2,1:T(8,128)(2,1)} %param.7, bf16[1024,1920]{0,1:T(8,128)(2,1)} %all-gather.3.cloned.1.call-done), kind=kOutput, calls=%fused_computation.21 | convolution fusion | flops 5663784960 | bytes 12410880 | tf_op jit(solution)/shard_map/td,dkc->tkc/dot_general | solution.py:146
  98.2 0.0 copy-start.1
  98.2 1.6 collective-permute-start
  99.8 0.8 collective-permute-done
  100.6 0.0 copy-done.1
  100.6 4.8 %fusion.12.d_ref = f32[1024,480]{1,0:T(8,128)} fusion(bf16[6,3,480]{2,0,1:T(8,128)(2,1)S(1)} %collective-permute-done, bf16[1024,3,480]{2,0,1:T(8,128)(2,1)S(1)} %fusion.2, f32[480]{0:T(512)S(1)} %bitcast.165, f32[480]{0:T(512)S(1)} %bitcast.164, f32[480]{0:T(512)S(1)} %bitcast.163, f32[480]{0:T(512)S(1)} %bitcast.162, f32[480]{0:T(512)S(1)} %bitcast.161, ...), kind=kLoop, calls=%fused_computation.37 | loop fusion | flops 43745280 | bytes 7262208 | tf_op jit(solution)/shard_map/mul | solution.py:166
  105.4 8.4 %shard_map.64 = (f32[1024,480]{1,0:T(8,128)}, f32[2048,480]{1,0:T(8,128)}, f32[16,480]{1,0:T(8,128)}) custom-call(f32[1024,480]{1,0:T(8,128)} %fusion.12.d_ref, f32[8,8,480]{2,1,0:T(8,128)} %bitcast_select_fusion.hcol_ref, f32[8,16,480]{2,1,0:T(8,128)} %multiply_exponential_fusion.w_ref, f32[16,480]{1,0:T(8,128)} %multiply_exponential_fusion.1.a8_ref), custom_call_target="tpu_custom_call" | custom-call | tf_op jit(solution)/shard_map/pallas_call | solution.py:100
  113.8 7.9 %all-gather = f32[64,480]{1,0:T(8,128)S(1)} all-gather(f32[16,480]{1,0:T(8,128)} %get-tuple-element.10), channel_id=2, replica_groups=mesh['groups'=2,'context'=4,'tensor'=4] {'context'}, dimensions={0}, use_global_device_ids=true | all-gather | bytes 153600 | tf_op jit(solution)/shard_map/all_gather | solution.py:171
  121.8 0.7 multiply_reduce_fusion.sin_ref
  122.5 6.5 %fusion.5.q_ref = f32[1024,480]{1,0:T(8,128)} fusion(bf16[6,3,480]{2,0,1:T(8,128)(2,1)S(1)} %collective-permute-done, bf16[1024,3,480]{2,0,1:T(8,128)(2,1)} %copy-done.1, f32[480]{0:T(512)S(1)} %bitcast.151, f32[480]{0:T(512)S(1)} %bitcast.150, f32[480]{0:T(512)S(1)} %bitcast.149, f32[480]{0:T(512)S(1)} %bitcast.148, f32[480]{0:T(512)S(1)} %bitcast.147, ...), kind=kLoop, calls=%fused_computation.23 | loop fusion | flops 21626880 | bytes 6191104 | tf_op jit(solution)/shard_map/add | solution.py:160
  128.9 8.8 %shard_map.65 = f32[1024,480]{1,0:T(8,128)} custom-call(f32[1024,480]{1,0:T(8,128)} %get-tuple-element.8.conv_ref, f32[1024,480]{1,0:T(8,128)} %fusion.5.q_ref, f32[2048,480]{1,0:T(8,128)} %get-tuple-element.9.sums_ref, f32[16,8,480]{2,1,0:T(8,128)} %get-tuple-element.11.g_ref, f32[16,480]{1,0:T(8,128)} %multiply_exponential_fusion.1.a8_ref, ...), custom_call_target="tpu_custom_call" | custom-call | tf_op jit(solution)/shard_map/pallas_call | solution.py:125
  137.8 0.0 copy-done
  137.8 5.7 %convolution_convert_fusion = bf16[1024,1920]{0,1:T(8,128)(2,1)} fusion(bf16[480,1920]{1,0:T(8,128)(2,1)S(1)} %copy-done, f32[1024,480]{1,0:T(8,128)} %shard_map.65), kind=kOutput, calls=%fused_computation.20 | convolution fusion | flops 1889894400 | bytes 7741440 | tf_op jit(solution)/shard_map/dot_general | solution.py:184
  143.5 0.0 reduce-scatter.2.cloned.1.call-update
  143.5 71.7 %reduce-scatter.2.cloned.1.call-done = bf16[1024,480]{0,1:T(8,128)(2,1)} async-done(((bf16[1024,1920]{0,1:T(8,128)(2,1)}), bf16[1024,480]{0,1:T(8,128)(2,1)}) %reduce-scatter.2.cloned.1.call-update) | async-done | bytes 983056 | tf_op jit(solution)/shard_map/reduce_scatter | solution.py:185
  (9 shorter events, 0.1 us)
Async XLA Ops:
  6.5 131.2 %copy-start = (bf16[480,1920]{1,0:T(8,128)(2,1)S(1)}, bf16[480,1920]{1,0:T(8,128)(2,1)}, u32[]{:S(2)}) copy-start(bf16[480,1920]{1,0:T(8,128)(2,1)} %param.11) | copy-start | bytes 5529604
  6.5 3.4 %copy-start.2 = (f32[480,16]{0,1:T(8,128)S(1)}, f32[480,16]{0,1:T(8,128)}, u32[]{:S(2)}) copy-start(f32[480,16]{0,1:T(8,128)} %param.10) | copy-start | bytes 92164
  6.5 3.3 %copy-start.3 = (bf16[7,3,480]{2,0,1:T(8,128)(2,1)S(1)}, bf16[7,3,480]{2,0,1:T(8,128)(2,1)}, u32[]{:S(2)}) copy-start(bf16[7,3,480]{2,0,1:T(8,128)(2,1)} %param.8) | copy-start | bytes 60484
  6.5 81.5 %all-gather.3.cloned.1.call-start = ((), (), s32[]{:S(2)}) async-start(), calls=%async_computation.1 | async-start | bytes 4915200 | tf_op jit(solution)/shard_map/all_gather | solution.py:148
  7.3 208.0 %reduce-scatter.2.cloned.1.call-start = ((), (), s32[]{:S(2)}) async-start(), calls=%async_computation.2 | async-start | bytes 4915200 | tf_op jit(solution)/shard_map/reduce_scatter | solution.py:185
  98.2 2.5 %copy-start.1 = (bf16[1024,3,480]{2,0,1:T(8,128)(2,1)}, bf16[1024,3,480]{2,0,1:T(8,128)(2,1)S(1)}, u32[]{:S(2)}) copy-start(bf16[1024,3,480]{2,0,1:T(8,128)(2,1)S(1)} %fusion.2) | copy-start | bytes 8847364
  98.2 2.4 %collective-permute-start = (bf16[6,3,480]{2,0,1:T(8,128)(2,1)S(1)}, bf16[6,3,480]{2,0,1:T(8,128)(2,1)S(1)}, u32[]{:S(2)}, u32[]{:S(2)}) collective-permute-start(bf16[6,3,480]{2,0,1:T(8,128)(2,1)S(1)} %slice.177), channel_id=1, source_target_pairs={{0,4},{4,8},{8,12},{1,5},{5,9},{9,13},{2,6},{6,10},{10,14},{3,7},{... | collective-permute-start | bytes 51848 | tf_op jit(solution)/shard_map/ppermute | solution.py:15
Sparse Core Ops, SparseCore 0:
  8.9 79.1 all-gather.2
  143.6 71.5 reduce-scatter.1

commit v11 on v9

--- a/solution.py
+++ b/solution.py
@@ -44,7 +44,7 @@
     end_ref[...] = s_ref[...]
 
 
-def gate_kernel(conv_ref, q_ref, sums_ref, g_ref, a8_ref, sin_ref, out_ref, s_ref):
+def gate_kernel(conv_ref, q_ref, sums_ref, g_ref, a8_ref, sin_ref, wo_ref, out_ref, s_ref, gated_ref):
     rows = conv_ref.shape[0]
     modes = a8_ref.shape[0]
 
@@ -58,12 +58,16 @@
         acc = conv_ref[pl.ds(start, CHUNK), :]
         for n in range(modes):
             acc = acc + g_ref[n] * state[n : n + 1, :]
-        out_ref[pl.ds(start, CHUNK), :] = q_ref[pl.ds(start, CHUNK), :] * acc
+        gated_ref[pl.ds(start, CHUNK), :] = q_ref[pl.ds(start, CHUNK), :] * acc
         piece = sums_ref[pl.ds(pl.multiple_of(b * modes, modes), modes), :]
         s_ref[...] = a8_ref[...] * state + piece
         return carry
 
     lax.fori_loop(0, rows // CHUNK, body, 0, unroll=4)
+    gated = gated_ref[...].astype(jnp.bfloat16)
+    out_ref[...] = lax.dot_general(
+        wo_ref[...], gated, (((0,), (1,)), ((), ())), preferred_element_type=jnp.float32
+    ).astype(out_ref.dtype)
 
 
 def rows_spec(rows, channels):
@@ -117,15 +121,16 @@
     )(drive, hcol, w_tab, a8)
 
 
-def gate(conv_local, query, sums, g_tab, a8, state_in):
+def gate(conv_local, query, sums, g_tab, a8, state_in, out_weight):
     rows, channels = conv_local.shape
+    width = out_weight.shape[1]
     modes = a8.shape[0]
     blk = min(BLOCK, rows)
     per = blk // CHUNK * modes
     return pl.pallas_call(
         gate_kernel,
         grid=(rows // blk,),
-        out_shape=jax.ShapeDtypeStruct((rows, channels), jnp.float32),
+        out_shape=jax.ShapeDtypeStruct((width, rows), jnp.bfloat16),
         in_specs=[
             rows_spec(blk, channels),
             rows_spec(blk, channels),
@@ -133,11 +138,15 @@
             whole_spec(g_tab.shape),
             whole_spec(a8.shape),
             whole_spec(state_in.shape),
+            whole_spec(out_weight.shape),
         ],
-        out_specs=rows_spec(blk, channels),
-        scratch_shapes=[pltpu.VMEM((modes, channels), jnp.float32)],
+        out_specs=pl.BlockSpec((width, blk), lambda i: (0, i)),
+        scratch_shapes=[
+            pltpu.VMEM((modes, channels), jnp.float32),
+            pltpu.VMEM((blk, channels), jnp.float32),
+        ],
         compiler_params=sequential(),
-    )(conv_local, query, sums, g_tab, a8, state_in)
+    )(conv_local, query, sums, g_tab, a8, state_in, out_weight)
 
 
 def per_device(tokens, in_weight, short_filter, mode_weight, decay_rate, out_weight):
@@ -174,12 +183,8 @@
     )
     state_in = jnp.sum(factor * ends, axis=0)
 
-    gated = gate(conv_local, query, sums, g_tab, a8, state_in)
-    gated = gated.astype(jnp.bfloat16)
-    partial_sums = jnp.dot(gated, out_weight, preferred_element_type=jnp.float32)
-    summed = lax.psum_scatter(
-        partial_sums.astype(jnp.bfloat16), "tensor", scatter_dimension=1, tiled=True
-    )
+    partial_sums = gate(conv_local, query, sums, g_tab, a8, state_in, out_weight)
+    summed = lax.psum_scatter(partial_sums, "tensor", scatter_dimension=0, tiled=True).T
     return summed
 
 

time: 220 us -> 219 us (level)
  matrix products: 15.8 us -> 10.1 us
  Pallas kernels: 17.3 us -> 21.4 us
    dot_general x1 -> x0, matrix products: 5.72 us -> none  [per_device(): jnp.dot(gated, out_weight, preferred_element_type=jnp.float32)]
    pallas_call x1, Pallas kernels: 8.84 us -> 13.2 us  [gate(): pl.pallas_call(gate_kernel, grid=(rows // blk,), out_shape=jax.ShapeDtype...]
where the time goes in v11:
time: 219 us; the launch traced here: 218 us
  waiting for transfers between devices  147 us (67%)
  Pallas kernels  21.4 us (10%)
  other arithmetic  15.1 us (7%)
  between operations  13.5 us (6%)
  matrix products  10.1 us (5%)
  blocking collectives  7.94 us (4%)
    all_gather x1, waiting for transfers between devices, per_device(): lax.all_gather(tokens, 'tensor', axis=1, tiled=True)  74.2 us
    reduce_scatter x1, waiting for transfers between devices, per_device(): lax.psum_scatter(partial_sums, 'tensor', scatter_dimension=0, tiled=True)  71.7 us
    pallas_call x1, Pallas kernels, gate(): pl.pallas_call(gate_kernel, grid=(rows // blk,), out_shape=jax.ShapeDtype...  13.2 us
    dot_general x1, matrix products, per_device(): jnp.einsum('td,dkc->tkc', lax.all_gather(tokens, 'tensor', axis=1, tiled=...  10.1 us
    pallas_call x1, Pallas kernels, local_conv(): pl.pallas_call(local_kernel, grid=(rows // blk,), out_shape=(jax.ShapeDty...  8.25 us
    all_gather x1, blocking collectives, per_device(): ends = lax.all_gather(end_state, 'context', axis=0, tiled=False)  7.94 us
    add x1, other arithmetic, per_device(): filtered + short_filter[tap_number].astype(jnp.float32)[None] * padded[be...  5.82 us
  transfers between devices with their start and end apart: 3, of which 3 were waited for; matrix products, arithmetic and copies ran while one was open for 3% of the time, Pallas kernels for 0%

profile of v11, /device:TPU:0, one launch (start us, length us, event | category | flops | bytes accessed | tf_op | source)
XLA Modules:
  0.0 218.0 jit_solution(16451847176326270424)
XLA Ops:
  6.5 0.0 all-gather.3.cloned.1.call-start
  6.5 0.7 all-gather.3.cloned.1.call-update
  7.3 0.0 reduce-scatter.2.cloned.1.call-start
  7.3 0.1 compare_select_fusion
  7.4 0.1 reshape.127
  7.5 0.8 multiply_bitcast_fusion
  8.3 0.8 exponential_multiply_fusion
  9.1 0.7 gather_fusion
  9.8 0.1 subtract_compare_fusion
  9.9 1.0 slice_convert_fusion.6
  10.9 1.4 multiply_exponential_fusion.1.a8_ref
  12.3 0.7 bitcast_select_fusion.hcol_ref
  13.0 0.8 multiply_exponential_fusion.w_ref
  13.8 74.2 %all-gather.3.cloned.1.call-done = bf16[1024,1920]{0,1:T(8,128)(2,1)} async-done(((bf16[1024,480]{0,1:T(8,128)(2,1)}), bf16[1024,1920]{0,1:T(8,128)(2,1)}) %all-gather.3.cloned.1.call-update) | async-done | bytes 3932176 | tf_op jit(solution)/shard_map/all_gather | solution.py:157
  88.1 10.1 %fusion.7 = bf16[1024,3,480]{2,0,1:T(8,128)(2,1)S(1)} fusion(bf16[1920,3,480]{0,2,1:T(8,128)(2,1)} %param.7, bf16[1024,1920]{0,1:T(8,128)(2,1)} %all-gather.3.cloned.1.call-done), kind=kOutput, calls=%fused_computation.18 | convolution fusion | flops 5663784960 | bytes 12410880 | tf_op jit(solution)/shard_map/td,dkc->tkc/dot_general | solution.py:155
  98.2 1.6 collective-permute-start
  99.8 0.8 collective-permute-done
  100.6 5.8 %multiply_add_fusion = f32[1024,3,480]{2,0,1:T(8,128)S(1)} fusion(bf16[1024,3,480]{2,0,1:T(8,128)(2,1)S(1)} %fusion.7, bf16[6,3,480]{2,0,1:T(8,128)(2,1)S(1)} %collective-permute-done, f32[3,480]{1,0:T(4,128)S(1)} %get-tuple-element.24, f32[3,480]{1,0:T(4,128)S(1)} %get-tuple-element.25, f32[3,480]{1,0:T(4,128)S(1)} %get-tuple-element.26, ...), kind=kLoop, calls=%fused_computation.6 | loop fusion | flops 56033280 | bytes 8904960 | tf_op jit(solution)/shard_map/add | solution.py:166
  106.4 2.8 %slice_bitcast_fusion = (f32[1024,480]{1,0:T(8,128)}, f32[1024,480]{1,0:T(8,128)}) fusion(f32[1024,3,480]{2,0,1:T(8,128)S(1)} %multiply_add_fusion), kind=kLoop, calls=%fused_computation.19 | loop fusion | flops 491520 | bytes 9830400 | tf_op jit(solution)/shard_map/squeeze | solution.py:169
  109.3 8.3 %shard_map.64 = (f32[1024,480]{1,0:T(8,128)}, f32[2048,480]{1,0:T(8,128)}, f32[16,480]{1,0:T(8,128)}) custom-call(f32[1024,480]{1,0:T(8,128)} %get-tuple-element.12.d_ref, f32[8,8,480]{2,1,0:T(8,128)} %bitcast_select_fusion.hcol_ref, f32[8,16,480]{2,1,0:T(8,128)} %multiply_exponential_fusion.w_ref, f32[16,480]{1,0:T(8,128)} %multiply_exponential_fusion.1.a8_ref), custom_call_target="tpu_custom_call" | custom-call | tf_op jit(solution)/shard_map/pallas_call | solution.py:104
  117.5 7.9 %all-gather = f32[64,480]{1,0:T(8,128)S(1)} all-gather(f32[16,480]{1,0:T(8,128)} %get-tuple-element.10), channel_id=2, replica_groups=mesh['groups'=2,'context'=4,'tensor'=4] {'context'}, dimensions={0}, use_global_device_ids=true | all-gather | bytes 153600 | tf_op jit(solution)/shard_map/all_gather | solution.py:175
  125.5 0.7 multiply_reduce_fusion.sin_ref
  126.2 13.2 %shard_map.65 = bf16[1920,1024]{1,0:T(8,128)(2,1)} custom-call(f32[1024,480]{1,0:T(8,128)} %get-tuple-element.8.conv_ref, f32[1024,480]{1,0:T(8,128)} %get-tuple-element.11.q_ref, f32[2048,480]{1,0:T(8,128)} %get-tuple-element.9.sums_ref, f32[16,8,480]{2,1,0:T(8,128)} %get-tuple-element.13.g_ref, f32[16,480]{1,0:T(8,128)} %multiply_exponential_fusion.1.a8_ref, ...), custom_call_target="tpu_custom_call" | custom-call | tf_op jit(solution)/shard_map/pallas_call | solution.py:130
  139.4 0.0 reduce-scatter.2.cloned.1.call-update
  139.4 71.7 %reduce-scatter.2.cloned.1.call-done = bf16[480,1024]{1,0:T(8,128)(2,1)} async-done(((bf16[1920,1024]{1,0:T(8,128)(2,1)}), bf16[480,1024]{1,0:T(8,128)(2,1)}) %reduce-scatter.2.cloned.1.call-update) | async-done | bytes 983056 | tf_op jit(solution)/shard_map/reduce_scatter | solution.py:187
  (10 shorter events, 0.1 us)
Async XLA Ops:
  6.5 81.5 %all-gather.3.cloned.1.call-start = ((), (), s32[]{:S(2)}) async-start(), calls=%async_computation.1 | async-start | bytes 4915200 | tf_op jit(solution)/shard_map/all_gather | solution.py:157
  7.3 203.9 %reduce-scatter.2.cloned.1.call-start = ((), (), s32[]{:S(2)}) async-start(), calls=%async_computation.2 | async-start | bytes 4915200 | tf_op jit(solution)/shard_map/reduce_scatter | solution.py:187
  98.2 2.4 %collective-permute-start = (bf16[6,3,480]{2,0,1:T(8,128)(2,1)S(1)}, bf16[6,3,480]{2,0,1:T(8,128)(2,1)S(1)}, u32[]{:S(2)}, u32[]{:S(2)}) collective-permute-start(bf16[6,3,480]{2,0,1:T(8,128)(2,1)S(1)} %slice.70), channel_id=1, source_target_pairs={{0,4},{4,8},{8,12},{1,5},{5,9},{9,13},{2,6},{6,10},{10,14},{3,7},{... | collective-permute-start | bytes 51848 | tf_op jit(solution)/shard_map/ppermute | solution.py:15
Sparse Core Ops, SparseCore 0:
  8.9 79.1 all-gather.2
  139.5 71.5 reduce-scatter.1

commit v12 on v11

--- a/solution.py
+++ b/solution.py
@@ -15,7 +15,7 @@
     return lax.ppermute(array, axis, pairs)
 
 
-BLOCK = 128
+BLOCK = 256
 
 
 def local_kernel(d_ref, hcol_ref, w_ref, a8_ref, conv_ref, sums_ref, end_ref, s_ref):

time: 219 us -> 214 us (0.977)
  Pallas kernels: 21.4 us -> 17.4 us
    pallas_call x1, Pallas kernels: 13.2 us -> 10.5 us  [gate(): pl.pallas_call(gate_kernel, grid=(rows // blk,), out_shape=jax.ShapeDtype...]
where the time goes in v12:
time: 214 us
  waiting for transfers between devices  147 us (69%)
  Pallas kernels  17.4 us (8%)
  other arithmetic  15.1 us (7%)
  between operations  13.5 us (6%)
  matrix products  10.1 us (5%)
  blocking collectives  7.94 us (4%)
    all_gather x1, waiting for transfers between devices, per_device(): lax.all_gather(tokens, 'tensor', axis=1, tiled=True)  74.2 us
    reduce_scatter x1, waiting for transfers between devices, per_device(): lax.psum_scatter(partial_sums, 'tensor', scatter_dimension=0, tiled=True)  71.7 us
    pallas_call x1, Pallas kernels, gate(): pl.pallas_call(gate_kernel, grid=(rows // blk,), out_shape=jax.ShapeDtype...  10.5 us
    dot_general x1, matrix products, per_device(): jnp.einsum('td,dkc->tkc', lax.all_gather(tokens, 'tensor', axis=1, tiled=...  10.1 us
    all_gather x1, blocking collectives, per_device(): ends = lax.all_gather(end_state, 'context', axis=0, tiled=False)  7.94 us
    pallas_call x1, Pallas kernels, local_conv(): pl.pallas_call(local_kernel, grid=(rows // blk,), out_shape=(jax.ShapeDty...  6.85 us
    add x1, other arithmetic, per_device(): filtered + short_filter[tap_number].astype(jnp.float32)[None] * padded[be...  5.82 us
  transfers between devices with their start and end apart: 3, of which 3 were waited for; matrix products, arithmetic and copies ran while one was open for 3% of the time, Pallas kernels for 0%

profile of v12, /device:TPU:0, one launch (start us, length us, event | category | flops | bytes accessed | tf_op | source)
XLA Modules:
  0.0 213.9 jit_solution(11890057499676562232)
XLA Ops:
  6.5 0.0 all-gather.3.cloned.1.call-start
  6.5 0.7 all-gather.3.cloned.1.call-update
  7.3 0.0 reduce-scatter.2.cloned.1.call-start
  7.3 0.1 compare_select_fusion
  7.4 0.1 reshape.127
  7.5 0.8 multiply_bitcast_fusion
  8.3 0.8 exponential_multiply_fusion
  9.1 0.7 gather_fusion
  9.8 0.1 subtract_compare_fusion
  9.9 1.0 slice_convert_fusion.6
  10.9 1.4 multiply_exponential_fusion.1.a8_ref
  12.3 0.7 bitcast_select_fusion.hcol_ref
  13.0 0.8 multiply_exponential_fusion.w_ref
  13.8 74.2 %all-gather.3.cloned.1.call-done = bf16[1024,1920]{0,1:T(8,128)(2,1)} async-done(((bf16[1024,480]{0,1:T(8,128)(2,1)}), bf16[1024,1920]{0,1:T(8,128)(2,1)}) %all-gather.3.cloned.1.call-update) | async-done | bytes 3932176 | tf_op jit(solution)/shard_map/all_gather | solution.py:157
  88.1 10.1 %fusion.7 = bf16[1024,3,480]{2,0,1:T(8,128)(2,1)S(1)} fusion(bf16[1920,3,480]{0,2,1:T(8,128)(2,1)} %param.7, bf16[1024,1920]{0,1:T(8,128)(2,1)} %all-gather.3.cloned.1.call-done), kind=kOutput, calls=%fused_computation.18 | convolution fusion | flops 5663784960 | bytes 12410880 | tf_op jit(solution)/shard_map/td,dkc->tkc/dot_general | solution.py:155
  98.2 1.6 collective-permute-start
  99.8 0.8 collective-permute-done
  100.6 5.8 %multiply_add_fusion = f32[1024,3,480]{2,0,1:T(8,128)S(1)} fusion(bf16[1024,3,480]{2,0,1:T(8,128)(2,1)S(1)} %fusion.7, bf16[6,3,480]{2,0,1:T(8,128)(2,1)S(1)} %collective-permute-done, f32[3,480]{1,0:T(4,128)S(1)} %get-tuple-element.24, f32[3,480]{1,0:T(4,128)S(1)} %get-tuple-element.25, f32[3,480]{1,0:T(4,128)S(1)} %get-tuple-element.26, ...), kind=kLoop, calls=%fused_computation.6 | loop fusion | flops 56033280 | bytes 8904960 | tf_op jit(solution)/shard_map/add | solution.py:166
  106.4 2.8 %slice_bitcast_fusion = (f32[1024,480]{1,0:T(8,128)}, f32[1024,480]{1,0:T(8,128)}) fusion(f32[1024,3,480]{2,0,1:T(8,128)S(1)} %multiply_add_fusion), kind=kLoop, calls=%fused_computation.19 | loop fusion | flops 491520 | bytes 9830400 | tf_op jit(solution)/shard_map/squeeze | solution.py:169
  109.3 6.8 %shard_map.64 = (f32[1024,480]{1,0:T(8,128)}, f32[2048,480]{1,0:T(8,128)}, f32[16,480]{1,0:T(8,128)}) custom-call(f32[1024,480]{1,0:T(8,128)} %get-tuple-element.12.d_ref, f32[8,8,480]{2,1,0:T(8,128)} %bitcast_select_fusion.hcol_ref, f32[8,16,480]{2,1,0:T(8,128)} %multiply_exponential_fusion.w_ref, f32[16,480]{1,0:T(8,128)} %multiply_exponential_fusion.1.a8_ref), custom_call_target="tpu_custom_call" | custom-call | tf_op jit(solution)/shard_map/pallas_call | solution.py:104
  116.1 7.9 %all-gather = f32[64,480]{1,0:T(8,128)S(1)} all-gather(f32[16,480]{1,0:T(8,128)} %get-tuple-element.10), channel_id=2, replica_groups=mesh['groups'=2,'context'=4,'tensor'=4] {'context'}, dimensions={0}, use_global_device_ids=true | all-gather | bytes 153600 | tf_op jit(solution)/shard_map/all_gather | solution.py:175
  124.1 0.7 multiply_reduce_fusion.sin_ref
  124.8 10.5 %shard_map.65 = bf16[1920,1024]{1,0:T(8,128)(2,1)} custom-call(f32[1024,480]{1,0:T(8,128)} %get-tuple-element.8.conv_ref, f32[1024,480]{1,0:T(8,128)} %get-tuple-element.11.q_ref, f32[2048,480]{1,0:T(8,128)} %get-tuple-element.9.sums_ref, f32[16,8,480]{2,1,0:T(8,128)} %get-tuple-element.13.g_ref, f32[16,480]{1,0:T(8,128)} %multiply_exponential_fusion.1.a8_ref, ...), custom_call_target="tpu_custom_call" | custom-call | tf_op jit(solution)/shard_map/pallas_call | solution.py:130
  135.3 0.0 reduce-scatter.2.cloned.1.call-update
  135.3 71.7 %reduce-scatter.2.cloned.1.call-done = bf16[480,1024]{1,0:T(8,128)(2,1)} async-done(((bf16[1920,1024]{1,0:T(8,128)(2,1)}), bf16[480,1024]{1,0:T(8,128)(2,1)}) %reduce-scatter.2.cloned.1.call-update) | async-done | bytes 983056 | tf_op jit(solution)/shard_map/reduce_scatter | solution.py:187
  (10 shorter events, 0.1 us)
Async XLA Ops:
  6.5 81.5 %all-gather.3.cloned.1.call-start = ((), (), s32[]{:S(2)}) async-start(), calls=%async_computation.1 | async-start | bytes 4915200 | tf_op jit(solution)/shard_map/all_gather | solution.py:157
  7.3 199.8 %reduce-scatter.2.cloned.1.call-start = ((), (), s32[]{:S(2)}) async-start(), calls=%async_computation.2 | async-start | bytes 4915200 | tf_op jit(solution)/shard_map/reduce_scatter | solution.py:187
  98.2 2.4 %collective-permute-start = (bf16[6,3,480]{2,0,1:T(8,128)(2,1)S(1)}, bf16[6,3,480]{2,0,1:T(8,128)(2,1)S(1)}, u32[]{:S(2)}, u32[]{:S(2)}) collective-permute-start(bf16[6,3,480]{2,0,1:T(8,128)(2,1)S(1)} %slice.70), channel_id=1, source_target_pairs={{0,4},{4,8},{8,12},{1,5},{5,9},{9,13},{2,6},{6,10},{10,14},{3,7},{... | collective-permute-start | bytes 51848 | tf_op jit(solution)/shard_map/ppermute | solution.py:15
Sparse Core Ops, SparseCore 0:
  8.9 79.1 all-gather.2
  135.4 71.5 reduce-scatter.1

commit v13 on v12

--- a/solution.py
+++ b/solution.py
@@ -15,7 +15,7 @@
     return lax.ppermute(array, axis, pairs)
 
 
-BLOCK = 256
+BLOCK = 512
 
 
 def local_kernel(d_ref, hcol_ref, w_ref, a8_ref, conv_ref, sums_ref, end_ref, s_ref):

time: 214 us -> 215 us (level)
  no operation moved by 1% of the time
where the time goes in v13:
time: 215 us; the launch traced here: 214 us
  waiting for transfers between devices  147 us (68%)
  Pallas kernels  17.7 us (8%)
  other arithmetic  15.1 us (7%)
  between operations  13.5 us (6%)
  matrix products  10.1 us (5%)
  blocking collectives  7.93 us (4%)
    all_gather x1, waiting for transfers between devices, per_device(): lax.all_gather(tokens, 'tensor', axis=1, tiled=True)  74.2 us
    reduce_scatter x1, waiting for transfers between devices, per_device(): lax.psum_scatter(partial_sums, 'tensor', scatter_dimension=0, tiled=True)  71.7 us
    pallas_call x1, Pallas kernels, gate(): pl.pallas_call(gate_kernel, grid=(rows // blk,), out_shape=jax.ShapeDtype...  10.9 us
    dot_general x1, matrix products, per_device(): jnp.einsum('td,dkc->tkc', lax.all_gather(tokens, 'tensor', axis=1, tiled=...  10.1 us
    all_gather x1, blocking collectives, per_device(): ends = lax.all_gather(end_state, 'context', axis=0, tiled=False)  7.93 us
    pallas_call x1, Pallas kernels, local_conv(): pl.pallas_call(local_kernel, grid=(rows // blk,), out_shape=(jax.ShapeDty...  6.84 us
    add x1, other arithmetic, per_device(): filtered + short_filter[tap_number].astype(jnp.float32)[None] * padded[be...  5.82 us
  transfers between devices with their start and end apart: 3, of which 3 were waited for; matrix products, arithmetic and copies ran while one was open for 3% of the time, Pallas kernels for 0%

profile of v13, /device:TPU:0, one launch (start us, length us, event | category | flops | bytes accessed | tf_op | source)
XLA Modules:
  0.0 214.2 jit_solution(8570072316663758925)
XLA Ops:
  6.5 0.0 all-gather.3.cloned.1.call-start
  6.5 0.7 all-gather.3.cloned.1.call-update
  7.3 0.0 reduce-scatter.2.cloned.1.call-start
  7.3 0.1 compare_select_fusion
  7.4 0.1 reshape.127
  7.5 0.8 multiply_bitcast_fusion
  8.3 0.8 exponential_multiply_fusion
  9.1 0.7 gather_fusion
  9.8 0.1 subtract_compare_fusion
  9.9 1.0 slice_convert_fusion.6
  10.9 1.4 multiply_exponential_fusion.1.a8_ref
  12.3 0.7 bitcast_select_fusion.hcol_ref
  13.0 0.8 multiply_exponential_fusion.w_ref
  13.8 74.2 %all-gather.3.cloned.1.call-done = bf16[1024,1920]{0,1:T(8,128)(2,1)} async-done(((bf16[1024,480]{0,1:T(8,128)(2,1)}), bf16[1024,1920]{0,1:T(8,128)(2,1)}) %all-gather.3.cloned.1.call-update) | async-done | bytes 3932176 | tf_op jit(solution)/shard_map/all_gather | solution.py:157
  88.1 10.1 %fusion.7 = bf16[1024,3,480]{2,0,1:T(8,128)(2,1)S(1)} fusion(bf16[1920,3,480]{0,2,1:T(8,128)(2,1)} %param.7, bf16[1024,1920]{0,1:T(8,128)(2,1)} %all-gather.3.cloned.1.call-done), kind=kOutput, calls=%fused_computation.18 | convolution fusion | flops 5663784960 | bytes 12410880 | tf_op jit(solution)/shard_map/td,dkc->tkc/dot_general | solution.py:155
  98.2 1.6 collective-permute-start
  99.8 0.8 collective-permute-done
  100.6 5.8 %multiply_add_fusion = f32[1024,3,480]{2,0,1:T(8,128)S(1)} fusion(bf16[1024,3,480]{2,0,1:T(8,128)(2,1)S(1)} %fusion.7, bf16[6,3,480]{2,0,1:T(8,128)(2,1)S(1)} %collective-permute-done, f32[3,480]{1,0:T(4,128)S(1)} %get-tuple-element.24, f32[3,480]{1,0:T(4,128)S(1)} %get-tuple-element.25, f32[3,480]{1,0:T(4,128)S(1)} %get-tuple-element.26, ...), kind=kLoop, calls=%fused_computation.6 | loop fusion | flops 56033280 | bytes 8904960 | tf_op jit(solution)/shard_map/add | solution.py:166
  106.4 2.8 %slice_bitcast_fusion = (f32[1024,480]{1,0:T(8,128)}, f32[1024,480]{1,0:T(8,128)}) fusion(f32[1024,3,480]{2,0,1:T(8,128)S(1)} %multiply_add_fusion), kind=kLoop, calls=%fused_computation.19 | loop fusion | flops 491520 | bytes 9830400 | tf_op jit(solution)/shard_map/squeeze | solution.py:169
  109.3 6.8 %shard_map.64 = (f32[1024,480]{1,0:T(8,128)}, f32[2048,480]{1,0:T(8,128)}, f32[16,480]{1,0:T(8,128)}) custom-call(f32[1024,480]{1,0:T(8,128)} %get-tuple-element.12.d_ref, f32[8,8,480]{2,1,0:T(8,128)} %bitcast_select_fusion.hcol_ref, f32[8,16,480]{2,1,0:T(8,128)} %multiply_exponential_fusion.w_ref, f32[16,480]{1,0:T(8,128)} %multiply_exponential_fusion.1.a8_ref), custom_call_target="tpu_custom_call" | custom-call | tf_op jit(solution)/shard_map/pallas_call | solution.py:104
  116.1 7.9 %all-gather = f32[64,480]{1,0:T(8,128)S(1)} all-gather(f32[16,480]{1,0:T(8,128)} %get-tuple-element.10), channel_id=2, replica_groups=mesh['groups'=2,'context'=4,'tensor'=4] {'context'}, dimensions={0}, use_global_device_ids=true | all-gather | bytes 153600 | tf_op jit(solution)/shard_map/all_gather | solution.py:175
  124.0 0.7 multiply_reduce_fusion.sin_ref
  124.8 10.9 %shard_map.65 = bf16[1920,1024]{1,0:T(8,128)(2,1)} custom-call(f32[1024,480]{1,0:T(8,128)} %get-tuple-element.8.conv_ref, f32[1024,480]{1,0:T(8,128)} %get-tuple-element.11.q_ref, f32[2048,480]{1,0:T(8,128)} %get-tuple-element.9.sums_ref, f32[16,8,480]{2,1,0:T(8,128)} %get-tuple-element.13.g_ref, f32[16,480]{1,0:T(8,128)} %multiply_exponential_fusion.1.a8_ref, ...), custom_call_target="tpu_custom_call" | custom-call | tf_op jit(solution)/shard_map/pallas_call | solution.py:130
  135.6 0.0 reduce-scatter.2.cloned.1.call-update
  135.6 71.7 %reduce-scatter.2.cloned.1.call-done = bf16[480,1024]{1,0:T(8,128)(2,1)} async-done(((bf16[1920,1024]{1,0:T(8,128)(2,1)}), bf16[480,1024]{1,0:T(8,128)(2,1)}) %reduce-scatter.2.cloned.1.call-update) | async-done | bytes 983056 | tf_op jit(solution)/shard_map/reduce_scatter | solution.py:187
  (10 shorter events, 0.1 us)
Async XLA Ops:
  6.5 81.5 %all-gather.3.cloned.1.call-start = ((), (), s32[]{:S(2)}) async-start(), calls=%async_computation.1 | async-start | bytes 4915200 | tf_op jit(solution)/shard_map/all_gather | solution.py:157
  7.3 200.1 %reduce-scatter.2.cloned.1.call-start = ((), (), s32[]{:S(2)}) async-start(), calls=%async_computation.2 | async-start | bytes 4915200 | tf_op jit(solution)/shard_map/reduce_scatter | solution.py:187
  98.2 2.4 %collective-permute-start = (bf16[6,3,480]{2,0,1:T(8,128)(2,1)S(1)}, bf16[6,3,480]{2,0,1:T(8,128)(2,1)S(1)}, u32[]{:S(2)}, u32[]{:S(2)}) collective-permute-start(bf16[6,3,480]{2,0,1:T(8,128)(2,1)S(1)} %slice.70), channel_id=1, source_target_pairs={{0,4},{4,8},{8,12},{1,5},{5,9},{9,13},{2,6},{6,10},{10,14},{3,7},{... | collective-permute-start | bytes 51848 | tf_op jit(solution)/shard_map/ppermute | solution.py:15
Sparse Core Ops, SparseCore 0:
  8.9 79.1 all-gather.2
  135.8 71.5 reduce-scatter.1

commit v14 on v12

--- a/solution.py
+++ b/solution.py
@@ -172,9 +172,11 @@
     lam, g_tab, w_tab, hcol, a8 = chunk_tables(decay_rate, mode_weight)
     conv_local, sums, end_state = local_conv(drive, hcol, w_tab, a8)
 
-    ends = lax.all_gather(end_state, "context", axis=0, tiled=False)
-    block_count = ends.shape[0]
+    block_count = lax.axis_size("context")
     me = lax.axis_index("context")
+    slots = jnp.zeros((block_count,) + end_state.shape, jnp.float32)
+    slots = lax.dynamic_update_slice_in_dim(slots, end_state[None], me, 0)
+    ends = lax.psum(slots, "context")
     gap = (me - 1 - jnp.arange(block_count)).astype(jnp.float32)
     factor = jnp.where(
         (gap >= 0.0)[:, None, None],

time: 214 us -> 243 us (1.14)
  waiting for transfers between devices: 147 us -> 182 us
  blocking collectives: 7.94 us -> 0 us
    psum x0 -> x1, waiting for transfers between devices: none -> 33.1 us  [per_device(): ends = lax.psum(slots, 'context')]
    all_gather x1 -> x0, blocking collectives: 7.94 us -> none  [per_device(): ends = lax.all_gather(end_state, 'context', axis=0, tiled=False)]
  transfers between devices with their start and end apart: 3 -> 4, of which waited for: 3 -> 4; matrix products, arithmetic and copies ran while one was open for 3% -> 3% of each run, Pallas kernels for 0% -> 0%
where the time goes in v14:
time: 243 us; the launch traced here: 242 us
  waiting for transfers between devices  182 us (75%)
  Pallas kernels  17.4 us (7%)
  other arithmetic  16 us (7%)
  between operations  13.2 us (5%)
  matrix products  10.1 us (4%)
    all_gather x1, waiting for transfers between devices, per_device(): lax.all_gather(tokens, 'tensor', axis=1, tiled=True)  74.3 us
    reduce_scatter x1, waiting for transfers between devices, per_device(): lax.psum_scatter(partial_sums, 'tensor', scatter_dimension=0, tiled=True)  72.8 us
    psum x1, waiting for transfers between devices, per_device(): ends = lax.psum(slots, 'context')  33.1 us
    pallas_call x1, Pallas kernels, gate(): pl.pallas_call(gate_kernel, grid=(rows // blk,), out_shape=jax.ShapeDtype...  10.5 us
    dot_general x1, matrix products, per_device(): jnp.einsum('td,dkc->tkc', lax.all_gather(tokens, 'tensor', axis=1, tiled=...  10.1 us
    pallas_call x1, Pallas kernels, local_conv(): pl.pallas_call(local_kernel, grid=(rows // blk,), out_shape=(jax.ShapeDty...  6.84 us
    add x1, other arithmetic, per_device(): filtered + short_filter[tap_number].astype(jnp.float32)[None] * padded[be...  5.82 us
  transfers between devices with their start and end apart: 4, of which 4 were waited for; matrix products, arithmetic and copies ran while one was open for 3% of the time, Pallas kernels for 0%

profile of v14, /device:TPU:0, one launch (start us, length us, event | category | flops | bytes accessed | tf_op | source)
XLA Modules:
  0.0 242.2 jit_solution(7916442417932881236)
XLA Ops:
  6.5 0.0 all-gather.2.cloned.1.call-start
  6.5 0.7 all-gather.2.cloned.1.call-update
  7.3 0.0 all-reduce.2.cloned.1.call-start
  7.3 0.1 compare_select_fusion
  7.4 0.1 reshape.127
  7.5 0.8 multiply_bitcast_fusion
  8.3 0.8 exponential_multiply_fusion
  9.1 0.7 gather_fusion
  9.8 0.1 subtract_compare_fusion
  9.8 1.0 slice_convert_fusion.6
  10.9 1.4 multiply_exponential_fusion.1.a8_ref
  12.3 0.7 bitcast_select_fusion.hcol_ref
  13.0 0.8 multiply_exponential_fusion.w_ref
  13.8 74.3 %all-gather.2.cloned.1.call-done = bf16[1024,1920]{0,1:T(8,128)(2,1)} async-done(((bf16[1024,480]{0,1:T(8,128)(2,1)}), bf16[1024,1920]{0,1:T(8,128)(2,1)}) %all-gather.2.cloned.1.call-update) | async-done | bytes 3932176 | tf_op jit(solution)/shard_map/all_gather | solution.py:157
  88.1 10.1 %fusion.7 = bf16[1024,3,480]{2,0,1:T(8,128)(2,1)S(1)} fusion(bf16[1920,3,480]{0,2,1:T(8,128)(2,1)} %param.7, bf16[1024,1920]{0,1:T(8,128)(2,1)} %all-gather.2.cloned.1.call-done), kind=kOutput, calls=%fused_computation.18 | convolution fusion | flops 5663784960 | bytes 12410880 | tf_op jit(solution)/shard_map/td,dkc->tkc/dot_general | solution.py:155
  98.2 1.6 collective-permute-start
  99.8 0.8 collective-permute-done
  100.6 5.8 %multiply_add_fusion = f32[1024,3,480]{2,0,1:T(8,128)S(1)} fusion(bf16[1024,3,480]{2,0,1:T(8,128)(2,1)S(1)} %fusion.7, bf16[6,3,480]{2,0,1:T(8,128)(2,1)S(1)} %collective-permute-done, f32[3,480]{1,0:T(4,128)S(1)} %get-tuple-element.24, f32[3,480]{1,0:T(4,128)S(1)} %get-tuple-element.25, f32[3,480]{1,0:T(4,128)S(1)} %get-tuple-element.26, ...), kind=kLoop, calls=%fused_computation.6 | loop fusion | flops 56033280 | bytes 8904960 | tf_op jit(solution)/shard_map/add | solution.py:166
  106.4 2.8 %slice_bitcast_fusion = (f32[1024,480]{1,0:T(8,128)}, f32[1024,480]{1,0:T(8,128)}) fusion(f32[1024,3,480]{2,0,1:T(8,128)S(1)} %multiply_add_fusion), kind=kLoop, calls=%fused_computation.19 | loop fusion | flops 491520 | bytes 9830400 | tf_op jit(solution)/shard_map/squeeze | solution.py:169
  109.3 6.8 %shard_map.64 = (f32[1024,480]{1,0:T(8,128)}, f32[2048,480]{1,0:T(8,128)}, f32[16,480]{1,0:T(8,128)}) custom-call(f32[1024,480]{1,0:T(8,128)} %get-tuple-element.12.d_ref, f32[8,8,480]{2,1,0:T(8,128)} %bitcast_select_fusion.hcol_ref, f32[8,16,480]{2,1,0:T(8,128)} %multiply_exponential_fusion.w_ref, f32[16,480]{1,0:T(8,128)} %multiply_exponential_fusion.1.a8_ref), custom_call_target="tpu_custom_call" | custom-call | tf_op jit(solution)/shard_map/pallas_call | solution.py:104
  116.1 0.8 bitcast_dynamic-update-slice_fusion
  116.9 0.0 copy-start
  116.9 0.6 copy-done
  117.5 0.0 all-reduce.2.cloned.1.call-update
  117.6 0.0 reduce-scatter.2.cloned.1.call-start
  117.6 33.1 %all-reduce.2.cloned.1.call-done = f32[4,16,480]{2,1,0:T(8,128)} async-done(((f32[4,16,480]{2,1,0:T(8,128)}), f32[4,16,480]{2,1,0:T(8,128)}) %all-reduce.2.cloned.1.call-update) | async-done | bytes 122896 | tf_op jit(solution)/shard_map/psum | solution.py:179
  150.7 1.6 multiply_reduce_fusion.sin_ref
  152.3 10.5 %shard_map.65 = bf16[1920,1024]{1,0:T(8,128)(2,1)} custom-call(f32[1024,480]{1,0:T(8,128)} %get-tuple-element.8.conv_ref, f32[1024,480]{1,0:T(8,128)} %get-tuple-element.11.q_ref, f32[2048,480]{1,0:T(8,128)} %get-tuple-element.9.sums_ref, f32[16,8,480]{2,1,0:T(8,128)} %get-tuple-element.13.g_ref, f32[16,480]{1,0:T(8,128)} %multiply_exponential_fusion.1.a8_ref, ...), custom_call_target="tpu_custom_call" | custom-call | tf_op jit(solution)/shard_map/pallas_call | solution.py:130
  162.9 0.0 reduce-scatter.2.cloned.1.call-update
  162.9 72.8 %reduce-scatter.2.cloned.1.call-done = bf16[480,1024]{1,0:T(8,128)(2,1)} async-done(((bf16[1920,1024]{1,0:T(8,128)(2,1)}), bf16[480,1024]{1,0:T(8,128)(2,1)}) %reduce-scatter.2.cloned.1.call-update) | async-done | bytes 983056 | tf_op jit(solution)/shard_map/reduce_scatter | solution.py:189
  (11 shorter events, 0.1 us)
Async XLA Ops:
  6.5 81.5 %all-gather.2.cloned.1.call-start = ((), (), s32[]{:S(2)}) async-start(), calls=%async_computation.1 | async-start | bytes 4915200 | tf_op jit(solution)/shard_map/all_gather | solution.py:157
  7.3 143.5 %all-reduce.2.cloned.1.call-start = ((), (), s32[]{:S(2)}) async-start(), calls=%async_computation.2 | async-start | bytes 262144 | tf_op jit(solution)/shard_map/psum | solution.py:179
  98.2 2.4 %collective-permute-start = (bf16[6,3,480]{2,0,1:T(8,128)(2,1)S(1)}, bf16[6,3,480]{2,0,1:T(8,128)(2,1)S(1)}, u32[]{:S(2)}, u32[]{:S(2)}) collective-permute-start(bf16[6,3,480]{2,0,1:T(8,128)(2,1)S(1)} %slice.70), channel_id=1, source_target_pairs={{0,4},{4,8},{8,12},{1,5},{5,9},{9,13},{2,6},{6,10},{10,14},{3,7},{... | collective-permute-start | bytes 51848 | tf_op jit(solution)/shard_map/ppermute | solution.py:15
  116.9 0.6 copy-start
  117.6 118.1 %reduce-scatter.2.cloned.1.call-start = ((), (), s32[]{:S(2)}) async-start(), calls=%async_computation.3 | async-start | bytes 4915200 | tf_op jit(solution)/shard_map/reduce_scatter | solution.py:189
Sparse Core Ops, SparseCore 0:
  8.9 79.1 all-gather.1
  117.7 33.0 all-reduce.1
  163.0 72.6 reduce-scatter.1

commit v15 on v12

--- a/solution.py
+++ b/solution.py
@@ -96,8 +96,8 @@
     return lam, g_tab, w_tab, hcol, a8
 
 
-def local_conv(drive, hcol, w_tab, a8):
-    rows, channels = drive.shape
+def local_conv(planes, hcol, w_tab, a8):
+    rows, channels = planes.shape[1:]
     modes = a8.shape[0]
     blk = min(BLOCK, rows)
     per = blk // CHUNK * modes
@@ -110,7 +110,7 @@
             jax.ShapeDtypeStruct((modes, channels), jnp.float32),
         ),
         in_specs=[
-            rows_spec(blk, channels),
+            pl.BlockSpec((None, blk, channels), lambda i: (1, i, 0)),
             whole_spec(hcol.shape),
             whole_spec(w_tab.shape),
             whole_spec(a8.shape),
@@ -118,7 +118,7 @@
         out_specs=(rows_spec(blk, channels), rows_spec(per, channels), whole_spec(a8.shape)),
         scratch_shapes=[pltpu.VMEM((modes, channels), jnp.float32)],
         compiler_params=sequential(),
-    )(drive, hcol, w_tab, a8)
+    )(planes, hcol, w_tab, a8)
 
 
 def gate(conv_local, query, sums, g_tab, a8, state_in, out_weight):
@@ -133,7 +133,7 @@
         out_shape=jax.ShapeDtypeStruct((width, rows), jnp.bfloat16),
         in_specs=[
             rows_spec(blk, channels),
-            rows_spec(blk, channels),
+            pl.BlockSpec((None, blk, channels), lambda i: (0, i, 0)),
             rows_spec(per, channels),
             whole_spec(g_tab.shape),
             whole_spec(a8.shape),
@@ -166,11 +166,10 @@
         filtered = filtered + short_filter[tap_number].astype(jnp.float32)[None] * padded[
             begin : begin + tok_rows
         ].astype(jnp.float32)
-    query = filtered[:, 0]
-    drive = filtered[:, 1] * filtered[:, 2]
+    planes = jnp.stack([filtered[:, 0], filtered[:, 1] * filtered[:, 2]], 0)
 
     lam, g_tab, w_tab, hcol, a8 = chunk_tables(decay_rate, mode_weight)
-    conv_local, sums, end_state = local_conv(drive, hcol, w_tab, a8)
+    conv_local, sums, end_state = local_conv(planes, hcol, w_tab, a8)
 
     ends = lax.all_gather(end_state, "context", axis=0, tiled=False)
     block_count = ends.shape[0]
@@ -183,7 +182,7 @@
     )
     state_in = jnp.sum(factor * ends, axis=0)
 
-    partial_sums = gate(conv_local, query, sums, g_tab, a8, state_in, out_weight)
+    partial_sums = gate(conv_local, planes, sums, g_tab, a8, state_in, out_weight)
     summed = lax.psum_scatter(partial_sums, "tensor", scatter_dimension=0, tiled=True).T
     return summed
 

time: 214 us -> 215 us (level)
    another operation x0 -> x2, other arithmetic: none -> 3.14 us  [per_device(): planes = jnp.stack([filtered[:, 0], filtered[:, 1] * filtered[:, 2]], 0)]
    squeeze x1 -> x0, other arithmetic: 2.85 us -> none  [per_device(): query = filtered[:, 0]]
where the time goes in v15:
time: 215 us; the launch traced here: 214 us
  waiting for transfers between devices  147 us (68%)
  Pallas kernels  17.4 us (8%)
  other arithmetic  15.4 us (7%)
  between operations  13.5 us (6%)
  matrix products  10.1 us (5%)
  blocking collectives  7.94 us (4%)
    all_gather x1, waiting for transfers between devices, per_device(): lax.all_gather(tokens, 'tensor', axis=1, tiled=True)  74.2 us
    reduce_scatter x1, waiting for transfers between devices, per_device(): lax.psum_scatter(partial_sums, 'tensor', scatter_dimension=0, tiled=True)  71.7 us
    pallas_call x1, Pallas kernels, gate(): pl.pallas_call(gate_kernel, grid=(rows // blk,), out_shape=jax.ShapeDtype...  10.5 us
    dot_general x1, matrix products, per_device(): jnp.einsum('td,dkc->tkc', lax.all_gather(tokens, 'tensor', axis=1, tiled=...  10.1 us
    all_gather x1, blocking collectives, per_device(): ends = lax.all_gather(end_state, 'context', axis=0, tiled=False)  7.94 us
    pallas_call x1, Pallas kernels, local_conv(): pl.pallas_call(local_kernel, grid=(rows // blk,), out_shape=(jax.ShapeDty...  6.9 us
    add x1, other arithmetic, per_device(): filtered + short_filter[tap_number].astype(jnp.float32)[None] * padded[be...  5.82 us
  transfers between devices with their start and end apart: 3, of which 3 were waited for; matrix products, arithmetic and copies ran while one was open for 3% of the time, Pallas kernels for 0%

profile of v15, /device:TPU:0, one launch (start us, length us, event | category | flops | bytes accessed | tf_op | source)
XLA Modules:
  0.0 214.2 jit_solution(2473952015818791376)
XLA Ops:
  6.5 0.0 all-gather.3.cloned.1.call-start
  6.5 0.7 all-gather.3.cloned.1.call-update
  7.3 0.0 reduce-scatter.2.cloned.1.call-start
  7.3 0.1 compare_select_fusion
  7.4 0.1 reshape.144
  7.5 0.8 multiply_bitcast_fusion
  8.3 0.8 exponential_multiply_fusion
  9.1 0.7 gather_fusion
  9.8 0.1 subtract_compare_fusion
  9.9 1.0 slice_convert_fusion.6
  10.9 1.4 multiply_exponential_fusion.1.a8_ref
  12.3 0.7 bitcast_select_fusion.hcol_ref
  13.0 0.8 multiply_exponential_fusion.w_ref
  13.9 74.2 %all-gather.3.cloned.1.call-done = bf16[1024,1920]{0,1:T(8,128)(2,1)} async-done(((bf16[1024,480]{0,1:T(8,128)(2,1)}), bf16[1024,1920]{0,1:T(8,128)(2,1)}) %all-gather.3.cloned.1.call-update) | async-done | bytes 3932176 | tf_op jit(solution)/shard_map/all_gather | solution.py:157
  88.1 10.1 %fusion.7 = bf16[1024,3,480]{2,0,1:T(8,128)(2,1)S(1)} fusion(bf16[1920,3,480]{0,2,1:T(8,128)(2,1)} %param.7, bf16[1024,1920]{0,1:T(8,128)(2,1)} %all-gather.3.cloned.1.call-done), kind=kOutput, calls=%fused_computation.19 | convolution fusion | flops 5663784960 | bytes 12410880 | tf_op jit(solution)/shard_map/td,dkc->tkc/dot_general | solution.py:155
  98.2 1.6 collective-permute-start
  99.8 0.8 collective-permute-done
  100.6 5.8 %multiply_add_fusion = f32[1024,3,480]{2,0,1:T(8,128)S(1)} fusion(bf16[1024,3,480]{2,0,1:T(8,128)(2,1)S(1)} %fusion.7, bf16[6,3,480]{2,0,1:T(8,128)(2,1)S(1)} %collective-permute-done, f32[3,480]{1,0:T(4,128)S(1)} %get-tuple-element.24, f32[3,480]{1,0:T(4,128)S(1)} %get-tuple-element.25, f32[3,480]{1,0:T(4,128)S(1)} %get-tuple-element.26, ...), kind=kLoop, calls=%fused_computation.6 | loop fusion | flops 56033280 | bytes 8904960 | tf_op jit(solution)/shard_map/add | solution.py:166
  106.4 0.7 slice_bitcast_fusion
  107.2 2.4 %pad_maximum_fusion.d_ref.q_ref = f32[2,1024,480]{2,1,0:T(8,128)} fusion(f32[1,1024,480]{2,1,0:T(8,128)S(1)} %get-tuple-element.12, f32[1,1024,480]{2,1,0:T(8,128)S(1)} %get-tuple-element.11), kind=kLoop, calls=%fused_computation.7 | loop fusion | flops 983040 | bytes 7864320 | tf_op jit(solution)/shard_map/stack | solution.py:169
  109.6 6.9 %shard_map.64 = (f32[1024,480]{1,0:T(8,128)}, f32[2048,480]{1,0:T(8,128)}, f32[16,480]{1,0:T(8,128)}) custom-call(f32[2,1024,480]{2,1,0:T(8,128)} %pad_maximum_fusion.d_ref.q_ref, f32[8,8,480]{2,1,0:T(8,128)} %bitcast_select_fusion.hcol_ref, f32[8,16,480]{2,1,0:T(8,128)} %multiply_exponential_fusion.w_ref, f32[16,480]{1,0:T(8,128)} %multiply_exponential_fusion.1.a8_ref), custom_call_target="tpu_custom_call" | custom-call | tf_op jit(solution)/shard_map/pallas_call | solution.py:104
  116.5 7.9 %all-gather = f32[64,480]{1,0:T(8,128)S(1)} all-gather(f32[16,480]{1,0:T(8,128)} %get-tuple-element.10), channel_id=2, replica_groups=mesh['groups'=2,'context'=4,'tensor'=4] {'context'}, dimensions={0}, use_global_device_ids=true | all-gather | bytes 153600 | tf_op jit(solution)/shard_map/all_gather | solution.py:174
  124.4 0.7 multiply_reduce_fusion.sin_ref
  125.1 10.5 %shard_map.65 = bf16[1920,1024]{1,0:T(8,128)(2,1)} custom-call(f32[1024,480]{1,0:T(8,128)} %get-tuple-element.8.conv_ref, f32[2,1024,480]{2,1,0:T(8,128)} %pad_maximum_fusion.d_ref.q_ref, f32[2048,480]{1,0:T(8,128)} %get-tuple-element.9.sums_ref, f32[16,8,480]{2,1,0:T(8,128)} %get-tuple-element.13.g_ref, f32[16,480]{1,0:T(8,128)} %multiply_exponential_fusion.1.a8_ref, ...), custom_call_target="tpu_custom_call" | custom-call | tf_op jit(solution)/shard_map/pallas_call | solution.py:130
  135.7 0.0 reduce-scatter.2.cloned.1.call-update
  135.7 71.7 %reduce-scatter.2.cloned.1.call-done = bf16[480,1024]{1,0:T(8,128)(2,1)} async-done(((bf16[1920,1024]{1,0:T(8,128)(2,1)}), bf16[480,1024]{1,0:T(8,128)(2,1)}) %reduce-scatter.2.cloned.1.call-update) | async-done | bytes 983056 | tf_op jit(solution)/shard_map/reduce_scatter | solution.py:186
  (10 shorter events, 0.1 us)
Async XLA Ops:
  6.5 81.5 %all-gather.3.cloned.1.call-start = ((), (), s32[]{:S(2)}) async-start(), calls=%async_computation.1 | async-start | bytes 4915200 | tf_op jit(solution)/shard_map/all_gather | solution.py:157
  7.3 200.1 %reduce-scatter.2.cloned.1.call-start = ((), (), s32[]{:S(2)}) async-start(), calls=%async_computation.2 | async-start | bytes 4915200 | tf_op jit(solution)/shard_map/reduce_scatter | solution.py:186
  98.2 2.4 %collective-permute-start = (bf16[6,3,480]{2,0,1:T(8,128)(2,1)S(1)}, bf16[6,3,480]{2,0,1:T(8,128)(2,1)S(1)}, u32[]{:S(2)}, u32[]{:S(2)}) collective-permute-start(bf16[6,3,480]{2,0,1:T(8,128)(2,1)S(1)} %slice.70), channel_id=1, source_target_pairs={{0,4},{4,8},{8,12},{1,5},{5,9},{9,13},{2,6},{6,10},{10,14},{3,7},{... | collective-permute-start | bytes 51848 | tf_op jit(solution)/shard_map/ppermute | solution.py:15
Sparse Core Ops, SparseCore 0:
  8.9 79.1 all-gather.2
  135.8 71.5 reduce-scatter.1

commit v16 on v12

--- a/solution.py
+++ b/solution.py
@@ -158,14 +158,22 @@
         in_weight,
         preferred_element_type=jnp.float32,
     ).astype(jnp.bfloat16)
-    rim = shifted(proj[tok_rows - (TAPS - 1) :], "context", 1)
-    padded = jnp.concatenate([rim, proj], 0)
+    rim_rows = TAPS - 1
+    rim = shifted(proj[tok_rows - rim_rows :], "context", 1)
+    taps = short_filter.astype(jnp.float32)
+    padded = jnp.concatenate([jnp.zeros_like(rim), proj], 0)
     filtered = jnp.zeros((tok_rows, 3, channels), jnp.float32)
     for tap_number in range(TAPS):
-        begin = TAPS - 1 - tap_number
-        filtered = filtered + short_filter[tap_number].astype(jnp.float32)[None] * padded[
-            begin : begin + tok_rows
-        ].astype(jnp.float32)
+        begin = rim_rows - tap_number
+        filtered = filtered + taps[tap_number][None] * padded[begin : begin + tok_rows].astype(
+            jnp.float32
+        )
+    edge = jnp.concatenate([rim, jnp.zeros_like(rim)], 0).astype(jnp.float32)
+    fix = jnp.zeros((rim_rows, 3, channels), jnp.float32)
+    for tap_number in range(1, TAPS):
+        begin = rim_rows - tap_number
+        fix = fix + taps[tap_number][None] * edge[begin : begin + rim_rows]
+    filtered = filtered.at[:rim_rows].add(fix)
     query = filtered[:, 0]
     drive = filtered[:, 1] * filtered[:, 2]
 

time: 214 us -> 218 us (1.019)
  local copies, waits for them, and re-layouts: 0.77 us -> 5.89 us
    squeeze x1, other arithmetic: 2.85 us -> 5.58 us  [per_device(): query = filtered[:, 0]]
    unnamed x4 -> x6, local copies, waits for them, and re-layouts: 0.02 us -> 2.64 us
    add x1 -> x2, other arithmetic: 5.82 us -> 5.81 us  [the longest x1 5.76 us: per_device(): filtered + taps[tap_number][None] * padded[begin:begin + tok_rows].astype...]
  transfers between devices with their start and end apart: 3 -> 3, of which waited for: 3 -> 2; matrix products, arithmetic and copies ran while one was open for 3% -> 6% of each run, Pallas kernels for 0% -> 0%
where the time goes in v16:
time: 218 us
  waiting for transfers between devices  146 us (67%)
  Pallas kernels  17.4 us (8%)
  other arithmetic  16.8 us (8%)
  between operations  13.5 us (6%)
  matrix products  10.1 us (5%)
  blocking collectives  6.2 us (3%)
  local copies, waits for them, and re-layouts  5.89 us (3%)
    all_gather x1, waiting for transfers between devices, per_device(): lax.all_gather(tokens, 'tensor', axis=1, tiled=True)  74.2 us
    reduce_scatter x1, waiting for transfers between devices, per_device(): lax.psum_scatter(partial_sums, 'tensor', scatter_dimension=0, tiled=True)  71.1 us
    pallas_call x1, Pallas kernels, gate(): pl.pallas_call(gate_kernel, grid=(rows // blk,), out_shape=jax.ShapeDtype...  10.5 us
    dot_general x1, matrix products, per_device(): jnp.einsum('td,dkc->tkc', lax.all_gather(tokens, 'tensor', axis=1, tiled=...  10.1 us
    pallas_call x1, Pallas kernels, local_conv(): pl.pallas_call(local_kernel, grid=(rows // blk,), out_shape=(jax.ShapeDty...  6.89 us
    all_gather x1, blocking collectives, per_device(): ends = lax.all_gather(end_state, 'context', axis=0, tiled=False)  6.2 us
    add x1, other arithmetic, per_device(): filtered + taps[tap_number][None] * padded[begin:begin + tok_rows].astype...  5.76 us
    squeeze x1, other arithmetic, per_device(): query = filtered[:, 0]  5.58 us
  transfers between devices with their start and end apart: 3, of which 2 were waited for; matrix products, arithmetic and copies ran while one was open for 6% of the time, Pallas kernels for 0%

profile of v16, /device:TPU:0, one launch (start us, length us, event | category | flops | bytes accessed | tf_op | source)
XLA Modules:
  0.0 217.6 jit_solution(5054746770066286133)
XLA Ops:
  6.5 0.0 all-gather.3.cloned.1.call-start
  6.5 0.7 all-gather.3.cloned.1.call-update
  7.3 0.0 reduce-scatter.2.cloned.1.call-start
  7.3 1.0 fusion.13
  8.4 0.1 compare_select_fusion
  8.4 0.1 reshape.152
  8.5 0.8 multiply_bitcast_fusion
  9.3 0.8 exponential_multiply_fusion
  10.1 0.7 gather_fusion
  10.8 0.1 subtract_compare_fusion
  10.9 1.4 multiply_exponential_fusion.1.a8_ref
  12.3 0.7 bitcast_select_fusion.hcol_ref
  13.1 0.8 multiply_exponential_fusion.w_ref
  13.9 74.2 %all-gather.3.cloned.1.call-done = bf16[1024,1920]{0,1:T(8,128)(2,1)} async-done(((bf16[1024,480]{0,1:T(8,128)(2,1)}), bf16[1024,1920]{0,1:T(8,128)(2,1)}) %all-gather.3.cloned.1.call-update) | async-done | bytes 3932176 | tf_op jit(solution)/shard_map/all_gather | solution.py:157
  88.1 10.1 %fusion.2 = bf16[1024,3,480]{2,0,1:T(8,128)(2,1)S(1)} fusion(bf16[1920,3,480]{0,2,1:T(8,128)(2,1)} %param.9, bf16[1024,1920]{0,1:T(8,128)(2,1)} %all-gather.3.cloned.1.call-done), kind=kOutput, calls=%fused_computation.8 | convolution fusion | flops 5663784960 | bytes 12410880 | tf_op jit(solution)/shard_map/td,dkc->tkc/dot_general | solution.py:155
  98.2 1.6 collective-permute-start
  99.8 5.8 %multiply_add_fusion = f32[1024,3,480]{2,0,1:T(8,128)S(1)} fusion(bf16[1024,3,480]{2,0,1:T(8,128)(2,1)S(1)} %fusion.2, f32[3,480]{1,0:T(4,128)S(1)} %get-tuple-element.36, f32[3,480]{1,0:T(4,128)S(1)} %get-tuple-element.37, f32[3,480]{1,0:T(4,128)S(1)} %get-tuple-element.38, f32[3,480]{1,0:T(4,128)S(1)} %get-tuple-element.39, ...), kind=kLoop, calls=%fused_computation.1 | loop fusion | flops 29491200 | bytes 8887680 | tf_op jit(solution)/shard_map/add | solution.py:168
  105.5 0.0 copy-start
  105.6 0.0 collective-permute-done
  105.6 2.6 %copy-done = f32[1024,3,480]{2,0,1:T(8,128)} copy-done((f32[1024,3,480]{2,0,1:T(8,128)}, f32[1024,3,480]{2,0,1:T(8,128)S(1)}, u32[]{:S(2)}) %copy-start) | copy-done | bytes 5898264
  108.2 1.5 scatter-add.4
  109.7 5.6 %slice_bitcast_fusion = (f32[1024,480]{1,0:T(8,128)}, f32[1024,480]{1,0:T(8,128)}) fusion(f32[1024,3,480]{2,0,1:T(8,128)} %scatter-add.4), kind=kLoop, calls=%fused_computation.9 | loop fusion | flops 491520 | bytes 9830400 | tf_op jit(solution)/shard_map/squeeze | solution.py:177
  115.3 6.9 %shard_map.64 = (f32[1024,480]{1,0:T(8,128)}, f32[2048,480]{1,0:T(8,128)}, f32[16,480]{1,0:T(8,128)}) custom-call(f32[1024,480]{1,0:T(8,128)} %get-tuple-element.24.d_ref, f32[8,8,480]{2,1,0:T(8,128)} %bitcast_select_fusion.hcol_ref, f32[8,16,480]{2,1,0:T(8,128)} %multiply_exponential_fusion.w_ref, f32[16,480]{1,0:T(8,128)} %multiply_exponential_fusion.1.a8_ref), custom_call_target="tpu_custom_call" | custom-call | tf_op jit(solution)/shard_map/pallas_call | solution.py:104
  122.2 6.2 %all-gather = f32[64,480]{1,0:T(8,128)S(1)} all-gather(f32[16,480]{1,0:T(8,128)} %get-tuple-element.22), channel_id=2, replica_groups=mesh['groups'=2,'context'=4,'tensor'=4] {'context'}, dimensions={0}, use_global_device_ids=true | all-gather | bytes 153600 | tf_op jit(solution)/shard_map/all_gather | solution.py:183
  128.4 0.7 multiply_reduce_fusion.sin_ref
  129.1 10.5 %shard_map.65 = bf16[1920,1024]{1,0:T(8,128)(2,1)} custom-call(f32[1024,480]{1,0:T(8,128)} %get-tuple-element.20.conv_ref, f32[1024,480]{1,0:T(8,128)} %get-tuple-element.23.q_ref, f32[2048,480]{1,0:T(8,128)} %get-tuple-element.21.sums_ref, f32[16,8,480]{2,1,0:T(8,128)} %get-tuple-element.25.g_ref, f32[16,480]{1,0:T(8,128)} %multiply_exponential_fusion.1.a8_ref, ...), custom_call_target="tpu_custom_call" | custom-call | tf_op jit(solution)/shard_map/pallas_call | solution.py:130
  139.6 0.0 reduce-scatter.2.cloned.1.call-update
  139.6 71.1 %reduce-scatter.2.cloned.1.call-done = bf16[480,1024]{1,0:T(8,128)(2,1)} async-done(((bf16[1920,1024]{1,0:T(8,128)(2,1)}), bf16[480,1024]{1,0:T(8,128)(2,1)}) %reduce-scatter.2.cloned.1.call-update) | async-done | bytes 983056 | tf_op jit(solution)/shard_map/reduce_scatter | solution.py:195
  (12 shorter events, 0.1 us)
Async XLA Ops:
  6.5 81.5 %all-gather.3.cloned.1.call-start = ((), (), s32[]{:S(2)}) async-start(), calls=%async_computation.1 | async-start | bytes 4915200 | tf_op jit(solution)/shard_map/all_gather | solution.py:157
  7.3 203.5 %reduce-scatter.2.cloned.1.call-start = ((), (), s32[]{:S(2)}) async-start(), calls=%async_computation.2 | async-start | bytes 4915200 | tf_op jit(solution)/shard_map/reduce_scatter | solution.py:195
  98.2 7.4 %collective-permute-start = (bf16[6,3,480]{2,0,1:T(8,128)(2,1)S(1)}, bf16[6,3,480]{2,0,1:T(8,128)(2,1)S(1)}, u32[]{:S(2)}, u32[]{:S(2)}) collective-permute-start(bf16[6,3,480]{2,0,1:T(8,128)(2,1)S(1)} %slice.133), channel_id=1, source_target_pairs={{0,4},{4,8},{8,12},{1,5},{5,9},{9,13},{2,6},{6,10},{10,14},{3,7},{... | collective-permute-start | bytes 51848 | tf_op jit(solution)/shard_map/ppermute | solution.py:15
  105.5 2.7 %copy-start = (f32[1024,3,480]{2,0,1:T(8,128)}, f32[1024,3,480]{2,0,1:T(8,128)S(1)}, u32[]{:S(2)}) copy-start(f32[1024,3,480]{2,0,1:T(8,128)S(1)} %multiply_add_fusion) | copy-start | bytes 17694724
Sparse Core Ops, SparseCore 0:
  8.9 79.1 all-gather.2
  139.8 70.9 reduce-scatter.1

commit v17 on v12

--- a/solution.py
+++ b/solution.py
@@ -66,7 +66,7 @@
     lax.fori_loop(0, rows // CHUNK, body, 0, unroll=4)
     gated = gated_ref[...].astype(jnp.bfloat16)
     out_ref[...] = lax.dot_general(
-        wo_ref[...], gated, (((0,), (1,)), ((), ())), preferred_element_type=jnp.float32
+        wo_ref[...], gated, (((1,), (1,)), ((), ())), preferred_element_type=jnp.float32
     ).astype(out_ref.dtype)
 
 
@@ -123,7 +123,7 @@
 
 def gate(conv_local, query, sums, g_tab, a8, state_in, out_weight):
     rows, channels = conv_local.shape
-    width = out_weight.shape[1]
+    width = out_weight.shape[0]
     modes = a8.shape[0]
     blk = min(BLOCK, rows)
     per = blk // CHUNK * modes
@@ -183,7 +183,7 @@
     )
     state_in = jnp.sum(factor * ends, axis=0)
 
-    partial_sums = gate(conv_local, query, sums, g_tab, a8, state_in, out_weight)
+    partial_sums = gate(conv_local, query, sums, g_tab, a8, state_in, out_weight.T)
     summed = lax.psum_scatter(partial_sums, "tensor", scatter_dimension=0, tiled=True).T
     return summed
 

time: 214 us -> 215 us (level)
  local copies, waits for them, and re-layouts: 0.77 us -> 4.71 us
    unnamed x4 -> x5, local copies, waits for them, and re-layouts: 0.02 us -> 3.97 us
  transfers between devices with their start and end apart: 3 -> 3, of which waited for: 3 -> 2; matrix products, arithmetic and copies ran while one was open for 3% -> 5% of each run, Pallas kernels for 0% -> 0%
where the time goes in v17:
time: 215 us
  waiting for transfers between devices  146 us (68%)
  Pallas kernels  17.3 us (8%)
  other arithmetic  15.1 us (7%)
  between operations  13.5 us (6%)
  matrix products  10.1 us (5%)
  blocking collectives  6.21 us (3%)
  local copies, waits for them, and re-layouts  4.71 us (2%)
    all_gather x1, waiting for transfers between devices, per_device(): lax.all_gather(tokens, 'tensor', axis=1, tiled=True)  74.2 us
    reduce_scatter x1, waiting for transfers between devices, per_device(): lax.psum_scatter(partial_sums, 'tensor', scatter_dimension=0, tiled=True)  71.1 us
    pallas_call x1, Pallas kernels, gate(): pl.pallas_call(gate_kernel, grid=(rows // blk,), out_shape=jax.ShapeDtype...  10.5 us
    dot_general x1, matrix products, per_device(): jnp.einsum('td,dkc->tkc', lax.all_gather(tokens, 'tensor', axis=1, tiled=...  10.1 us
    pallas_call x1, Pallas kernels, local_conv(): pl.pallas_call(local_kernel, grid=(rows // blk,), out_shape=(jax.ShapeDty...  6.85 us
    all_gather x1, blocking collectives, per_device(): ends = lax.all_gather(end_state, 'context', axis=0, tiled=False)  6.21 us
    add x1, other arithmetic, per_device(): filtered + short_filter[tap_number].astype(jnp.float32)[None] * padded[be...  5.82 us
  transfers between devices with their start and end apart: 3, of which 2 were waited for; matrix products, arithmetic and copies ran while one was open for 5% of the time, Pallas kernels for 0%

profile of v17, /device:TPU:0, one launch (start us, length us, event | category | flops | bytes accessed | tf_op | source)
XLA Modules:
  0.0 214.6 jit_solution(16828647335651753199)
XLA Ops:
  6.5 0.0 all-gather.3.cloned.1.call-start
  6.5 0.7 all-gather.3.cloned.1.call-update
  7.3 0.0 reduce-scatter.2.cloned.1.call-start
  7.3 0.1 compare_select_fusion
  7.4 0.1 reshape.127
  7.5 0.8 multiply_bitcast_fusion
  8.3 0.8 exponential_multiply_fusion
  9.1 0.7 gather_fusion
  9.8 0.1 subtract_compare_fusion
  9.9 1.0 slice_convert_fusion.6
  10.9 1.4 multiply_exponential_fusion.1.a8_ref
  12.3 0.7 bitcast_select_fusion.hcol_ref
  13.1 0.8 multiply_exponential_fusion.w_ref
  13.9 74.2 %all-gather.3.cloned.1.call-done = bf16[1024,1920]{0,1:T(8,128)(2,1)} async-done(((bf16[1024,480]{0,1:T(8,128)(2,1)}), bf16[1024,1920]{0,1:T(8,128)(2,1)}) %all-gather.3.cloned.1.call-update) | async-done | bytes 3932176 | tf_op jit(solution)/shard_map/all_gather | solution.py:157
  88.1 10.1 %fusion.7 = bf16[1024,3,480]{2,0,1:T(8,128)(2,1)S(1)} fusion(bf16[1920,3,480]{0,2,1:T(8,128)(2,1)} %param.7, bf16[1024,1920]{0,1:T(8,128)(2,1)} %all-gather.3.cloned.1.call-done), kind=kOutput, calls=%fused_computation.18 | convolution fusion | flops 5663784960 | bytes 12410880 | tf_op jit(solution)/shard_map/td,dkc->tkc/dot_general | solution.py:155
  98.2 1.6 collective-permute-start
  99.8 3.9 %copy.10 = bf16[480,1920]{0,1:T(8,128)(2,1)} copy(bf16[480,1920]{1,0:T(8,128)(2,1)} %param.11) | data formatting | bytes 3686400 | tf_op args[5]
  103.7 0.0 collective-permute-done
  103.7 5.8 %multiply_add_fusion = f32[1024,3,480]{2,0,1:T(8,128)S(1)} fusion(bf16[1024,3,480]{2,0,1:T(8,128)(2,1)S(1)} %fusion.7, bf16[6,3,480]{2,0,1:T(8,128)(2,1)S(1)} %collective-permute-done, f32[3,480]{1,0:T(4,128)S(1)} %get-tuple-element.24, f32[3,480]{1,0:T(4,128)S(1)} %get-tuple-element.25, f32[3,480]{1,0:T(4,128)S(1)} %get-tuple-element.26, ...), kind=kLoop, calls=%fused_computation.6 | loop fusion | flops 56033280 | bytes 8904960 | tf_op jit(solution)/shard_map/add | solution.py:166
  109.6 2.8 %slice_bitcast_fusion = (f32[1024,480]{1,0:T(8,128)}, f32[1024,480]{1,0:T(8,128)}) fusion(f32[1024,3,480]{2,0,1:T(8,128)S(1)} %multiply_add_fusion), kind=kLoop, calls=%fused_computation.19 | loop fusion | flops 491520 | bytes 9830400 | tf_op jit(solution)/shard_map/squeeze | solution.py:169
  112.4 6.8 %shard_map.64 = (f32[1024,480]{1,0:T(8,128)}, f32[2048,480]{1,0:T(8,128)}, f32[16,480]{1,0:T(8,128)}) custom-call(f32[1024,480]{1,0:T(8,128)} %get-tuple-element.12.d_ref, f32[8,8,480]{2,1,0:T(8,128)} %bitcast_select_fusion.hcol_ref, f32[8,16,480]{2,1,0:T(8,128)} %multiply_exponential_fusion.w_ref, f32[16,480]{1,0:T(8,128)} %multiply_exponential_fusion.1.a8_ref), custom_call_target="tpu_custom_call" | custom-call | tf_op jit(solution)/shard_map/pallas_call | solution.py:104
  119.3 6.2 %all-gather = f32[64,480]{1,0:T(8,128)S(1)} all-gather(f32[16,480]{1,0:T(8,128)} %get-tuple-element.10), channel_id=2, replica_groups=mesh['groups'=2,'context'=4,'tensor'=4] {'context'}, dimensions={0}, use_global_device_ids=true | all-gather | bytes 153600 | tf_op jit(solution)/shard_map/all_gather | solution.py:175
  125.5 0.7 multiply_reduce_fusion.sin_ref
  126.2 10.5 %shard_map.65 = bf16[1920,1024]{1,0:T(8,128)(2,1)} custom-call(f32[1024,480]{1,0:T(8,128)} %get-tuple-element.8.conv_ref, f32[1024,480]{1,0:T(8,128)} %get-tuple-element.11.q_ref, f32[2048,480]{1,0:T(8,128)} %get-tuple-element.9.sums_ref, f32[16,8,480]{2,1,0:T(8,128)} %get-tuple-element.13.g_ref, f32[16,480]{1,0:T(8,128)} %multiply_exponential_fusion.1.a8_ref, ...), custom_call_target="tpu_custom_call" | custom-call | tf_op jit(solution)/shard_map/pallas_call | solution.py:130
  136.7 0.0 reduce-scatter.2.cloned.1.call-update
  136.7 71.1 %reduce-scatter.2.cloned.1.call-done = bf16[480,1024]{1,0:T(8,128)(2,1)} async-done(((bf16[1920,1024]{1,0:T(8,128)(2,1)}), bf16[480,1024]{1,0:T(8,128)(2,1)}) %reduce-scatter.2.cloned.1.call-update) | async-done | bytes 983056 | tf_op jit(solution)/shard_map/reduce_scatter | solution.py:187
  (10 shorter events, 0.1 us)
Async XLA Ops:
  6.5 81.5 %all-gather.3.cloned.1.call-start = ((), (), s32[]{:S(2)}) async-start(), calls=%async_computation.1 | async-start | bytes 4915200 | tf_op jit(solution)/shard_map/all_gather | solution.py:157
  7.3 200.5 %reduce-scatter.2.cloned.1.call-start = ((), (), s32[]{:S(2)}) async-start(), calls=%async_computation.2 | async-start | bytes 4915200 | tf_op jit(solution)/shard_map/reduce_scatter | solution.py:187
  98.2 5.6 %collective-permute-start = (bf16[6,3,480]{2,0,1:T(8,128)(2,1)S(1)}, bf16[6,3,480]{2,0,1:T(8,128)(2,1)S(1)}, u32[]{:S(2)}, u32[]{:S(2)}) collective-permute-start(bf16[6,3,480]{2,0,1:T(8,128)(2,1)S(1)} %slice.70), channel_id=1, source_target_pairs={{0,4},{4,8},{8,12},{1,5},{5,9},{9,13},{2,6},{6,10},{10,14},{3,7},{... | collective-permute-start | bytes 51848 | tf_op jit(solution)/shard_map/ppermute | solution.py:15
Sparse Core Ops, SparseCore 0:
  8.9 79.1 all-gather.2
  136.8 70.9 reduce-scatter.1

commit v18 on v12

--- a/solution.py
+++ b/solution.py
@@ -63,7 +63,7 @@
         s_ref[...] = a8_ref[...] * state + piece
         return carry
 
-    lax.fori_loop(0, rows // CHUNK, body, 0, unroll=4)
+    lax.fori_loop(0, rows // CHUNK, body, 0, unroll=True)
     gated = gated_ref[...].astype(jnp.bfloat16)
     out_ref[...] = lax.dot_general(
         wo_ref[...], gated, (((0,), (1,)), ((), ())), preferred_element_type=jnp.float32

time: 214 us -> 214 us (level)
  no operation moved by 1% of the time
where the time goes in v18:
time: 214 us
  waiting for transfers between devices  147 us (69%)
  Pallas kernels  17 us (8%)
  other arithmetic  15.1 us (7%)
  between operations  13.5 us (6%)
  matrix products  10.1 us (5%)
  blocking collectives  7.94 us (4%)
    all_gather x1, waiting for transfers between devices, per_device(): lax.all_gather(tokens, 'tensor', axis=1, tiled=True)  74.2 us
    reduce_scatter x1, waiting for transfers between devices, per_device(): lax.psum_scatter(partial_sums, 'tensor', scatter_dimension=0, tiled=True)  71.7 us
    pallas_call x1, Pallas kernels, gate(): pl.pallas_call(gate_kernel, grid=(rows // blk,), out_shape=jax.ShapeDtype...  10.2 us
    dot_general x1, matrix products, per_device(): jnp.einsum('td,dkc->tkc', lax.all_gather(tokens, 'tensor', axis=1, tiled=...  10.1 us
    all_gather x1, blocking collectives, per_device(): ends = lax.all_gather(end_state, 'context', axis=0, tiled=False)  7.94 us
    pallas_call x1, Pallas kernels, local_conv(): pl.pallas_call(local_kernel, grid=(rows // blk,), out_shape=(jax.ShapeDty...  6.85 us
    add x1, other arithmetic, per_device(): filtered + short_filter[tap_number].astype(jnp.float32)[None] * padded[be...  5.82 us
  transfers between devices with their start and end apart: 3, of which 3 were waited for; matrix products, arithmetic and copies ran while one was open for 3% of the time, Pallas kernels for 0%

profile of v18, /device:TPU:0, one launch (start us, length us, event | category | flops | bytes accessed | tf_op | source)
XLA Modules:
  0.0 213.5 jit_solution(3861921470986257744)
XLA Ops:
  6.5 0.0 all-gather.3.cloned.1.call-start
  6.5 0.7 all-gather.3.cloned.1.call-update
  7.3 0.0 reduce-scatter.2.cloned.1.call-start
  7.3 0.1 compare_select_fusion
  7.4 0.1 reshape.127
  7.5 0.8 multiply_bitcast_fusion
  8.3 0.8 exponential_multiply_fusion
  9.1 0.7 gather_fusion
  9.8 0.1 subtract_compare_fusion
  9.9 1.0 slice_convert_fusion.6
  10.9 1.4 multiply_exponential_fusion.1.a8_ref
  12.3 0.7 bitcast_select_fusion.hcol_ref
  13.0 0.8 multiply_exponential_fusion.w_ref
  13.8 74.2 %all-gather.3.cloned.1.call-done = bf16[1024,1920]{0,1:T(8,128)(2,1)} async-done(((bf16[1024,480]{0,1:T(8,128)(2,1)}), bf16[1024,1920]{0,1:T(8,128)(2,1)}) %all-gather.3.cloned.1.call-update) | async-done | bytes 3932176 | tf_op jit(solution)/shard_map/all_gather | solution.py:157
  88.1 10.1 %fusion.7 = bf16[1024,3,480]{2,0,1:T(8,128)(2,1)S(1)} fusion(bf16[1920,3,480]{0,2,1:T(8,128)(2,1)} %param.7, bf16[1024,1920]{0,1:T(8,128)(2,1)} %all-gather.3.cloned.1.call-done), kind=kOutput, calls=%fused_computation.18 | convolution fusion | flops 5663784960 | bytes 12410880 | tf_op jit(solution)/shard_map/td,dkc->tkc/dot_general | solution.py:155
  98.2 1.6 collective-permute-start
  99.8 0.8 collective-permute-done
  100.6 5.8 %multiply_add_fusion = f32[1024,3,480]{2,0,1:T(8,128)S(1)} fusion(bf16[1024,3,480]{2,0,1:T(8,128)(2,1)S(1)} %fusion.7, bf16[6,3,480]{2,0,1:T(8,128)(2,1)S(1)} %collective-permute-done, f32[3,480]{1,0:T(4,128)S(1)} %get-tuple-element.24, f32[3,480]{1,0:T(4,128)S(1)} %get-tuple-element.25, f32[3,480]{1,0:T(4,128)S(1)} %get-tuple-element.26, ...), kind=kLoop, calls=%fused_computation.6 | loop fusion | flops 56033280 | bytes 8904960 | tf_op jit(solution)/shard_map/add | solution.py:166
  106.4 2.8 %slice_bitcast_fusion = (f32[1024,480]{1,0:T(8,128)}, f32[1024,480]{1,0:T(8,128)}) fusion(f32[1024,3,480]{2,0,1:T(8,128)S(1)} %multiply_add_fusion), kind=kLoop, calls=%fused_computation.19 | loop fusion | flops 491520 | bytes 9830400 | tf_op jit(solution)/shard_map/squeeze | solution.py:169
  109.3 6.8 %shard_map.64 = (f32[1024,480]{1,0:T(8,128)}, f32[2048,480]{1,0:T(8,128)}, f32[16,480]{1,0:T(8,128)}) custom-call(f32[1024,480]{1,0:T(8,128)} %get-tuple-element.12.d_ref, f32[8,8,480]{2,1,0:T(8,128)} %bitcast_select_fusion.hcol_ref, f32[8,16,480]{2,1,0:T(8,128)} %multiply_exponential_fusion.w_ref, f32[16,480]{1,0:T(8,128)} %multiply_exponential_fusion.1.a8_ref), custom_call_target="tpu_custom_call" | custom-call | tf_op jit(solution)/shard_map/pallas_call | solution.py:104
  116.1 7.9 %all-gather = f32[64,480]{1,0:T(8,128)S(1)} all-gather(f32[16,480]{1,0:T(8,128)} %get-tuple-element.10), channel_id=2, replica_groups=mesh['groups'=2,'context'=4,'tensor'=4] {'context'}, dimensions={0}, use_global_device_ids=true | all-gather | bytes 153600 | tf_op jit(solution)/shard_map/all_gather | solution.py:175
  124.1 0.7 multiply_reduce_fusion.sin_ref
  124.8 10.2 %shard_map.65 = bf16[1920,1024]{1,0:T(8,128)(2,1)} custom-call(f32[1024,480]{1,0:T(8,128)} %get-tuple-element.8.conv_ref, f32[1024,480]{1,0:T(8,128)} %get-tuple-element.11.q_ref, f32[2048,480]{1,0:T(8,128)} %get-tuple-element.9.sums_ref, f32[16,8,480]{2,1,0:T(8,128)} %get-tuple-element.13.g_ref, f32[16,480]{1,0:T(8,128)} %multiply_exponential_fusion.1.a8_ref, ...), custom_call_target="tpu_custom_call" | custom-call | tf_op jit(solution)/shard_map/pallas_call | solution.py:130
  134.9 0.0 reduce-scatter.2.cloned.1.call-update
  135.0 71.7 %reduce-scatter.2.cloned.1.call-done = bf16[480,1024]{1,0:T(8,128)(2,1)} async-done(((bf16[1920,1024]{1,0:T(8,128)(2,1)}), bf16[480,1024]{1,0:T(8,128)(2,1)}) %reduce-scatter.2.cloned.1.call-update) | async-done | bytes 983056 | tf_op jit(solution)/shard_map/reduce_scatter | solution.py:187
  (10 shorter events, 0.1 us)
Async XLA Ops:
  6.5 81.5 %all-gather.3.cloned.1.call-start = ((), (), s32[]{:S(2)}) async-start(), calls=%async_computation.1 | async-start | bytes 4915200 | tf_op jit(solution)/shard_map/all_gather | solution.py:157
  7.3 199.4 %reduce-scatter.2.cloned.1.call-start = ((), (), s32[]{:S(2)}) async-start(), calls=%async_computation.2 | async-start | bytes 4915200 | tf_op jit(solution)/shard_map/reduce_scatter | solution.py:187
  98.2 2.4 %collective-permute-start = (bf16[6,3,480]{2,0,1:T(8,128)(2,1)S(1)}, bf16[6,3,480]{2,0,1:T(8,128)(2,1)S(1)}, u32[]{:S(2)}, u32[]{:S(2)}) collective-permute-start(bf16[6,3,480]{2,0,1:T(8,128)(2,1)S(1)} %slice.70), channel_id=1, source_target_pairs={{0,4},{4,8},{8,12},{1,5},{5,9},{9,13},{2,6},{6,10},{10,14},{3,7},{... | collective-permute-start | bytes 51848 | tf_op jit(solution)/shard_map/ppermute | solution.py:15
Sparse Core Ops, SparseCore 0:
  8.9 79.1 all-gather.2
  135.1 71.5 reduce-scatter.1

commit v19 on v18

--- a/solution.py
+++ b/solution.py
@@ -37,10 +37,9 @@
             piece = piece + w_ref[j] * row
         conv_ref[pl.ds(start, CHUNK), :] = acc
         sums_ref[pl.ds(pl.multiple_of(b * modes, modes), modes), :] = piece
-        s_ref[...] = a8_ref[...] * s_ref[...] + piece
-        return carry
-
-    lax.fori_loop(0, rows // CHUNK, body, 0, unroll=4)
+        return a8_ref[...] * carry + piece
+
+    s_ref[...] = lax.fori_loop(0, rows // CHUNK, body, s_ref[...], unroll=4)
     end_ref[...] = s_ref[...]
 
 
@@ -52,18 +51,16 @@
     def _():
         s_ref[...] = sin_ref[...]
 
-    def body(b, carry):
+    def body(b, state):
         start = pl.multiple_of(b * CHUNK, CHUNK)
-        state = s_ref[...]
         acc = conv_ref[pl.ds(start, CHUNK), :]
         for n in range(modes):
             acc = acc + g_ref[n] * state[n : n + 1, :]
         gated_ref[pl.ds(start, CHUNK), :] = q_ref[pl.ds(start, CHUNK), :] * acc
         piece = sums_ref[pl.ds(pl.multiple_of(b * modes, modes), modes), :]
-        s_ref[...] = a8_ref[...] * state + piece
-        return carry
-
-    lax.fori_loop(0, rows // CHUNK, body, 0, unroll=True)
+        return a8_ref[...] * state + piece
+
+    s_ref[...] = lax.fori_loop(0, rows // CHUNK, body, s_ref[...], unroll=4)
     gated = gated_ref[...].astype(jnp.bfloat16)
     out_ref[...] = lax.dot_general(
         wo_ref[...], gated, (((0,), (1,)), ((), ())), preferred_element_type=jnp.float32

time: 214 us -> 215 us (level)
  no operation moved by 1% of the time
where the time goes in v19:
time: 215 us; the launch traced here: 214 us
  waiting for transfers between devices  147 us (68%)
  Pallas kernels  17.6 us (8%)
  other arithmetic  15.1 us (7%)
  between operations  13.5 us (6%)
  matrix products  10.1 us (5%)
  blocking collectives  7.94 us (4%)
    all_gather x1, waiting for transfers between devices, per_device(): lax.all_gather(tokens, 'tensor', axis=1, tiled=True)  74.2 us
    reduce_scatter x1, waiting for transfers between devices, per_device(): lax.psum_scatter(partial_sums, 'tensor', scatter_dimension=0, tiled=True)  71.7 us
    pallas_call x1, Pallas kernels, gate(): pl.pallas_call(gate_kernel, grid=(rows // blk,), out_shape=jax.ShapeDtype...  10.6 us
    dot_general x1, matrix products, per_device(): jnp.einsum('td,dkc->tkc', lax.all_gather(tokens, 'tensor', axis=1, tiled=...  10.1 us
    all_gather x1, blocking collectives, per_device(): ends = lax.all_gather(end_state, 'context', axis=0, tiled=False)  7.94 us
    pallas_call x1, Pallas kernels, local_conv(): pl.pallas_call(local_kernel, grid=(rows // blk,), out_shape=(jax.ShapeDty...  7.03 us
    add x1, other arithmetic, per_device(): filtered + short_filter[tap_number].astype(jnp.float32)[None] * padded[be...  5.82 us
  transfers between devices with their start and end apart: 3, of which 3 were waited for; matrix products, arithmetic and copies ran while one was open for 3% of the time, Pallas kernels for 0%

profile of v19, /device:TPU:0, one launch (start us, length us, event | category | flops | bytes accessed | tf_op | source)
XLA Modules:
  0.0 214.1 jit_solution(7468527523829301470)
XLA Ops:
  6.5 0.0 all-gather.3.cloned.1.call-start
  6.5 0.7 all-gather.3.cloned.1.call-update
  7.3 0.0 reduce-scatter.2.cloned.1.call-start
  7.3 0.1 compare_select_fusion
  7.4 0.1 reshape.127
  7.5 0.8 multiply_bitcast_fusion
  8.3 0.8 exponential_multiply_fusion
  9.1 0.7 gather_fusion
  9.8 0.1 subtract_compare_fusion
  9.9 1.0 slice_convert_fusion.6
  10.9 1.4 multiply_exponential_fusion.1.a8_ref
  12.3 0.7 bitcast_select_fusion.hcol_ref
  13.0 0.8 multiply_exponential_fusion.w_ref
  13.8 74.2 %all-gather.3.cloned.1.call-done = bf16[1024,1920]{0,1:T(8,128)(2,1)} async-done(((bf16[1024,480]{0,1:T(8,128)(2,1)}), bf16[1024,1920]{0,1:T(8,128)(2,1)}) %all-gather.3.cloned.1.call-update) | async-done | bytes 3932176 | tf_op jit(solution)/shard_map/all_gather | solution.py:154
  88.1 10.1 %fusion.7 = bf16[1024,3,480]{2,0,1:T(8,128)(2,1)S(1)} fusion(bf16[1920,3,480]{0,2,1:T(8,128)(2,1)} %param.7, bf16[1024,1920]{0,1:T(8,128)(2,1)} %all-gather.3.cloned.1.call-done), kind=kOutput, calls=%fused_computation.18 | convolution fusion | flops 5663784960 | bytes 12410880 | tf_op jit(solution)/shard_map/td,dkc->tkc/dot_general | solution.py:152
  98.2 1.6 collective-permute-start
  99.8 0.8 collective-permute-done
  100.6 5.8 %multiply_add_fusion = f32[1024,3,480]{2,0,1:T(8,128)S(1)} fusion(bf16[1024,3,480]{2,0,1:T(8,128)(2,1)S(1)} %fusion.7, bf16[6,3,480]{2,0,1:T(8,128)(2,1)S(1)} %collective-permute-done, f32[3,480]{1,0:T(4,128)S(1)} %get-tuple-element.24, f32[3,480]{1,0:T(4,128)S(1)} %get-tuple-element.25, f32[3,480]{1,0:T(4,128)S(1)} %get-tuple-element.26, ...), kind=kLoop, calls=%fused_computation.6 | loop fusion | flops 56033280 | bytes 8904960 | tf_op jit(solution)/shard_map/add | solution.py:163
  106.4 2.8 %slice_bitcast_fusion = (f32[1024,480]{1,0:T(8,128)}, f32[1024,480]{1,0:T(8,128)}) fusion(f32[1024,3,480]{2,0,1:T(8,128)S(1)} %multiply_add_fusion), kind=kLoop, calls=%fused_computation.19 | loop fusion | flops 491520 | bytes 9830400 | tf_op jit(solution)/shard_map/squeeze | solution.py:166
  109.3 7.0 %shard_map.64 = (f32[1024,480]{1,0:T(8,128)}, f32[2048,480]{1,0:T(8,128)}, f32[16,480]{1,0:T(8,128)}) custom-call(f32[1024,480]{1,0:T(8,128)} %get-tuple-element.12.d_ref, f32[8,8,480]{2,1,0:T(8,128)} %bitcast_select_fusion.hcol_ref, f32[8,16,480]{2,1,0:T(8,128)} %multiply_exponential_fusion.w_ref, f32[16,480]{1,0:T(8,128)} %multiply_exponential_fusion.1.a8_ref), custom_call_target="tpu_custom_call" | custom-call | tf_op jit(solution)/shard_map/pallas_call | solution.py:101
  116.3 7.9 %all-gather = f32[64,480]{1,0:T(8,128)S(1)} all-gather(f32[16,480]{1,0:T(8,128)} %get-tuple-element.10), channel_id=2, replica_groups=mesh['groups'=2,'context'=4,'tensor'=4] {'context'}, dimensions={0}, use_global_device_ids=true | all-gather | bytes 153600 | tf_op jit(solution)/shard_map/all_gather | solution.py:172
  124.2 0.7 multiply_reduce_fusion.sin_ref
  125.0 10.6 %shard_map.65 = bf16[1920,1024]{1,0:T(8,128)(2,1)} custom-call(f32[1024,480]{1,0:T(8,128)} %get-tuple-element.8.conv_ref, f32[1024,480]{1,0:T(8,128)} %get-tuple-element.11.q_ref, f32[2048,480]{1,0:T(8,128)} %get-tuple-element.9.sums_ref, f32[16,8,480]{2,1,0:T(8,128)} %get-tuple-element.13.g_ref, f32[16,480]{1,0:T(8,128)} %multiply_exponential_fusion.1.a8_ref, ...), custom_call_target="tpu_custom_call" | custom-call | tf_op jit(solution)/shard_map/pallas_call | solution.py:127
  135.6 0.0 reduce-scatter.2.cloned.1.call-update
  135.6 71.7 %reduce-scatter.2.cloned.1.call-done = bf16[480,1024]{1,0:T(8,128)(2,1)} async-done(((bf16[1920,1024]{1,0:T(8,128)(2,1)}), bf16[480,1024]{1,0:T(8,128)(2,1)}) %reduce-scatter.2.cloned.1.call-update) | async-done | bytes 983056 | tf_op jit(solution)/shard_map/reduce_scatter | solution.py:184
  (10 shorter events, 0.1 us)
Async XLA Ops:
  6.5 81.5 %all-gather.3.cloned.1.call-start = ((), (), s32[]{:S(2)}) async-start(), calls=%async_computation.1 | async-start | bytes 4915200 | tf_op jit(solution)/shard_map/all_gather | solution.py:154
  7.3 200.0 %reduce-scatter.2.cloned.1.call-start = ((), (), s32[]{:S(2)}) async-start(), calls=%async_computation.2 | async-start | bytes 4915200 | tf_op jit(solution)/shard_map/reduce_scatter | solution.py:184
  98.2 2.4 %collective-permute-start = (bf16[6,3,480]{2,0,1:T(8,128)(2,1)S(1)}, bf16[6,3,480]{2,0,1:T(8,128)(2,1)S(1)}, u32[]{:S(2)}, u32[]{:S(2)}) collective-permute-start(bf16[6,3,480]{2,0,1:T(8,128)(2,1)S(1)} %slice.70), channel_id=1, source_target_pairs={{0,4},{4,8},{8,12},{1,5},{5,9},{9,13},{2,6},{6,10},{10,14},{3,7},{... | collective-permute-start | bytes 51848 | tf_op jit(solution)/shard_map/ppermute | solution.py:15
Sparse Core Ops, SparseCore 0:
  8.9 79.1 all-gather.2
  135.7 71.5 reduce-scatter.1

commit v20 on v12

--- a/solution.py
+++ b/solution.py
@@ -99,7 +99,7 @@
 def local_conv(drive, hcol, w_tab, a8):
     rows, channels = drive.shape
     modes = a8.shape[0]
-    blk = min(BLOCK, rows)
+    blk = min(2 * BLOCK, rows)
     per = blk // CHUNK * modes
     return pl.pallas_call(
         local_kernel,

time: 214 us -> 214 us (level)
  no operation moved by 1% of the time
where the time goes in v20:
time: 214 us
  waiting for transfers between devices  147 us (69%)
  Pallas kernels  17.4 us (8%)
  other arithmetic  15.1 us (7%)
  between operations  13.5 us (6%)
  matrix products  10.1 us (5%)
  blocking collectives  7.93 us (4%)
    all_gather x1, waiting for transfers between devices, per_device(): lax.all_gather(tokens, 'tensor', axis=1, tiled=True)  74.2 us
    reduce_scatter x1, waiting for transfers between devices, per_device(): lax.psum_scatter(partial_sums, 'tensor', scatter_dimension=0, tiled=True)  71.7 us
    pallas_call x1, Pallas kernels, gate(): pl.pallas_call(gate_kernel, grid=(rows // blk,), out_shape=jax.ShapeDtype...  10.5 us
    dot_general x1, matrix products, per_device(): jnp.einsum('td,dkc->tkc', lax.all_gather(tokens, 'tensor', axis=1, tiled=...  10.1 us
    all_gather x1, blocking collectives, per_device(): ends = lax.all_gather(end_state, 'context', axis=0, tiled=False)  7.93 us
    pallas_call x1, Pallas kernels, local_conv(): pl.pallas_call(local_kernel, grid=(rows // blk,), out_shape=(jax.ShapeDty...  6.84 us
    add x1, other arithmetic, per_device(): filtered + short_filter[tap_number].astype(jnp.float32)[None] * padded[be...  5.82 us
  transfers between devices with their start and end apart: 3, of which 3 were waited for; matrix products, arithmetic and copies ran while one was open for 3% of the time, Pallas kernels for 0%

profile of v20, /device:TPU:0, one launch (start us, length us, event | category | flops | bytes accessed | tf_op | source)
XLA Modules:
  0.0 213.8 jit_solution(8796036475255516466)
XLA Ops:
  6.5 0.0 all-gather.3.cloned.1.call-start
  6.5 0.7 all-gather.3.cloned.1.call-update
  7.3 0.0 reduce-scatter.2.cloned.1.call-start
  7.3 0.1 compare_select_fusion
  7.4 0.1 reshape.127
  7.5 0.8 multiply_bitcast_fusion
  8.3 0.8 exponential_multiply_fusion
  9.1 0.7 gather_fusion
  9.8 0.1 subtract_compare_fusion
  9.9 1.0 slice_convert_fusion.6
  10.9 1.4 multiply_exponential_fusion.1.a8_ref
  12.3 0.7 bitcast_select_fusion.hcol_ref
  13.0 0.8 multiply_exponential_fusion.w_ref
  13.8 74.2 %all-gather.3.cloned.1.call-done = bf16[1024,1920]{0,1:T(8,128)(2,1)} async-done(((bf16[1024,480]{0,1:T(8,128)(2,1)}), bf16[1024,1920]{0,1:T(8,128)(2,1)}) %all-gather.3.cloned.1.call-update) | async-done | bytes 3932176 | tf_op jit(solution)/shard_map/all_gather | solution.py:157
  88.1 10.1 %fusion.7 = bf16[1024,3,480]{2,0,1:T(8,128)(2,1)S(1)} fusion(bf16[1920,3,480]{0,2,1:T(8,128)(2,1)} %param.7, bf16[1024,1920]{0,1:T(8,128)(2,1)} %all-gather.3.cloned.1.call-done), kind=kOutput, calls=%fused_computation.18 | convolution fusion | flops 5663784960 | bytes 12410880 | tf_op jit(solution)/shard_map/td,dkc->tkc/dot_general | solution.py:155
  98.2 1.6 collective-permute-start
  99.8 0.8 collective-permute-done
  100.6 5.8 %multiply_add_fusion = f32[1024,3,480]{2,0,1:T(8,128)S(1)} fusion(bf16[1024,3,480]{2,0,1:T(8,128)(2,1)S(1)} %fusion.7, bf16[6,3,480]{2,0,1:T(8,128)(2,1)S(1)} %collective-permute-done, f32[3,480]{1,0:T(4,128)S(1)} %get-tuple-element.24, f32[3,480]{1,0:T(4,128)S(1)} %get-tuple-element.25, f32[3,480]{1,0:T(4,128)S(1)} %get-tuple-element.26, ...), kind=kLoop, calls=%fused_computation.6 | loop fusion | flops 56033280 | bytes 8904960 | tf_op jit(solution)/shard_map/add | solution.py:166
  106.4 2.8 %slice_bitcast_fusion = (f32[1024,480]{1,0:T(8,128)}, f32[1024,480]{1,0:T(8,128)}) fusion(f32[1024,3,480]{2,0,1:T(8,128)S(1)} %multiply_add_fusion), kind=kLoop, calls=%fused_computation.19 | loop fusion | flops 491520 | bytes 9830400 | tf_op jit(solution)/shard_map/squeeze | solution.py:169
  109.3 6.8 %shard_map.64 = (f32[1024,480]{1,0:T(8,128)}, f32[2048,480]{1,0:T(8,128)}, f32[16,480]{1,0:T(8,128)}) custom-call(f32[1024,480]{1,0:T(8,128)} %get-tuple-element.12.d_ref, f32[8,8,480]{2,1,0:T(8,128)} %bitcast_select_fusion.hcol_ref, f32[8,16,480]{2,1,0:T(8,128)} %multiply_exponential_fusion.w_ref, f32[16,480]{1,0:T(8,128)} %multiply_exponential_fusion.1.a8_ref), custom_call_target="tpu_custom_call" | custom-call | tf_op jit(solution)/shard_map/pallas_call | solution.py:104
  116.1 7.9 %all-gather = f32[64,480]{1,0:T(8,128)S(1)} all-gather(f32[16,480]{1,0:T(8,128)} %get-tuple-element.10), channel_id=2, replica_groups=mesh['groups'=2,'context'=4,'tensor'=4] {'context'}, dimensions={0}, use_global_device_ids=true | all-gather | bytes 153600 | tf_op jit(solution)/shard_map/all_gather | solution.py:175
  124.0 0.7 multiply_reduce_fusion.sin_ref
  124.8 10.5 %shard_map.65 = bf16[1920,1024]{1,0:T(8,128)(2,1)} custom-call(f32[1024,480]{1,0:T(8,128)} %get-tuple-element.8.conv_ref, f32[1024,480]{1,0:T(8,128)} %get-tuple-element.11.q_ref, f32[2048,480]{1,0:T(8,128)} %get-tuple-element.9.sums_ref, f32[16,8,480]{2,1,0:T(8,128)} %get-tuple-element.13.g_ref, f32[16,480]{1,0:T(8,128)} %multiply_exponential_fusion.1.a8_ref, ...), custom_call_target="tpu_custom_call" | custom-call | tf_op jit(solution)/shard_map/pallas_call | solution.py:130
  135.3 0.0 reduce-scatter.2.cloned.1.call-update
  135.3 71.7 %reduce-scatter.2.cloned.1.call-done = bf16[480,1024]{1,0:T(8,128)(2,1)} async-done(((bf16[1920,1024]{1,0:T(8,128)(2,1)}), bf16[480,1024]{1,0:T(8,128)(2,1)}) %reduce-scatter.2.cloned.1.call-update) | async-done | bytes 983056 | tf_op jit(solution)/shard_map/reduce_scatter | solution.py:187
  (10 shorter events, 0.1 us)
Async XLA Ops:
  6.5 81.5 %all-gather.3.cloned.1.call-start = ((), (), s32[]{:S(2)}) async-start(), calls=%async_computation.1 | async-start | bytes 4915200 | tf_op jit(solution)/shard_map/all_gather | solution.py:157
  7.3 199.7 %reduce-scatter.2.cloned.1.call-start = ((), (), s32[]{:S(2)}) async-start(), calls=%async_computation.2 | async-start | bytes 4915200 | tf_op jit(solution)/shard_map/reduce_scatter | solution.py:187
  98.2 2.4 %collective-permute-start = (bf16[6,3,480]{2,0,1:T(8,128)(2,1)S(1)}, bf16[6,3,480]{2,0,1:T(8,128)(2,1)S(1)}, u32[]{:S(2)}, u32[]{:S(2)}) collective-permute-start(bf16[6,3,480]{2,0,1:T(8,128)(2,1)S(1)} %slice.70), channel_id=1, source_target_pairs={{0,4},{4,8},{8,12},{1,5},{5,9},{9,13},{2,6},{6,10},{10,14},{3,7},{... | collective-permute-start | bytes 51848 | tf_op jit(solution)/shard_map/ppermute | solution.py:15
Sparse Core Ops, SparseCore 0:
  8.9 79.1 all-gather.2
  135.4 71.5 reduce-scatter.1
